TPU v7x, 128 devices: a whole 4x4x4 slice. The times are simulated.
128 devices in a mesh: src: 4 (over x), frame: 8 (over y, z_lo), tile: 4 (over z_hi, core).
Axes of the slice: x: 4, y: 4, z: 4 (z_hi: 2, z_lo: 2; z = z_hi * 2 + z_lo), core: 2. Of those that a mesh axis runs over, the one named last changes fastest.
Arguments:
- feats: float32 [196608, 512], P(('src', 'frame', 'tile')), may hold values from -40 to 40
- row_map: int32 [196608], P(('src', 'frame', 'tile')), may hold values from 0 to 196607, as said below
- clip_ids: int32 [48], replicated, may hold values from 0 to 3, never falling along the last dimension, each value on 1 to 24 neighbouring positions
- norm_gain: float32 [512], replicated, may hold values from 0.1 to 1.9
- norm_bias: float32 [512], replicated, may hold values from -3 to 3
- conv_weight: bfloat16 [3, 3, 3, 512, 512], replicated, may hold values from -0.0546875 to 0.0546875
- conv_bias: float32 [512], replicated, may hold values from -2 to 2
Outputs:
- decoded: bfloat16 [48, 32, 128, 512], P('frame', 'tile', 'src')
Inputs may be any that keep to these rules, and one draw needn't show every extreme that they name: `row_map`: every decoder index occurs once; the rows of each device of src+frame+tile hold exactly 12 indices of each aligned block of 1536 decoder indices. `clip_ids`: clip numbers never fall along the frames; each clip has 1 to 24 frames, one exactly 24.
All inputs are finite; a program needn't handle non-finite values.
Results may differ from a plain program's by a relative error of at most 0.0029.
Values may be sent and summed in bfloat16 or wider, within the bound.
No kernel may reach another device: no remote copies, remote signals or barrier semaphores. Data moves between devices by JAX's collectives and lax.ppermute only.
A program may use at most 128 MiB of HBM per device.

v0:
```python
import jax
import jax.numpy as jnp
from jax import lax
from jax.sharding import PartitionSpec as P

GROUPS = 32
CLIPS = 4
FR_DEV = 6
HR = 8
WCOL = 32
HIGH = lax.Precision.HIGHEST


def passed_along(x, axis, by):
    peers = lax.axis_size(axis)
    pairs = [(i, i + by) for i in range(peers) if 0 <= i + by < peers]
    return lax.ppermute(x, axis, pairs)


def with_halo(x, sides, width):
    for axis, dim in sides:
        peers, length = (lax.axis_size(axis), x.shape[dim])
        up = [(i, (i + 1) % peers) for i in range(peers - 1)]
        down = [(j, i) for i, j in up]
        last = lax.slice_in_dim(x, length - width, length, axis=dim)
        leading = lax.slice_in_dim(x, 0, width, axis=dim)
        before = lax.ppermute(last, axis, up)
        after = lax.ppermute(leading, axis, down)
        x = jnp.concatenate([before, x, after], axis=dim)
    return x


def shards(feats, row_map, clip_ids, norm_gain, norm_bias, conv_weight, conv_bias):
    local_rows, channels = feats.shape
    n_src = lax.axis_size("src")
    n_frame = lax.axis_size("frame")
    n_tile = lax.axis_size("tile")
    devices = n_src * n_frame * n_tile
    per_pair = local_rows // devices
    group_width = channels // GROUPS
    per_frame = HR * WCOL

    owners = row_map // local_rows
    slot_ids = row_map % local_rows
    row_frame = (owners // n_tile) % n_frame * FR_DEV + slot_ids // per_frame
    row_clip = jnp.take(clip_ids, row_frame)
    row_onehot = (row_clip[:, None] == jnp.arange(CLIPS, dtype=jnp.int32)[None, :]).astype(
        jnp.float32
    )

    grouped = feats.reshape(local_rows, GROUPS, group_width)
    local_n = jnp.sum(row_onehot, axis=0) * group_width
    local_s = jnp.dot(row_onehot.T, jnp.sum(grouped, axis=2), precision=HIGH)
    local_m = local_s / jnp.maximum(local_n, 1.0)[:, None]
    row_m = jnp.dot(row_onehot, local_m, precision=HIGH)
    dev = grouped - row_m[:, :, None]
    local_m2 = jnp.dot(row_onehot.T, jnp.sum(dev * dev, axis=2), precision=HIGH)

    ordering = jnp.argsort(owners, stable=True)
    outgoing = feats[ordering].reshape(devices, per_pair, channels)
    sent_slots = slot_ids[ordering].astype(jnp.float32).reshape(devices, per_pair)
    stats = jnp.concatenate([local_n, local_s.reshape(-1), local_m2.reshape(-1)])
    tail = jnp.zeros((channels - per_pair - stats.shape[0],), jnp.float32)
    extra = jnp.concatenate(
        [sent_slots, jnp.broadcast_to(jnp.concatenate([stats, tail]), (devices, channels - per_pair))],
        axis=1,
    )
    payload = jnp.concatenate([outgoing, extra[:, None, :]], axis=1)
    arrived = lax.all_to_all(
        payload, ("src", "frame", "tile"), split_axis=0, concat_axis=0, tiled=True
    )

    rows = arrived[:, :per_pair, :].reshape(-1, channels)
    info = arrived[:, per_pair, :]
    targets = info[:, :per_pair].reshape(-1).astype(jnp.int32)
    part_n = info[:, per_pair : per_pair + CLIPS]
    base = per_pair + CLIPS
    part_s = info[:, base : base + CLIPS * GROUPS].reshape(devices, CLIPS, GROUPS)
    part_m2 = info[:, base + CLIPS * GROUPS : base + 2 * CLIPS * GROUPS].reshape(
        devices, CLIPS, GROUPS
    )
    total_n = jnp.sum(part_n, axis=0)
    clip_mean = jnp.sum(part_s, axis=0) / total_n[:, None]
    part_m = part_s / jnp.maximum(part_n, 1.0)[:, :, None]
    spread = part_m - clip_mean[None]
    clip_m2 = jnp.sum(part_m2, axis=0) + jnp.sum(part_n[:, :, None] * spread * spread, axis=0)
    clip_var = clip_m2 / total_n[:, None]

    inverse = jnp.argsort(targets)
    features = rows[inverse].reshape(FR_DEV, HR, WCOL, channels)

    first_frame = lax.axis_index("frame") * FR_DEV
    padded_ids = jnp.concatenate([jnp.full((2,), -1, jnp.int32), clip_ids])
    window_ids = lax.dynamic_slice_in_dim(padded_ids, first_frame, FR_DEV + 2)
    own_ids = window_ids[2:]
    onehot = (own_ids[:, None] == jnp.arange(CLIPS, dtype=jnp.int32)[None, :]).astype(jnp.float32)
    shaped = features.reshape(FR_DEV, per_frame, GROUPS, group_width)
    frame_mean = jnp.dot(onehot, clip_mean, precision=HIGH)
    centred = shaped - frame_mean[:, None, :, None]
    inverse_std = 1.0 / jnp.sqrt(clip_var + 1e-06)
    frame_inv = jnp.dot(onehot, inverse_std, precision=HIGH)
    normed = (centred * frame_inv[:, None, :, None]).reshape(FR_DEV, HR, WCOL, channels)
    activated = jax.nn.silu(normed * norm_gain + norm_bias).astype(jnp.bfloat16)
    previous = passed_along(activated[FR_DEV - 2 :], "frame", 1)
    extended = jnp.concatenate([previous, activated], axis=0)
    padded = with_halo(extended, (("tile", 1), ("src", 2)), 1)
    conv_sum = jnp.zeros((FR_DEV, HR, WCOL, channels), jnp.float32)
    for tap_time in range(3):
        validity = (window_ids[tap_time : tap_time + FR_DEV] == own_ids).astype(jnp.float32)
        partial_value = lax.conv_general_dilated(
            padded[tap_time : tap_time + FR_DEV],
            conv_weight[tap_time],
            (1, 1),
            "VALID",
            dimension_numbers=("NHWC", "HWIO", "NHWC"),
            preferred_element_type=jnp.float32,
        )
        conv_sum = conv_sum + partial_value * validity[:, None, None, None]
    decoded = features + conv_sum + conv_bias
    return decoded.astype(jnp.bfloat16)


def solution(mesh):
    placed = (
        P(("src", "frame", "tile"), None),
        P(("src", "frame", "tile")),
        P(),
        P(),
        P(),
        P(),
        P(),
    )
    return jax.shard_map(
        shards,
        mesh=mesh,
        in_specs=placed,
        out_specs=P("frame", "tile", "src", None),
        check_vma=False,
    )
```

profile of v0, /device:TPU:1, one launch (start us, length us, event | category | flops | bytes accessed | tf_op | source)
XLA Modules:
  0.0 270.8 jit_solution(4027087848465468306)
XLA Ops:
  0.0 2.1 fusion.66
  2.1 2.1 fusion.67
  4.2 1.7 fusion.68
  5.9 3.6 %copy.70 = f32[1536,512]{0,1:T(8,128)} copy(f32[1536,512]{1,0:T(8,128)} %param.7) | data formatting | bytes 6291456 | tf_op args[0]
  9.4 2.6 bitcast_reduce_fusion
  12.1 29.5 %select_select_fusion = s32[1536]{0:T(1024)S(1)} fusion(s32[]{:T(128)} %bitcast, s32[]{:T(128)} %bitcast.1, s32[]{:T(128)} %bitcast.2, s32[]{:T(128)} %bitcast.3, s32[]{:T(128)} %bitcast.4, s32[]{:T(128)} %bitcast.5, s32[]{:T(128)} %bitcast.6, s32[]{:T(128)} %bitcast.7, s32[]{:T(128)} %bitcast.8, s32[]{:T(128)} %bitcast.9, s32[]{:T(128)} %bitcast.10, ...), kind=kLoop, calls=%fused_computation.92 | loop fusion | flops 239616 | bytes 12480 | tf_op jit(solution)/shard_map/jit(_take)/select_n | solution.py:46
  42.4 2.7 fusion.34
  45.3 5.1 %sort.34 = (s32[1536]{0:T(1024)}, s32[1536]{0:T(1024)S(1)}) sort(s32[1536]{0:T(1024)S(1)} %get-tuple-element.21, s32[1536]{0:T(1024)S(1)} %iota.14), dimensions={0}, to_apply=%region_0.1 | sort | flops 16896 | bytes 24576 | tf_op jit(solution)/shard_map/jit(argsort)/sort | solution.py:59
  50.5 5.0 %gather_fusion = f32[1536,512]{1,0:T(8,128)} fusion(f32[1536,512]{1,0:T(8,128)S(1)} %copy-done, s32[2048]{0:T(1024)S(1)} %pad_clamp_fusion.1), kind=kCustom, calls=%fused_computation | custom fusion | bytes 6297600 | tf_op jit(solution)/shard_map/gather | solution.py:60
  55.4 8.4 %gather_fusion.1 = s32[1536]{0:T(1024)S(1)} fusion(s32[1536]{0:T(1024)S(1)} %get-tuple-element.22, s32[2048]{0:T(1024)S(1)} %pad_clamp_fusion.1), kind=kCustom, calls=%fused_computation.1 | custom fusion | bytes 18432 | tf_op jit(solution)/shard_map/gather | solution.py:61
  64.3 2.2 reshape.73
  66.4 4.9 %pad_maximum_fusion = f32[128,13,512]{2,1,0:T(8,128)} fusion(f32[128,1,512]{2,1,0:T(1,128)S(1)} %broadcast_in_dim.23, f32[128,12,512]{2,1,0:T(8,128)} %reshape.73), kind=kLoop, calls=%fused_computation.19 | loop fusion | flops 851968 | bytes 6815744 | tf_op jit(solution)/shard_map/concatenate | solution.py:68
  71.3 12.4 %all-to-all-start = ((f32[128,13,512]{2,1,0:T(8,128)}), f32[128,13,512]{2,1,0:T(8,128)}, u32[]{:S(2)}, u32[]{:S(2)}) async-start(f32[128,13,512]{2,1,0:T(8,128)} %pad_maximum_fusion), calls=%async_computation | async-start | bytes 8388608 | tf_op jit(solution)/shard_map/all_to_all | solution.py:69
  83.9 52.3 %all-to-all-done = f32[128,13,512]{2,1,0:T(8,128)} async-done(((f32[128,13,512]{2,1,0:T(8,128)}), f32[128,13,512]{2,1,0:T(8,128)}, u32[]{:S(2)}, u32[]{:S(2)}) %all-to-all-start) | async-done | bytes 3407904 | tf_op jit(solution)/shard_map/all_to_all | solution.py:69
  136.2 1.9 slice.141
  139.8 3.0 %reshape.77 = f32[1536,512]{1,0:T(8,128)S(1)} reshape(f32[128,12,512]{2,1,0:T(8,128)} %bitcast.111) | data formatting | bytes 6291456 | tf_op jit(solution)/shard_map/reshape | solution.py:73
  143.0 5.0 %sort.35 = (s32[1536]{0:T(1024)}, s32[1536]{0:T(1024)S(1)}) sort(s32[1536]{0:T(1024)S(1)} %convert_element_type.36, s32[1536]{0:T(1024)S(1)} %iota.15), dimensions={0}, to_apply=%region_4.5 | sort | flops 16896 | bytes 24576 | tf_op jit(solution)/shard_map/jit(argsort)/sort | solution.py:89
  148.0 5.0 %gather_fusion.2 = f32[1536,512]{1,0:T(8,128)} fusion(f32[1536,512]{1,0:T(8,128)S(1)} %reshape.77, s32[2048]{0:T(1024)S(1)} %pad_clamp_fusion), kind=kCustom, calls=%fused_computation.2 | custom fusion | bytes 6297600 | tf_op jit(solution)/shard_map/gather | solution.py:90
  153.0 4.8 %multiply_convert_fusion = bf16[6,8,32,512]{3,0,2,1:T(8,128)(2,1)S(1)} fusion(f32[6,8,32,512]{3,2,1,0:T(8,128)} %bitcast.112, f32[512]{0:T(512)S(1)} %copy-done.5, f32[512]{0:T(512)S(1)} %copy-done.6, f32[6,512]{1,0:T(8,128)S(1)} %mul.89, f32[6,512]{1,0:T(8,128)S(1)} %sub.50), kind=kLoop, calls=%fused_computation.24 | loop fusion | flops 7077888 | bytes 4747264 | tf_op jit(solution)/shard_map/convert_element_type | solution.py:103
  158.4 1.7 collective-permute-start
  160.1 10.1 %collective-permute-done = bf16[2,8,32,512]{3,0,2,1:T(2,128)(2,1)S(1)} collective-permute-done((bf16[2,8,32,512]{3,0,2,1:T(2,128)(2,1)S(1)}, bf16[2,8,32,512]{3,0,2,1:T(2,128)(2,1)S(1)}, u32[]{:S(2)}, u32[]{:S(2)}) %collective-permute-start) | collective-permute-done | bytes 524320 | tf_op jit(solution)/shard_map/ppermute | solution.py:17
  170.4 5.9 %collective-permute-start.1 = (bf16[8,1,32,512]{3,0,2,1:T(8,128)(2,1)S(1)}, bf16[8,1,32,512]{3,0,2,1:T(8,128)(2,1)S(1)}, u32[]{:S(2)}, u32[]{:S(2)}) collective-permute-start(bf16[8,1,32,512]{3,0,2,1:T(8,128)(2,1)S(1)} %get-tuple-element.16), channel_id=1, source_target_pairs={{0,1},{1,2},{2,3},{4,5},{5,6},{6,7},{8,9},{9,10},{10,11},{12,13},{... | collective-permute-start | bytes 786440 | tf_op jit(solution)/shard_map/ppermute | solution.py:27
  176.4 1.9 collective-permute-start.2
  179.7 5.9 %collective-permute-done.2 = bf16[8,1,32,512]{3,0,2,1:T(8,128)(2,1)S(1)} collective-permute-done((bf16[8,1,32,512]{3,0,2,1:T(8,128)(2,1)S(1)}, bf16[8,1,32,512]{3,0,2,1:T(8,128)(2,1)S(1)}, u32[]{:S(2)}, u32[]{:S(2)}) %collective-permute-start.2) | collective-permute-done | bytes 262176 | tf_op jit(solution)/shard_map/ppermute | solution.py:28
  185.6 1.9 collective-permute-start.3
  189.2 4.6 %collective-permute-done.4 = bf16[8,10,1,512]{3,0,2,1:T(8,128)(2,1)S(1)} collective-permute-done((bf16[8,10,1,512]{3,0,2,1:T(8,128)(2,1)S(1)}, bf16[8,10,1,512]{3,0,2,1:T(8,128)(2,1)S(1)}, u32[]{:S(2)}, u32[]{:S(2)}) %collective-permute-start.4) | collective-permute-done | bytes 81952 | tf_op jit(solution)/shard_map/ppermute | solution.py:28
  201.9 16.0 %fusion.7 = f32[8,48,5,512]{3,1,2,0:T(8,128)S(1)} fusion(bf16[3,3,3,512,512]{4,3,2,1,0:T(8,128)(2,1)} %param.12, bf16[10,6,8,7,512]{4,1,3,2,0:T(8,128)(2,1)S(1)} %fusion.12), kind=kOutput, calls=%fused_computation.11 | convolution fusion | flops 9059696640 | bytes 12091392 | tf_op jit(solution)/shard_map/conv_general_dilated | solution.py:110
  217.8 23.2 %fusion.5 = f32[8,48,5,512]{3,1,2,0:T(8,128)} fusion(bf16[3,3,3,512,512]{4,3,2,1,0:T(8,128)(2,1)} %param.12, bf16[10,6,8,7,512]{4,1,3,2,0:T(8,128)(2,1)S(1)} %fusion.13), kind=kOutput, calls=%fused_computation.9 | convolution fusion | flops 9059696640 | bytes 12091392 | tf_op jit(solution)/shard_map/conv_general_dilated | solution.py:110
  242.1 21.8 %fusion.19 = f32[8,48,5,512]{3,1,2,0:T(8,128)S(1)} fusion(f32[8,48,5,512]{3,0,2,1:T(8,128)S(1)} %bitcast.122, f32[8,48,5,512]{3,0,2,1:T(8,128)S(1)} %bitcast.121, f32[8,48,5,512]{3,1,2,0:T(8,128)} %fusion.5, f32[8,48,5,512]{3,1,2,0:T(8,128)S(1)} %fusion.7, bf16[3,3,3,512,512]{4,3,2,1,0:T(8,128)(2,1)} %param.12, bf16[10,6,8,7,512]{4,1,3,2,0:T(8,128)(2,1)S(1)} %fusion.14, ...), kind=kOutput, calls=%fused_computation.27 | convolution fusion | flops 9066577920 | bytes 27820272 | tf_op jit(solution)/shard_map/conv_general_dilated | solution.py:110
  264.0 2.3 copy.79
  266.3 2.6 fusion.32
  268.9 1.7 copy.81
  (79 shorter events, 16.5 us)
Async XLA Ops:
  5.9 6.2 %copy-start.4 = (s32[1536]{0:T(1024)S(1)}, s32[1536]{0:T(1024)}, u32[]{:S(2)}) copy-start(s32[1536]{0:T(1024)} %param.8) | copy-start | bytes 18436
  9.4 41.0 %copy-start = (f32[1536,512]{1,0:T(8,128)S(1)}, f32[1536,512]{1,0:T(8,128)}, u32[]{:S(2)}) copy-start(f32[1536,512]{1,0:T(8,128)} %param.7) | copy-start | bytes 9437188
  55.4 8.8 %copy-start.2 = (f32[1536,512]{1,0:T(8,128)S(1)}, f32[1536,512]{1,0:T(8,128)}, u32[]{:S(2)}) copy-start(f32[1536,512]{1,0:T(8,128)} %gather_fusion) | copy-start | bytes 9437188
  71.3 12.4 %copy-start.3 = (s32[48]{0:T(128)S(1)}, s32[48]{0:T(128)}, u32[]{:S(2)}) copy-start(s32[48]{0:T(128)} %param.9) | copy-start | bytes 580
  71.3 64.8 %all-to-all-start = ((f32[128,13,512]{2,1,0:T(8,128)}), f32[128,13,512]{2,1,0:T(8,128)}, u32[]{:S(2)}, u32[]{:S(2)}) async-start(f32[128,13,512]{2,1,0:T(8,128)} %pad_maximum_fusion), calls=%async_computation | async-start | bytes 8388608 | tf_op jit(solution)/shard_map/all_to_all | solution.py:69
  148.0 5.0 %copy-start.5 = (f32[512]{0:T(512)S(1)}, f32[512]{0:T(512)}, u32[]{:S(2)}) copy-start(f32[512]{0:T(512)} %param.11) | copy-start | bytes 6148
  148.0 5.0 %copy-start.6 = (f32[512]{0:T(512)S(1)}, f32[512]{0:T(512)}, u32[]{:S(2)}) copy-start(f32[512]{0:T(512)} %param.10) | copy-start | bytes 6148
  158.4 11.8 %collective-permute-start = (bf16[2,8,32,512]{3,0,2,1:T(2,128)(2,1)S(1)}, bf16[2,8,32,512]{3,0,2,1:T(2,128)(2,1)S(1)}, u32[]{:S(2)}, u32[]{:S(2)}) collective-permute-start(bf16[2,8,32,512]{3,0,2,1:T(2,128)(2,1)S(1)} %slice.146), channel_id=1, source_target_pairs={{0,4},{4,8},{8,12},{12,16},{16,20},{20,24},{24,28},{1,5},{5,9},{9,... | collective-permute-start | bytes 1572872 | tf_op jit(solution)/shard_map/ppermute | solution.py:17
  170.4 9.2 %collective-permute-start.1 = (bf16[8,1,32,512]{3,0,2,1:T(8,128)(2,1)S(1)}, bf16[8,1,32,512]{3,0,2,1:T(8,128)(2,1)S(1)}, u32[]{:S(2)}, u32[]{:S(2)}) collective-permute-start(bf16[8,1,32,512]{3,0,2,1:T(8,128)(2,1)S(1)} %get-tuple-element.16), channel_id=1, source_target_pairs={{0,1},{1,2},{2,3},{4,5},{5,6},{6,7},{8,9},{9,10},{10,11},{12,13},{... | collective-permute-start | bytes 786440 | tf_op jit(solution)/shard_map/ppermute | solution.py:27
  176.4 9.2 %collective-permute-start.2 = (bf16[8,1,32,512]{3,0,2,1:T(8,128)(2,1)S(1)}, bf16[8,1,32,512]{3,0,2,1:T(8,128)(2,1)S(1)}, u32[]{:S(2)}, u32[]{:S(2)}) collective-permute-start(bf16[8,1,32,512]{3,0,2,1:T(8,128)(2,1)S(1)} %get-tuple-element.17), channel_id=1, source_target_pairs={{1,0},{2,1},{3,2},{5,4},{6,5},{7,6},{9,8},{10,9},{11,10},{13,12},{... | collective-permute-start | bytes 786440 | tf_op jit(solution)/shard_map/ppermute | solution.py:28
  185.6 3.6 %collective-permute-start.3 = (bf16[8,10,1,512]{3,0,2,1:T(8,128)(2,1)S(1)}, bf16[8,10,1,512]{3,0,2,1:T(8,128)(2,1)S(1)}, u32[]{:S(2)}, u32[]{:S(2)}) collective-permute-start(bf16[8,10,1,512]{3,0,2,1:T(8,128)(2,1)S(1)} %get-tuple-element.11), channel_id=1, source_target_pairs={{0,32},{32,64},{64,96},{1,33},{33,65},{65,97},{2,34},{34,66},{66,9... | collective-permute-start | bytes 245768 | tf_op jit(solution)/shard_map/ppermute | solution.py:27
  187.5 6.3 %collective-permute-start.4 = (bf16[8,10,1,512]{3,0,2,1:T(8,128)(2,1)S(1)}, bf16[8,10,1,512]{3,0,2,1:T(8,128)(2,1)S(1)}, u32[]{:S(2)}, u32[]{:S(2)}) collective-permute-start(bf16[8,10,1,512]{3,0,2,1:T(8,128)(2,1)S(1)} %get-tuple-element.12), channel_id=1, source_target_pairs={{32,0},{64,32},{96,64},{33,1},{65,33},{97,65},{34,2},{66,34},{98,6... | collective-permute-start | bytes 245768 | tf_op jit(solution)/shard_map/ppermute | solution.py:28
  241.0 1.1 copy-start.8
  263.9 2.3 copy-start.1
  263.9 2.3 copy-start.7
where the time goes:
time: 272 us; the launch traced here: 271 us
  waiting for transfers between devices  74.3 us (27%)
  other arithmetic  62.7 us (23%)
  matrix products  62 us (23%)
  local copies, waits for them, and re-layouts  45.8 us (17%)
  starting transfers between devices  25.4 us (9%)
    conv_general_dilated x3, matrix products, shards(): lax.conv_general_dilated(padded[tap_time:tap_time + FR_DEV], conv_weight[...  61 us
    all_to_all x1, waiting for transfers between devices, shards(): lax.all_to_all(payload, ('src', 'frame', 'tile'), split_axis=0, concat_ax...  52.3 us
    select_n x1, other arithmetic, shards(): row_clip = jnp.take(clip_ids, row_frame)  29.5 us
    all_to_all x1, starting transfers between devices, shards(): lax.all_to_all(payload, ('src', 'frame', 'tile'), split_axis=0, concat_ax...  12.4 us
    ppermute x2, waiting for transfers between devices, with_halo(): after = lax.ppermute(leading, axis, down)  10.5 us
    ppermute x1, waiting for transfers between devices, passed_along(): return lax.ppermute(x, axis, pairs)  10.1 us
    gather x1, local copies, waits for them, and re-layouts, shards(): slot_ids[ordering].astype(jnp.float32).reshape(devices, per_pair)  8.38 us
    ppermute x2, starting transfers between devices, with_halo(): before = lax.ppermute(last, axis, up)  7.79 us
  transfers between devices with their start and end apart: 6, of which 5 were waited for; matrix products, arithmetic and copies ran while one was open for 0% of the time, Pallas kernels for 0%

commit v1 on v0

--- a/solution.py
+++ b/solution.py
@@ -1,6 +1,8 @@
 import jax
 import jax.numpy as jnp
 from jax import lax
+from jax.experimental import pallas as pl
+from jax.experimental.pallas import tpu as pltpu
 from jax.sharding import PartitionSpec as P
 
 GROUPS = 32
@@ -42,35 +44,54 @@
 
     owners = row_map // local_rows
     slot_ids = row_map % local_rows
+    frames = clip_ids.shape[0]
     row_frame = (owners // n_tile) % n_frame * FR_DEV + slot_ids // per_frame
-    row_clip = jnp.take(clip_ids, row_frame)
-    row_onehot = (row_clip[:, None] == jnp.arange(CLIPS, dtype=jnp.int32)[None, :]).astype(
+    frame_onehot = (row_frame[:, None] == jnp.arange(frames, dtype=jnp.int32)[None, :]).astype(
         jnp.float32
     )
-
-    grouped = feats.reshape(local_rows, GROUPS, group_width)
+    clip_onehot = (clip_ids[:, None] == jnp.arange(CLIPS, dtype=jnp.int32)[None, :]).astype(
+        jnp.float32
+    )
+    row_onehot = jnp.dot(frame_onehot, clip_onehot)
+
     local_n = jnp.sum(row_onehot, axis=0) * group_width
-    local_s = jnp.dot(row_onehot.T, jnp.sum(grouped, axis=2), precision=HIGH)
+    local_s = jnp.sum(
+        jnp.dot(row_onehot.T, feats, precision=HIGH).reshape(CLIPS, GROUPS, group_width), axis=2
+    )
     local_m = local_s / jnp.maximum(local_n, 1.0)[:, None]
-    row_m = jnp.dot(row_onehot, local_m, precision=HIGH)
-    dev = grouped - row_m[:, :, None]
-    local_m2 = jnp.dot(row_onehot.T, jnp.sum(dev * dev, axis=2), precision=HIGH)
-
-    ordering = jnp.argsort(owners, stable=True)
-    outgoing = feats[ordering].reshape(devices, per_pair, channels)
-    sent_slots = slot_ids[ordering].astype(jnp.float32).reshape(devices, per_pair)
+    row_m = jnp.dot(row_onehot, jnp.repeat(local_m, group_width, axis=1), precision=HIGH)
+    dev = feats - row_m
+    local_m2 = jnp.sum(
+        jnp.dot(row_onehot.T, dev * dev, precision=HIGH).reshape(CLIPS, GROUPS, group_width),
+        axis=2,
+    )
+
+    block = 16
+    iota = lax.iota(jnp.int32, local_rows)
+    _, sent_slots, ordering = lax.sort((owners, slot_ids, iota), num_keys=1, is_stable=True)
     stats = jnp.concatenate([local_n, local_s.reshape(-1), local_m2.reshape(-1)])
-    tail = jnp.zeros((channels - per_pair - stats.shape[0],), jnp.float32)
-    extra = jnp.concatenate(
-        [sent_slots, jnp.broadcast_to(jnp.concatenate([stats, tail]), (devices, channels - per_pair))],
+    info = jnp.concatenate(
+        [
+            sent_slots.astype(jnp.float32).reshape(devices, per_pair),
+            jnp.broadcast_to(stats, (devices, stats.shape[0])),
+            jnp.zeros((devices, channels - per_pair - stats.shape[0]), jnp.float32),
+        ],
         axis=1,
     )
-    payload = jnp.concatenate([outgoing, extra[:, None, :]], axis=1)
+    table = jnp.concatenate([feats, info, jnp.zeros((1, channels), jnp.float32)], axis=0)
+    pick = jnp.concatenate(
+        [
+            ordering.reshape(devices, per_pair),
+            local_rows + jnp.arange(devices, dtype=jnp.int32)[:, None],
+            jnp.full((devices, block - per_pair - 1), local_rows + devices, jnp.int32),
+        ],
+        axis=1,
+    )
+    payload = table[pick.reshape(-1)].reshape(devices, block, channels)
     arrived = lax.all_to_all(
         payload, ("src", "frame", "tile"), split_axis=0, concat_axis=0, tiled=True
     )
 
-    rows = arrived[:, :per_pair, :].reshape(-1, channels)
     info = arrived[:, per_pair, :]
     targets = info[:, :per_pair].reshape(-1).astype(jnp.int32)
     part_n = info[:, per_pair : per_pair + CLIPS]
@@ -86,8 +107,9 @@
     clip_m2 = jnp.sum(part_m2, axis=0) + jnp.sum(part_n[:, :, None] * spread * spread, axis=0)
     clip_var = clip_m2 / total_n[:, None]
 
-    inverse = jnp.argsort(targets)
-    features = rows[inverse].reshape(FR_DEV, HR, WCOL, channels)
+    arrival_row = (iota // per_pair) * block + iota % per_pair
+    _, gather_rows = lax.sort((targets, arrival_row), num_keys=1)
+    features = arrived.reshape(-1, channels)[gather_rows].reshape(FR_DEV, HR, WCOL, channels)
 
     first_frame = lax.axis_index("frame") * FR_DEV
     padded_ids = jnp.concatenate([jnp.full((2,), -1, jnp.int32), clip_ids])
@@ -104,20 +126,59 @@
     previous = passed_along(activated[FR_DEV - 2 :], "frame", 1)
     extended = jnp.concatenate([previous, activated], axis=0)
     padded = with_halo(extended, (("tile", 1), ("src", 2)), 1)
-    conv_sum = jnp.zeros((FR_DEV, HR, WCOL, channels), jnp.float32)
-    for tap_time in range(3):
-        validity = (window_ids[tap_time : tap_time + FR_DEV] == own_ids).astype(jnp.float32)
-        partial_value = lax.conv_general_dilated(
-            padded[tap_time : tap_time + FR_DEV],
-            conv_weight[tap_time],
-            (1, 1),
-            "VALID",
-            dimension_numbers=("NHWC", "HWIO", "NHWC"),
-            preferred_element_type=jnp.float32,
-        )
-        conv_sum = conv_sum + partial_value * validity[:, None, None, None]
-    decoded = features + conv_sum + conv_bias
-    return decoded.astype(jnp.bfloat16)
+    widened = jnp.concatenate([padded[:, :, e : e + WCOL] for e in range(3)], axis=-1)
+    validity = jnp.stack(
+        [(window_ids[a : a + FR_DEV] == own_ids).astype(jnp.int32) for a in range(3)]
+    ).reshape(-1)
+    weights = conv_weight.reshape(9, 3 * channels, channels)
+    return causal_conv(validity, widened, weights, features, conv_bias.reshape(1, channels))
+
+
+def conv_kernel(valid_ref, x_ref, w_ref, f_ref, b_ref, o_ref, acc_ref):
+    tap_time = pl.program_id(0)
+    tap_high = pl.program_id(1)
+
+    @pl.when((tap_time == 0) & (tap_high == 0))
+    def _():
+        acc_ref[...] = jnp.zeros_like(acc_ref)
+
+    for t in range(FR_DEV):
+
+        @pl.when(valid_ref[tap_time * FR_DEV + t] != 0)
+        def _():
+            lhs = x_ref[tap_time + t, pl.ds(tap_high, HR)].reshape(HR * WCOL, -1)
+            acc_ref[t] += jnp.dot(lhs, w_ref[0], preferred_element_type=jnp.float32)
+
+    @pl.when((tap_time == 2) & (tap_high == 2))
+    def _():
+        conv_sum = acc_ref[...].reshape(o_ref.shape)
+        o_ref[...] = ((f_ref[...] + conv_sum) + b_ref[...]).astype(o_ref.dtype)
+
+
+def causal_conv(validity, widened, weights, features, bias):
+    frames, high, wide, channels = features.shape
+    whole = lambda *shape: pl.BlockSpec(
+        shape, lambda a, b, v: (0,) * len(shape), pipeline_mode=pl.Buffered(1)
+    )
+    return pl.pallas_call(
+        conv_kernel,
+        grid_spec=pltpu.PrefetchScalarGridSpec(
+            num_scalar_prefetch=1,
+            grid=(3, 3),
+            in_specs=[
+                whole(*widened.shape),
+                pl.BlockSpec((1,) + weights.shape[1:], lambda a, b, v: (a * 3 + b, 0, 0)),
+                whole(*features.shape),
+                whole(*bias.shape),
+            ],
+            out_specs=pl.BlockSpec(features.shape, lambda a, b, v: (0, 0, 0, 0)),
+            scratch_shapes=[pltpu.VMEM((frames, high * wide, channels), jnp.float32)],
+        ),
+        out_shape=jax.ShapeDtypeStruct(features.shape, jnp.bfloat16),
+        compiler_params=pltpu.CompilerParams(
+            dimension_semantics=("arbitrary", "arbitrary"), vmem_limit_bytes=60 * 1024 * 1024
+        ),
+    )(validity, widened, weights, features, bias)
 
 
 def solution(mesh):

time: 272 us -> 206 us (0.76)
  the two profiles are of different devices: /device:TPU:1 before, /device:TPU:57 now
where the time goes in v1:
time: 206 us; the launch traced here: 205 us
  waiting for transfers between devices  74 us (36%)
  Pallas kernels  38.2 us (19%)
  other arithmetic  37.9 us (18%)
  starting transfers between devices  23.5 us (11%)
  local copies, waits for them, and re-layouts  21.6 us (10%)
  matrix products  9.41 us (5%)
    all_to_all x1, waiting for transfers between devices, shards(): lax.all_to_all(payload, ('src', 'frame', 'tile'), split_axis=0, concat_ax...  49.4 us
    pallas_call x1, Pallas kernels, causal_conv(): pl.pallas_call(conv_kernel, grid_spec=pltpu.PrefetchScalarGridSpec(num_sc...  38.2 us
    concatenate x1, other arithmetic, shards(): jnp.concatenate([padded[:, :, e:e + WCOL] for e in range(3)], axis=-1)  17.4 us
    ppermute x1, waiting for transfers between devices, passed_along(): return lax.ppermute(x, axis, pairs)  13.3 us
    all_to_all x1, starting transfers between devices, shards(): lax.all_to_all(payload, ('src', 'frame', 'tile'), split_axis=0, concat_ax...  10.9 us
    ppermute x2, waiting for transfers between devices, with_halo(): after = lax.ppermute(leading, axis, down)  9.73 us
    gather x1, local copies, waits for them, and re-layouts, shards(): payload = table[pick.reshape(-1)].reshape(devices, block, channels)  8.92 us
    ppermute x2, starting transfers between devices, with_halo(): before = lax.ppermute(last, axis, up)  8.09 us
  transfers between devices with their start and end apart: 6, of which 6 were waited for; matrix products, arithmetic and copies ran while one was open for 0% of the time, Pallas kernels for 0%

profile of v1, /device:TPU:57, one launch (start us, length us, event | category | flops | bytes accessed | tf_op | source)
XLA Modules:
  0.0 205.0 jit_solution(7239322157796114981)
XLA Ops:
  0.0 0.9 add_select_fusion.4
  0.9 5.1 %sort.44 = (s32[1536]{0:T(1024)}, s32[1536]{0:T(1024)S(1)}, s32[1536]{0:T(1024)S(1)}) sort(s32[1536]{0:T(1024)S(1)} %get-tuple-element.24, s32[1536]{0:T(1024)S(1)} %get-tuple-element.22, s32[1536]{0:T(1024)S(1)} %iota.22), dimensions={0}, to_apply=%region_0.1 | sort | flops 16896 | bytes 36864 | tf_op jit(solution)/shard_map/sort | solution.py:71
  6.0 1.2 fusion.40
  7.2 3.5 %fusion.41 = f32[4,512]{1,0:T(4,128)S(1)} fusion(f32[1536,4]{0,1:T(4,128)S(1)} %get-tuple-element.30, f32[1536,512]{1,0:T(8,128)} %param.7), kind=kOutput, calls=%fused_computation.105 | convolution fusion | flops 37748736 | bytes 3178496 | tf_op jit(solution)/shard_map/dot_general | solution.py:59
  11.8 2.8 %fusion.2 = f32[1536,512]{1,0:T(8,128)S(1)} fusion(f32[1536,512]{1,0:T(8,128)S(1)} %copy-done, f32[1536,4]{0,1:T(4,128)S(1)} %get-tuple-element.30, f32[4,512]{1,0:T(4,128)S(1)} %reshape.123), kind=kOutput, calls=%fused_computation.14 | convolution fusion | flops 39321600 | bytes 6324224 | tf_op jit(solution)/shard_map/dot_general | solution.py:62
  14.5 1.6 fusion.42
  16.5 5.2 %maximum_maximum_fusion = f32[1665,512]{1,0:T(8,128)S(1)} fusion(f32[128,240]{1,0:T(8,128)S(1)} %broadcast_in_dim.14, f32[128,260]{1,0:T(8,128)S(1)} %broadcast_in_dim.13, f32[128,12]{1,0:T(8,128)S(1)} %reshape.120, f32[1536,512]{1,0:T(8,128)} %param.7, f32[1665]{0:T(1024)S(1)} %pad.30.clone), kind=kLoop, calls=%fused_computation.12 | loop fusion | flops 3409920 | bytes 6824452 | tf_op jit(solution)/shard_map/concatenate | solution.py:81
  21.8 8.9 %gather_fusion = f32[2048,512]{1,0:T(8,128)} fusion(f32[1665,512]{1,0:T(8,128)S(1)} %maximum_maximum_fusion, s32[2048]{0:T(1024)S(1)} %broadcast_clamp_fusion), kind=kCustom, calls=%fused_computation | custom fusion | bytes 8396800 | tf_op jit(solution)/shard_map/gather | solution.py:90
  30.7 10.9 %all-to-all-start = ((f32[128,16,512]{2,1,0:T(8,128)}), f32[128,16,512]{2,1,0:T(8,128)}, u32[]{:S(2)}, u32[]{:S(2)}) async-start(f32[128,16,512]{2,1,0:T(8,128)} %bitcast.31), calls=%async_computation | async-start | bytes 8388608 | tf_op jit(solution)/shard_map/all_to_all | solution.py:91
  41.7 49.4 %all-to-all-done = f32[128,16,512]{2,1,0:T(8,128)} async-done(((f32[128,16,512]{2,1,0:T(8,128)}), f32[128,16,512]{2,1,0:T(8,128)}, u32[]{:S(2)}, u32[]{:S(2)}) %all-to-all-start) | async-done | bytes 4194336 | tf_op jit(solution)/shard_map/all_to_all | solution.py:91
  91.2 1.9 slice.67
  93.0 0.1 copy.17
  93.7 0.2 fusion.5
  93.9 0.2 fusion.25
  94.1 0.2 fusion.26
  94.6 5.1 %sort.45 = (s32[1536]{0:T(1024)}, s32[1536]{0:T(1024)S(1)}, s32[1536]{0:T(1024)}) sort(s32[1536]{0:T(1024)S(1)} %convert_element_type.22, s32[1536]{0:T(1024)S(1)} %fusion.15, s32[1536]{0:T(1024)S(1)} %iota.25), dimensions={0}, to_apply=%region_4.5 | sort | flops 16896 | bytes 36864 | tf_op jit(solution)/shard_map/sort | solution.py:111
  100.1 8.0 %gather_fusion.1 = f32[1536,512]{1,0:T(8,128)} fusion(f32[2048,512]{1,0:T(8,128)} %bitcast.4, s32[2048]{0:T(1024)S(1)} %pad_clamp_fusion), kind=kCustom, calls=%fused_computation.1 | custom fusion | bytes 6297600 | tf_op jit(solution)/shard_map/gather | solution.py:112
  108.1 2.9 %multiply_convert_fusion = bf16[6,8,32,512]{3,2,1,0:T(8,128)(2,1)S(1)} fusion(f32[6,8,32,512]{3,2,1,0:T(8,128)} %bitcast.29, f32[512]{0:T(512)S(1)} %copy-done.1, f32[512]{0:T(512)S(1)} %copy-done.2, f32[6,512]{1,0:T(8,128)S(1)} %mul.77, f32[6,512]{1,0:T(8,128)S(1)} %sub.49), kind=kLoop, calls=%fused_computation.15 | loop fusion | flops 7077888 | bytes 4747264 | tf_op jit(solution)/shard_map/convert_element_type | solution.py:125
  111.1 1.3 collective-permute-start
  112.4 13.3 %collective-permute-done = bf16[2,8,32,512]{3,2,1,0:T(8,128)(2,1)S(1)} collective-permute-done((bf16[2,8,32,512]{3,2,1,0:T(8,128)(2,1)S(1)}, bf16[2,8,32,512]{3,2,1,0:T(8,128)(2,1)S(1)}, u32[]{:S(2)}, u32[]{:S(2)}) %collective-permute-start) | collective-permute-done | bytes 524320 | tf_op jit(solution)/shard_map/ppermute | solution.py:19
  125.8 4.4 %collective-permute-start.1 = (bf16[8,1,32,512]{3,2,1,0:T(8,128)(2,1)S(1)}, bf16[8,1,32,512]{3,2,1,0:T(8,128)(2,1)S(1)}, u32[]{:S(2)}, u32[]{:S(2)}) collective-permute-start(bf16[8,1,32,512]{3,2,1,0:T(8,128)(2,1)S(1)} %get-tuple-element.17), channel_id=1, source_target_pairs={{0,1},{1,2},{2,3},{4,5},{5,6},{6,7},{8,9},{9,10},{10,11},{12,13},{... | collective-permute-start | bytes 786440 | tf_op jit(solution)/shard_map/ppermute | solution.py:29
  130.1 1.9 collective-permute-start.2
  132.2 1.2 collective-permute-done.1
  133.4 5.9 %collective-permute-done.2 = bf16[8,1,32,512]{3,2,1,0:T(8,128)(2,1)S(1)} collective-permute-done((bf16[8,1,32,512]{3,2,1,0:T(8,128)(2,1)S(1)}, bf16[8,1,32,512]{3,2,1,0:T(8,128)(2,1)S(1)}, u32[]{:S(2)}, u32[]{:S(2)}) %collective-permute-start.2) | collective-permute-done | bytes 262176 | tf_op jit(solution)/shard_map/ppermute | solution.py:30
  139.3 0.3 pad_maximum_fusion.13
  139.6 3.7 %collective-permute-start.3 = (bf16[8,10,1,512]{3,2,1,0:T(2,128)(2,1)S(1)}, bf16[8,10,1,512]{3,2,1,0:T(2,128)(2,1)S(1)}, u32[]{:S(2)}, u32[]{:S(2)}) collective-permute-start(bf16[8,10,1,512]{3,2,1,0:T(2,128)(2,1)S(1)} %get-tuple-element.15), channel_id=1, source_target_pairs={{0,32},{32,64},{64,96},{1,33},{33,65},{65,97},{2,34},{34,66},{66,9... | collective-permute-start | bytes 245768 | tf_op jit(solution)/shard_map/ppermute | solution.py:29
  143.3 1.3 collective-permute-start.4
  144.7 0.6 reshape.119.valid_ref
  145.3 0.3 collective-permute-done.3
  145.6 3.8 %collective-permute-done.4 = bf16[8,10,1,512]{3,2,1,0:T(2,128)(2,1)S(1)} collective-permute-done((bf16[8,10,1,512]{3,2,1,0:T(2,128)(2,1)S(1)}, bf16[8,10,1,512]{3,2,1,0:T(2,128)(2,1)S(1)}, u32[]{:S(2)}, u32[]{:S(2)}) %collective-permute-start.4) | collective-permute-done | bytes 81952 | tf_op jit(solution)/shard_map/ppermute | solution.py:30
  149.4 17.4 %fusion.x_ref = bf16[8,10,32,1536]{3,2,1,0:T(8,128)(2,1)} fusion(bf16[8,10,1,512]{3,2,1,0:T(2,128)(2,1)S(1)} %collective-permute-done.4, bf16[8,1,32,512]{3,2,1,0:T(8,128)(2,1)S(1)} %collective-permute-done.2, bf16[8,1,32,512]{3,2,1,0:T(8,128)(2,1)S(1)} %collective-permute-done.1, bf16[6,8,32,512]{3,2,1,0:T(8,128)(2,1)S(1)} %multiply_convert_fusion, ...), kind=kLoop, calls=%fused_computation.3 | loop fusion | flops 110100480 | bytes 10649600 | tf_op jit(solution)/shard_map/concatenate | solution.py:129
  166.8 38.2 %shard_map.73 = bf16[6,8,32,512]{3,2,1,0:T(8,128)(2,1)} custom-call(s32[18]{0:T(128)} %reshape.119.valid_ref, bf16[8,10,32,1536]{3,2,1,0:T(8,128)(2,1)} %fusion.x_ref, bf16[9,1536,512]{2,1,0:T(8,128)(2,1)} %bitcast.32, f32[6,8,32,512]{3,2,1,0:T(8,128)} %bitcast.30, f32[1,512]{1,0:T(1,128)} %bitcast.38), custom_call_target="tpu_custom_call" | custom-call | tf_op jit(solution)/shard_map/pallas_call | solution.py:163
  (59 shorter events, 3.1 us)
Async XLA Ops:
  0.0 11.8 %copy-start = (f32[1536,512]{1,0:T(8,128)S(1)}, f32[1536,512]{1,0:T(8,128)}, u32[]{:S(2)}) copy-start(f32[1536,512]{1,0:T(8,128)} %param.7) | copy-start | bytes 9437188
  30.7 10.9 %copy-start.3 = (s32[48]{0:T(128)S(1)}, s32[48]{0:T(128)}, u32[]{:S(2)}) copy-start(s32[48]{0:T(128)} %param.9) | copy-start | bytes 580
  30.7 60.5 %all-to-all-start = ((f32[128,16,512]{2,1,0:T(8,128)}), f32[128,16,512]{2,1,0:T(8,128)}, u32[]{:S(2)}, u32[]{:S(2)}) async-start(f32[128,16,512]{2,1,0:T(8,128)} %bitcast.31), calls=%async_computation | async-start | bytes 8388608 | tf_op jit(solution)/shard_map/all_to_all | solution.py:91
  100.1 8.0 %copy-start.1 = (f32[512]{0:T(512)S(1)}, f32[512]{0:T(512)}, u32[]{:S(2)}) copy-start(f32[512]{0:T(512)} %param.11) | copy-start | bytes 6148
  100.1 8.0 %copy-start.2 = (f32[512]{0:T(512)S(1)}, f32[512]{0:T(512)}, u32[]{:S(2)}) copy-start(f32[512]{0:T(512)} %param.10) | copy-start | bytes 6148
  111.1 14.6 %collective-permute-start = (bf16[2,8,32,512]{3,2,1,0:T(8,128)(2,1)S(1)}, bf16[2,8,32,512]{3,2,1,0:T(8,128)(2,1)S(1)}, u32[]{:S(2)}, u32[]{:S(2)}) collective-permute-start(bf16[2,8,32,512]{3,2,1,0:T(8,128)(2,1)S(1)} %slice.72), channel_id=1, source_target_pairs={{0,4},{4,8},{8,12},{12,16},{16,20},{20,24},{24,28},{1,5},{5,9},{9,... | collective-permute-start | bytes 1572872 | tf_op jit(solution)/shard_map/ppermute | solution.py:19
  125.8 7.7 %collective-permute-start.1 = (bf16[8,1,32,512]{3,2,1,0:T(8,128)(2,1)S(1)}, bf16[8,1,32,512]{3,2,1,0:T(8,128)(2,1)S(1)}, u32[]{:S(2)}, u32[]{:S(2)}) collective-permute-start(bf16[8,1,32,512]{3,2,1,0:T(8,128)(2,1)S(1)} %get-tuple-element.17), channel_id=1, source_target_pairs={{0,1},{1,2},{2,3},{4,5},{5,6},{6,7},{8,9},{9,10},{10,11},{12,13},{... | collective-permute-start | bytes 786440 | tf_op jit(solution)/shard_map/ppermute | solution.py:29
  130.1 9.2 %collective-permute-start.2 = (bf16[8,1,32,512]{3,2,1,0:T(8,128)(2,1)S(1)}, bf16[8,1,32,512]{3,2,1,0:T(8,128)(2,1)S(1)}, u32[]{:S(2)}, u32[]{:S(2)}) collective-permute-start(bf16[8,1,32,512]{3,2,1,0:T(8,128)(2,1)S(1)} %get-tuple-element.18), channel_id=1, source_target_pairs={{1,0},{2,1},{3,2},{5,4},{6,5},{7,6},{9,8},{10,9},{11,10},{13,12},{... | collective-permute-start | bytes 786440 | tf_op jit(solution)/shard_map/ppermute | solution.py:30
  139.6 6.0 %collective-permute-start.3 = (bf16[8,10,1,512]{3,2,1,0:T(2,128)(2,1)S(1)}, bf16[8,10,1,512]{3,2,1,0:T(2,128)(2,1)S(1)}, u32[]{:S(2)}, u32[]{:S(2)}) collective-permute-start(bf16[8,10,1,512]{3,2,1,0:T(2,128)(2,1)S(1)} %get-tuple-element.15), channel_id=1, source_target_pairs={{0,32},{32,64},{64,96},{1,33},{33,65},{65,97},{2,34},{34,66},{66,9... | collective-permute-start | bytes 245768 | tf_op jit(solution)/shard_map/ppermute | solution.py:29
  143.3 6.1 %collective-permute-start.4 = (bf16[8,10,1,512]{3,2,1,0:T(2,128)(2,1)S(1)}, bf16[8,10,1,512]{3,2,1,0:T(2,128)(2,1)S(1)}, u32[]{:S(2)}, u32[]{:S(2)}) collective-permute-start(bf16[8,10,1,512]{3,2,1,0:T(2,128)(2,1)S(1)} %get-tuple-element.16), channel_id=1, source_target_pairs={{32,0},{64,32},{96,64},{33,1},{65,33},{97,65},{34,2},{66,34},{98,6... | collective-permute-start | bytes 245768 | tf_op jit(solution)/shard_map/ppermute | solution.py:30

commit v2 on v1

--- a/solution.py
+++ b/solution.py
@@ -54,15 +54,17 @@
     )
     row_onehot = jnp.dot(frame_onehot, clip_onehot)
 
+    clip_mask = row_onehot.T[:, :, None]
     local_n = jnp.sum(row_onehot, axis=0) * group_width
     local_s = jnp.sum(
-        jnp.dot(row_onehot.T, feats, precision=HIGH).reshape(CLIPS, GROUPS, group_width), axis=2
+        jnp.sum(feats[None] * clip_mask, axis=1).reshape(CLIPS, GROUPS, group_width), axis=2
     )
     local_m = local_s / jnp.maximum(local_n, 1.0)[:, None]
-    row_m = jnp.dot(row_onehot, jnp.repeat(local_m, group_width, axis=1), precision=HIGH)
+    wide_m = jnp.repeat(local_m, group_width, axis=1)
+    row_m = jnp.sum(clip_mask * wide_m[:, None, :], axis=0)
     dev = feats - row_m
     local_m2 = jnp.sum(
-        jnp.dot(row_onehot.T, dev * dev, precision=HIGH).reshape(CLIPS, GROUPS, group_width),
+        jnp.sum((dev * dev)[None] * clip_mask, axis=1).reshape(CLIPS, GROUPS, group_width),
         axis=2,
     )
 
@@ -78,16 +80,12 @@
         ],
         axis=1,
     )
-    table = jnp.concatenate([feats, info, jnp.zeros((1, channels), jnp.float32)], axis=0)
     pick = jnp.concatenate(
-        [
-            ordering.reshape(devices, per_pair),
-            local_rows + jnp.arange(devices, dtype=jnp.int32)[:, None],
-            jnp.full((devices, block - per_pair - 1), local_rows + devices, jnp.int32),
-        ],
+        [ordering.reshape(devices, per_pair), jnp.zeros((devices, block - per_pair), jnp.int32)],
         axis=1,
     )
-    payload = table[pick.reshape(-1)].reshape(devices, block, channels)
+    payload = feats[pick.reshape(-1)].reshape(devices, block, channels)
+    payload = lax.dynamic_update_slice(payload, info[:, None, :], (0, per_pair, 0))
     arrived = lax.all_to_all(
         payload, ("src", "frame", "tile"), split_axis=0, concat_axis=0, tiled=True
     )
@@ -123,18 +121,42 @@
     frame_inv = jnp.dot(onehot, inverse_std, precision=HIGH)
     normed = (centred * frame_inv[:, None, :, None]).reshape(FR_DEV, HR, WCOL, channels)
     activated = jax.nn.silu(normed * norm_gain + norm_bias).astype(jnp.bfloat16)
-    previous = passed_along(activated[FR_DEV - 2 :], "frame", 1)
-    extended = jnp.concatenate([previous, activated], axis=0)
-    padded = with_halo(extended, (("tile", 1), ("src", 2)), 1)
-    widened = jnp.concatenate([padded[:, :, e : e + WCOL] for e in range(3)], axis=-1)
+    zero_col = jnp.zeros((FR_DEV, HR + 2, 1, channels), jnp.bfloat16)
+    high_padded = with_halo(activated, (("tile", 1),), 1)
+    n_wide = lax.axis_size("src")
+    up = [(i, i + 1) for i in range(n_wide - 1)]
+    left = lax.ppermute(high_padded[:, :, WCOL - 1 :], "src", up)
+    right = lax.ppermute(high_padded[:, :, :1], "src", [(j, i) for i, j in up])
+    own_wide = widen(high_padded, zero_col, left, right)
+    sent_prev = jnp.concatenate(
+        [high_padded[FR_DEV - 2 :], left[FR_DEV - 2 :], right[FR_DEV - 2 :]], axis=2
+    )
+    prev = passed_along(sent_prev, "frame", 1)
+    prev_wide = widen(prev[:, :, :WCOL], zero_col[:2], prev[:, :, WCOL : WCOL + 1], prev[:, :, WCOL + 1 :])
+
     validity = jnp.stack(
         [(window_ids[a : a + FR_DEV] == own_ids).astype(jnp.int32) for a in range(3)]
-    ).reshape(-1)
+    )
+    reach = jnp.arange(3)[:, None] + jnp.arange(FR_DEV)[None, :]
+    own_valid = jnp.where(reach >= 2, validity, 0).reshape(-1)
+    prev_valid = jnp.where(reach < 2, validity, 0)[:2, :2].reshape(-1)
     weights = conv_weight.reshape(9, 3 * channels, channels)
-    return causal_conv(validity, widened, weights, features, conv_bias.reshape(1, channels))
-
-
-def conv_kernel(valid_ref, x_ref, w_ref, f_ref, b_ref, o_ref, acc_ref):
+    partial_sum = own_conv(own_valid, own_wide, weights)
+    return prev_conv(
+        prev_valid, prev_wide, weights, partial_sum, features, conv_bias.reshape(1, channels)
+    )
+
+
+def widen(block, zero_col, left, right):
+    shifted_in = jnp.concatenate([zero_col, block[:, :, : WCOL - 1]], axis=2)
+    shifted_out = jnp.concatenate([block[:, :, 1:], zero_col], axis=2)
+    wide = jnp.concatenate([shifted_in, block, shifted_out], axis=-1)
+    channels = block.shape[-1]
+    wide = lax.dynamic_update_slice(wide, left, (0, 0, 0, 0))
+    return lax.dynamic_update_slice(wide, right, (0, 0, WCOL - 1, 2 * channels))
+
+
+def own_kernel(valid_ref, x_ref, w_ref, acc_ref):
     tap_time = pl.program_id(0)
     tap_high = pl.program_id(1)
 
@@ -146,39 +168,78 @@
 
         @pl.when(valid_ref[tap_time * FR_DEV + t] != 0)
         def _():
-            lhs = x_ref[tap_time + t, pl.ds(tap_high, HR)].reshape(HR * WCOL, -1)
+            frame = jnp.maximum(tap_time + t - 2, 0)
+            lhs = x_ref[frame, pl.ds(tap_high, HR)].reshape(HR * WCOL, -1)
             acc_ref[t] += jnp.dot(lhs, w_ref[0], preferred_element_type=jnp.float32)
 
-    @pl.when((tap_time == 2) & (tap_high == 2))
-    def _():
-        conv_sum = acc_ref[...].reshape(o_ref.shape)
-        o_ref[...] = ((f_ref[...] + conv_sum) + b_ref[...]).astype(o_ref.dtype)
-
-
-def causal_conv(validity, widened, weights, features, bias):
-    frames, high, wide, channels = features.shape
-    whole = lambda *shape: pl.BlockSpec(
-        shape, lambda a, b, v: (0,) * len(shape), pipeline_mode=pl.Buffered(1)
-    )
+
+def own_conv(validity, wide, weights):
+    frames = wide.shape[0]
+    channels = weights.shape[-1]
     return pl.pallas_call(
-        conv_kernel,
+        own_kernel,
         grid_spec=pltpu.PrefetchScalarGridSpec(
             num_scalar_prefetch=1,
             grid=(3, 3),
             in_specs=[
-                whole(*widened.shape),
+                pl.BlockSpec(wide.shape, lambda a, b, v: (0, 0, 0, 0), pipeline_mode=pl.Buffered(1)),
                 pl.BlockSpec((1,) + weights.shape[1:], lambda a, b, v: (a * 3 + b, 0, 0)),
-                whole(*features.shape),
-                whole(*bias.shape),
+            ],
+            out_specs=pl.BlockSpec((frames, HR * WCOL, channels), lambda a, b, v: (0, 0, 0)),
+        ),
+        out_shape=jax.ShapeDtypeStruct((frames, HR * WCOL, channels), jnp.float32),
+        compiler_params=pltpu.CompilerParams(
+            dimension_semantics=("arbitrary", "arbitrary"), vmem_limit_bytes=60 * 1024 * 1024
+        ),
+    )(validity, wide, weights)
+
+
+def prev_kernel(valid_ref, x_ref, w_ref, part_ref, f_ref, b_ref, o_ref, acc_ref):
+    tap_time = pl.program_id(0)
+    tap_high = pl.program_id(1)
+
+    @pl.when((tap_time == 0) & (tap_high == 0))
+    def _():
+        acc_ref[...] = part_ref[...]
+
+    for t in range(2):
+
+        @pl.when(valid_ref[tap_time * 2 + t] != 0)
+        def _():
+            frame = jnp.minimum(tap_time + t, 1)
+            lhs = x_ref[frame, pl.ds(tap_high, HR)].reshape(HR * WCOL, -1)
+            acc_ref[t] += jnp.dot(lhs, w_ref[0], preferred_element_type=jnp.float32)
+
+    @pl.when((tap_time == 1) & (tap_high == 2))
+    def _():
+        conv_sum = acc_ref[...].reshape(o_ref.shape)
+        o_ref[...] = ((f_ref[...] + conv_sum) + b_ref[...]).astype(o_ref.dtype)
+
+
+def prev_conv(validity, wide, weights, partial_sum, features, bias):
+    whole = lambda shape: pl.BlockSpec(
+        shape, lambda a, b, v: (0,) * len(shape), pipeline_mode=pl.Buffered(1)
+    )
+    return pl.pallas_call(
+        prev_kernel,
+        grid_spec=pltpu.PrefetchScalarGridSpec(
+            num_scalar_prefetch=1,
+            grid=(2, 3),
+            in_specs=[
+                whole(wide.shape),
+                pl.BlockSpec((1,) + weights.shape[1:], lambda a, b, v: (a * 3 + b, 0, 0)),
+                whole(partial_sum.shape),
+                whole(features.shape),
+                whole(bias.shape),
             ],
             out_specs=pl.BlockSpec(features.shape, lambda a, b, v: (0, 0, 0, 0)),
-            scratch_shapes=[pltpu.VMEM((frames, high * wide, channels), jnp.float32)],
+            scratch_shapes=[pltpu.VMEM(partial_sum.shape, jnp.float32)],
         ),
         out_shape=jax.ShapeDtypeStruct(features.shape, jnp.bfloat16),
         compiler_params=pltpu.CompilerParams(
             dimension_semantics=("arbitrary", "arbitrary"), vmem_limit_bytes=60 * 1024 * 1024
         ),
-    )(validity, widened, weights, features, bias)
+    )(validity, wide, weights, partial_sum, features, bias)
 
 
 def solution(mesh):

time: 206 us -> 200 us (0.971)
  the two profiles are of different devices: /device:TPU:57 before, /device:TPU:1 now
where the time goes in v2:
time: 200 us; the launch traced here: 198 us
  waiting for transfers between devices  60.5 us (30%)
  local copies, waits for them, and re-layouts  45.7 us (23%)
  Pallas kernels  41.4 us (21%)
  other arithmetic  25.5 us (13%)
  starting transfers between devices  23.3 us (12%)
    all_to_all x1, waiting for transfers between devices, shards(): lax.all_to_all(payload, ('src', 'frame', 'tile'), split_axis=0, concat_ax...  52.3 us
    pallas_call x1, Pallas kernels, own_conv(): pl.pallas_call(own_kernel, grid_spec=pltpu.PrefetchScalarGridSpec(num_sca...  31.7 us
    all_to_all x1, starting transfers between devices, shards(): lax.all_to_all(payload, ('src', 'frame', 'tile'), split_axis=0, concat_ax...  12 us
    pallas_call x1, Pallas kernels, prev_conv(): pl.pallas_call(prev_kernel, grid_spec=pltpu.PrefetchScalarGridSpec(num_sc...  9.65 us
    gather x1, local copies, waits for them, and re-layouts, shards(): payload = feats[pick.reshape(-1)].reshape(devices, block, channels)  8.92 us
    gather x1, local copies, waits for them, and re-layouts, shards(): arrived.reshape(-1, channels)[gather_rows]  7.93 us
    dynamic_update_slice x1, local copies, waits for them, and re-layouts, shards(): lax.dynamic_update_slice(payload, info[:, None, :], (0, per_pair, 0))  6.35 us
    dynamic_update_slice x2, local copies, waits for them, and re-layouts, widen(): wide = lax.dynamic_update_slice(wide, left, (0, 0, 0, 0))  6.35 us
  transfers between devices with their start and end apart: 6, of which 3 were waited for; matrix products, arithmetic and copies ran while one was open for 9% of the time, Pallas kernels for 16%

profile of v2, /device:TPU:1, one launch (start us, length us, event | category | flops | bytes accessed | tf_op | source)
XLA Modules:
  0.0 198.3 jit_solution(9159429933560282581)
XLA Ops:
  0.0 0.7 fusion.24
  0.7 1.2 fusion.53
  1.9 3.3 %multiply_reduce_fusion.2 = f32[4,512]{1,0:T(4,128)S(1)} fusion(f32[4,1536]{1,0:T(4,128)S(1)} %bitcast.32, f32[1536,512]{1,0:T(8,128)} %param.7), kind=kLoop, calls=%fused_computation.4 | loop fusion | flops 6289408 | bytes 3178496 | tf_op jit(solution)/shard_map/reduce_sum | solution.py:60
  5.8 1.3 multiply_reduce_fusion.1
  7.1 0.8 subtract_multiply_fusion
  7.9 1.1 multiply_reduce_fusion
  9.3 5.1 %sort.44 = (s32[1536]{0:T(1024)}, s32[1536]{0:T(1024)S(1)}, s32[1536]{0:T(1024)S(1)}) sort(s32[1536]{0:T(1024)S(1)} %get-tuple-element.29, s32[1536]{0:T(1024)S(1)} %get-tuple-element.30, s32[1536]{0:T(1024)S(1)} %iota.28), dimensions={0}, to_apply=%region_0.1 | sort | flops 16896 | bytes 36864 | tf_op jit(solution)/shard_map/sort | solution.py:73
  15.2 8.9 %gather_fusion = f32[2048,512]{1,0:T(8,128)} fusion(f32[1536,512]{1,0:T(8,128)S(1)} %copy-done, s32[2048]{0:T(1024)S(1)} %broadcast_clamp_fusion), kind=kCustom, calls=%fused_computation | custom fusion | bytes 8396800 | tf_op jit(solution)/shard_map/gather | solution.py:87
  24.1 6.4 %dynamic_update_slice.15 = f32[128,16,512]{2,1,0:T(8,128)} dynamic-update-slice(f32[128,16,512]{2,1,0:T(8,128)} %bitcast.27, f32[128,1,512]{2,1,0:T(1,128)S(1)} %broadcast_in_dim.18, s32[]{:T(128)} %constant.90.clone.1, s32[]{:T(128)} %constant.101.clone.1, s32[]{:T(128)} %constant.90.clone.1) | dynamic-update-slice | bytes 524292 | tf_op jit(solution)/shard_map/dynamic_update_slice | solution.py:88
  30.4 12.0 %all-to-all-start = ((f32[128,16,512]{2,1,0:T(8,128)}), f32[128,16,512]{2,1,0:T(8,128)}, u32[]{:S(2)}, u32[]{:S(2)}) async-start(f32[128,16,512]{2,1,0:T(8,128)} %dynamic_update_slice.15), calls=%async_computation | async-start | bytes 8388608 | tf_op jit(solution)/shard_map/all_to_all | solution.py:89
  42.7 52.3 %all-to-all-done = f32[128,16,512]{2,1,0:T(8,128)} async-done(((f32[128,16,512]{2,1,0:T(8,128)}), f32[128,16,512]{2,1,0:T(8,128)}, u32[]{:S(2)}, u32[]{:S(2)}) %all-to-all-start) | async-done | bytes 4194336 | tf_op jit(solution)/shard_map/all_to_all | solution.py:89
  95.1 1.9 slice.100
  98.9 5.1 %sort.45 = (s32[1536]{0:T(1024)}, s32[1536]{0:T(1024)S(1)}, s32[1536]{0:T(1024)}) sort(s32[1536]{0:T(1024)S(1)} %convert_element_type.22, s32[1536]{0:T(1024)S(1)} %fusion.20, s32[1536]{0:T(1024)S(1)} %iota.30), dimensions={0}, to_apply=%region_7.8 | sort | flops 16896 | bytes 36864 | tf_op jit(solution)/shard_map/sort | solution.py:109
  104.0 7.9 %gather_fusion.1 = f32[1536,512]{1,0:T(8,128)} fusion(f32[2048,512]{1,0:T(8,128)} %bitcast.5, s32[2048]{0:T(1024)S(1)} %pad_clamp_fusion), kind=kCustom, calls=%fused_computation.1 | custom fusion | bytes 6297600 | tf_op jit(solution)/shard_map/gather | solution.py:110
  111.9 2.9 %multiply_convert_fusion = bf16[6,8,32,512]{3,2,1,0:T(8,128)(2,1)S(1)} fusion(f32[6,8,32,512]{3,2,1,0:T(8,128)} %bitcast.25, f32[512]{0:T(512)S(1)} %copy-done.3, f32[512]{0:T(512)S(1)} %copy-done.4, f32[6,512]{1,0:T(8,128)S(1)} %mul.122, f32[6,512]{1,0:T(8,128)S(1)} %sub.49), kind=kLoop, calls=%fused_computation.15 | loop fusion | flops 7077888 | bytes 4747264 | tf_op jit(solution)/shard_map/convert_element_type | solution.py:123
  114.9 3.6 %collective-permute-start = (bf16[6,1,32,512]{3,2,1,0:T(8,128)(2,1)S(1)}, bf16[6,1,32,512]{3,2,1,0:T(8,128)(2,1)S(1)}, u32[]{:S(2)}, u32[]{:S(2)}) collective-permute-start(bf16[6,1,32,512]{3,2,1,0:T(8,128)(2,1)S(1)} %get-tuple-element.19), channel_id=1, source_target_pairs={{0,1},{1,2},{2,3},{4,5},{5,6},{6,7},{8,9},{9,10},{10,11},{12,13},{... | collective-permute-start | bytes 589832 | tf_op jit(solution)/shard_map/ppermute | solution.py:29
  118.5 1.9 collective-permute-start.1
  121.7 5.3 %collective-permute-done.1 = bf16[6,1,32,512]{3,2,1,0:T(8,128)(2,1)S(1)} collective-permute-done((bf16[6,1,32,512]{3,2,1,0:T(8,128)(2,1)S(1)}, bf16[6,1,32,512]{3,2,1,0:T(8,128)(2,1)S(1)}, u32[]{:S(2)}, u32[]{:S(2)}) %collective-permute-start.1) | collective-permute-done | bytes 196640 | tf_op jit(solution)/shard_map/ppermute | solution.py:30
  127.2 1.5 collective-permute-start.2
  128.7 1.5 collective-permute-start.3
  130.4 1.3 fusion.48
  131.8 2.8 %collective-permute-done.3 = bf16[6,10,1,512]{3,2,1,0:T(2,128)(2,1)S(1)} collective-permute-done((bf16[6,10,1,512]{3,2,1,0:T(2,128)(2,1)S(1)}, bf16[6,10,1,512]{3,2,1,0:T(2,128)(2,1)S(1)}, u32[]{:S(2)}, u32[]{:S(2)}) %collective-permute-start.3) | collective-permute-done | bytes 61472 | tf_op jit(solution)/shard_map/ppermute | solution.py:129
  134.8 0.7 copy.22
  135.5 2.9 %collective-permute-start.4 = (bf16[2,10,34,512]{3,0,2,1:T(2,128)(2,1)S(1)}, bf16[2,10,34,512]{3,0,2,1:T(2,128)(2,1)S(1)}, u32[]{:S(2)}, u32[]{:S(2)}) collective-permute-start(bf16[2,10,34,512]{3,0,2,1:T(2,128)(2,1)S(1)} %copy.22), channel_id=1, source_target_pairs={{0,4},{4,8},{8,12},{12,16},{16,20},{20,24},{24,28},{1,5},{5,9},{9,... | collective-permute-start | bytes 2088968 | tf_op jit(solution)/shard_map/ppermute | solution.py:19
  138.4 3.3 %fusion.2 = bf16[6,10,32,1536]{3,2,1,0:T(8,128)(2,1)} fusion(bf16[6,10,31,512]{3,2,1,0:T(8,128)(2,1)S(1)} %get-tuple-element.16, bf16[6,10,31,512]{3,2,1,0:T(8,128)(2,1)S(1)} %get-tuple-element.15, bf16[6,1,32,512]{3,2,1,0:T(8,128)(2,1)S(1)} %collective-permute-done.1, bf16[6,8,32,512]{3,2,1,0:T(8,128)(2,1)S(1)} %multiply_convert_fusion, ...), kind=kLoop, calls=%fused_computation.9 | loop fusion | flops 41287680 | bytes 11673600 | tf_op jit(solution)/shard_map/concatenate | solution.py:153
  141.7 5.6 %dynamic_update_slice.18 = bf16[6,10,32,1536]{3,2,1,0:T(8,128)(2,1)} dynamic-update-slice(bf16[6,10,32,1536]{3,2,1,0:T(8,128)(2,1)} %fusion.2, bf16[6,10,1,512]{3,2,1,0:T(2,128)(2,1)S(1)} %collective-permute-done.2, s32[]{:T(128)} %constant.90.clone.1, s32[]{:T(128)} %constant.90.clone.1, s32[]{:T(128)} %constant.90.clone.1, s32[]{:T(128)} %constant.90.clone.1) | dynamic-update-slice | bytes 122884 | tf_op jit(solution)/shard_map/dynamic_update_slice | solution.py:155
  147.3 5.0 %dynamic_update_slice.19.x_ref = bf16[6,10,32,1536]{3,2,1,0:T(8,128)(2,1)} dynamic-update-slice(bf16[6,10,32,1536]{3,2,1,0:T(8,128)(2,1)} %dynamic_update_slice.18, bf16[6,10,1,512]{3,2,1,0:T(2,128)(2,1)} %copy-done.2, s32[]{:T(128)} %constant.90.clone.1, s32[]{:T(128)} %constant.90.clone.1, s32[]{:T(128)} %constant.106.clone.1, s32[]{:T(128)} %constant.107.clone.1) | dynamic-update-slice | bytes 122884 | tf_op jit(solution)/shard_map/dynamic_update_slice | solution.py:156
  152.2 31.7 %shard_map.73.part_ref = f32[6,256,512]{2,1,0:T(8,128)} custom-call(s32[18]{0:T(128)} %select_n.68.valid_ref, bf16[6,10,32,1536]{3,2,1,0:T(8,128)(2,1)} %dynamic_update_slice.19.x_ref, bf16[9,1536,512]{2,1,0:T(8,128)(2,1)} %bitcast.23), custom_call_target="tpu_custom_call" | custom-call | tf_op jit(solution)/shard_map/pallas_call | solution.py:179
  185.9 0.8 dynamic_update_slice.16
  186.7 0.7 dynamic_update_slice.17.x_ref
  187.4 1.3 copy-done.1
  188.7 9.7 %shard_map.74 = bf16[6,8,32,512]{3,2,1,0:T(8,128)(2,1)} custom-call(s32[4]{0:T(128)} %reshape.121.valid_ref, bf16[2,10,32,1536]{3,2,1,0:T(8,128)(2,1)} %copy-done.1, bf16[9,1536,512]{2,1,0:T(8,128)(2,1)} %bitcast.24, f32[6,256,512]{2,1,0:T(8,128)} %shard_map.73.part_ref, f32[6,8,32,512]{3,2,1,0:T(8,128)} %bitcast.26, f32[1,512]{1,0:T(1,128)} %bitcast.36), custom_call_target="tpu_custom_call" | custom-call | tf_op jit(solution)/shard_map/pallas_call | solution.py:223
  (84 shorter events, 7.6 us)
Async XLA Ops:
  1.9 5.2 %copy-start = (f32[1536,512]{1,0:T(8,128)S(1)}, f32[1536,512]{1,0:T(8,128)}, u32[]{:S(2)}) copy-start(f32[1536,512]{1,0:T(8,128)} %param.7) | copy-start | bytes 9437188
  30.4 12.0 %copy-start.5 = (s32[48]{0:T(128)S(1)}, s32[48]{0:T(128)}, u32[]{:S(2)}) copy-start(s32[48]{0:T(128)} %param.9) | copy-start | bytes 580
  30.4 64.6 %all-to-all-start = ((f32[128,16,512]{2,1,0:T(8,128)}), f32[128,16,512]{2,1,0:T(8,128)}, u32[]{:S(2)}, u32[]{:S(2)}) async-start(f32[128,16,512]{2,1,0:T(8,128)} %dynamic_update_slice.15), calls=%async_computation | async-start | bytes 8388608 | tf_op jit(solution)/shard_map/all_to_all | solution.py:89
  104.0 8.0 %copy-start.3 = (f32[512]{0:T(512)S(1)}, f32[512]{0:T(512)}, u32[]{:S(2)}) copy-start(f32[512]{0:T(512)} %param.11) | copy-start | bytes 6148
  104.0 7.9 %copy-start.4 = (f32[512]{0:T(512)S(1)}, f32[512]{0:T(512)}, u32[]{:S(2)}) copy-start(f32[512]{0:T(512)} %param.10) | copy-start | bytes 6148
  114.9 6.9 %collective-permute-start = (bf16[6,1,32,512]{3,2,1,0:T(8,128)(2,1)S(1)}, bf16[6,1,32,512]{3,2,1,0:T(8,128)(2,1)S(1)}, u32[]{:S(2)}, u32[]{:S(2)}) collective-permute-start(bf16[6,1,32,512]{3,2,1,0:T(8,128)(2,1)S(1)} %get-tuple-element.19), channel_id=1, source_target_pairs={{0,1},{1,2},{2,3},{4,5},{5,6},{6,7},{8,9},{9,10},{10,11},{12,13},{... | collective-permute-start | bytes 589832 | tf_op jit(solution)/shard_map/ppermute | solution.py:29
  118.5 8.5 %collective-permute-start.1 = (bf16[6,1,32,512]{3,2,1,0:T(8,128)(2,1)S(1)}, bf16[6,1,32,512]{3,2,1,0:T(8,128)(2,1)S(1)}, u32[]{:S(2)}, u32[]{:S(2)}) collective-permute-start(bf16[6,1,32,512]{3,2,1,0:T(8,128)(2,1)S(1)} %get-tuple-element.20), channel_id=1, source_target_pairs={{1,0},{2,1},{3,2},{5,4},{6,5},{7,6},{9,8},{10,9},{11,10},{13,12},{... | collective-permute-start | bytes 589832 | tf_op jit(solution)/shard_map/ppermute | solution.py:30
  127.2 4.5 %collective-permute-start.2 = (bf16[6,10,1,512]{3,2,1,0:T(2,128)(2,1)S(1)}, bf16[6,10,1,512]{3,2,1,0:T(2,128)(2,1)S(1)}, u32[]{:S(2)}, u32[]{:S(2)}) collective-permute-start(bf16[6,10,1,512]{3,2,1,0:T(2,128)(2,1)S(1)} %get-tuple-element.17), channel_id=1, source_target_pairs={{0,32},{32,64},{64,96},{1,33},{33,65},{65,97},{2,34},{34,66},{66,9... | collective-permute-start | bytes 184328 | tf_op jit(solution)/shard_map/ppermute | solution.py:128
  128.7 6.0 %collective-permute-start.3 = (bf16[6,10,1,512]{3,2,1,0:T(2,128)(2,1)S(1)}, bf16[6,10,1,512]{3,2,1,0:T(2,128)(2,1)S(1)}, u32[]{:S(2)}, u32[]{:S(2)}) collective-permute-start(bf16[6,10,1,512]{3,2,1,0:T(2,128)(2,1)S(1)} %get-tuple-element.18), channel_id=1, source_target_pairs={{32,0},{64,32},{96,64},{33,1},{65,33},{97,65},{34,2},{66,34},{98,6... | collective-permute-start | bytes 184328 | tf_op jit(solution)/shard_map/ppermute | solution.py:129
  134.7 3.8 %copy-start.2 = (bf16[6,10,1,512]{3,2,1,0:T(2,128)(2,1)}, bf16[6,10,1,512]{3,2,1,0:T(2,128)(2,1)S(1)}, u32[]{:S(2)}) copy-start(bf16[6,10,1,512]{3,2,1,0:T(2,128)(2,1)S(1)} %collective-permute-done.3) | copy-start | bytes 184324
  135.5 48.4 %collective-permute-start.4 = (bf16[2,10,34,512]{3,0,2,1:T(2,128)(2,1)S(1)}, bf16[2,10,34,512]{3,0,2,1:T(2,128)(2,1)S(1)}, u32[]{:S(2)}, u32[]{:S(2)}) collective-permute-start(bf16[2,10,34,512]{3,0,2,1:T(2,128)(2,1)S(1)} %copy.22), channel_id=1, source_target_pairs={{0,4},{4,8},{8,12},{12,16},{16,20},{20,24},{24,28},{1,5},{5,9},{9,... | collective-permute-start | bytes 2088968 | tf_op jit(solution)/shard_map/ppermute | solution.py:19
  187.4 1.3 copy-start.1

commit v3 on v2

--- a/solution.py
+++ b/solution.py
@@ -121,18 +121,17 @@
     frame_inv = jnp.dot(onehot, inverse_std, precision=HIGH)
     normed = (centred * frame_inv[:, None, :, None]).reshape(FR_DEV, HR, WCOL, channels)
     activated = jax.nn.silu(normed * norm_gain + norm_bias).astype(jnp.bfloat16)
-    zero_col = jnp.zeros((FR_DEV, HR + 2, 1, channels), jnp.bfloat16)
     high_padded = with_halo(activated, (("tile", 1),), 1)
     n_wide = lax.axis_size("src")
     up = [(i, i + 1) for i in range(n_wide - 1)]
     left = lax.ppermute(high_padded[:, :, WCOL - 1 :], "src", up)
     right = lax.ppermute(high_padded[:, :, :1], "src", [(j, i) for i, j in up])
-    own_wide = widen(high_padded, zero_col, left, right)
+    own_wide = widen(high_padded, left, right)
     sent_prev = jnp.concatenate(
         [high_padded[FR_DEV - 2 :], left[FR_DEV - 2 :], right[FR_DEV - 2 :]], axis=2
     )
     prev = passed_along(sent_prev, "frame", 1)
-    prev_wide = widen(prev[:, :, :WCOL], zero_col[:2], prev[:, :, WCOL : WCOL + 1], prev[:, :, WCOL + 1 :])
+    prev_wide = widen(prev[:, :, :WCOL], prev[:, :, WCOL : WCOL + 1], prev[:, :, WCOL + 1 :])
 
     validity = jnp.stack(
         [(window_ids[a : a + FR_DEV] == own_ids).astype(jnp.int32) for a in range(3)]
@@ -141,27 +140,25 @@
     own_valid = jnp.where(reach >= 2, validity, 0).reshape(-1)
     prev_valid = jnp.where(reach < 2, validity, 0)[:2, :2].reshape(-1)
     weights = conv_weight.reshape(9, 3 * channels, channels)
-    partial_sum = own_conv(own_valid, own_wide, weights)
-    return prev_conv(
-        prev_valid, prev_wide, weights, partial_sum, features, conv_bias.reshape(1, channels)
-    )
-
-
-def widen(block, zero_col, left, right):
-    shifted_in = jnp.concatenate([zero_col, block[:, :, : WCOL - 1]], axis=2)
-    shifted_out = jnp.concatenate([block[:, :, 1:], zero_col], axis=2)
-    wide = jnp.concatenate([shifted_in, block, shifted_out], axis=-1)
-    channels = block.shape[-1]
-    wide = lax.dynamic_update_slice(wide, left, (0, 0, 0, 0))
-    return lax.dynamic_update_slice(wide, right, (0, 0, WCOL - 1, 2 * channels))
-
-
-def own_kernel(valid_ref, x_ref, w_ref, acc_ref):
+    bias = conv_bias.reshape(1, channels)
+    decoded, early = own_conv(own_valid, own_wide, weights, features, bias)
+    return prev_conv(prev_valid, prev_wide, weights, early, decoded)
+
+
+def widen(block, left, right):
+    shifted_in = jnp.concatenate([left, block[:, :, : WCOL - 1]], axis=2)
+    shifted_out = jnp.concatenate([block[:, :, 1:], right], axis=2)
+    return jnp.concatenate([shifted_in, block, shifted_out], axis=-1)
+
+
+def own_kernel(valid_ref, x_ref, w_ref, b_ref, f_hbm, o_ref, early_ref, f_ref, acc_ref, sem):
     tap_time = pl.program_id(0)
     tap_high = pl.program_id(1)
+    fetch = pltpu.make_async_copy(f_hbm, f_ref, sem)
 
     @pl.when((tap_time == 0) & (tap_high == 0))
     def _():
+        fetch.start()
         acc_ref[...] = jnp.zeros_like(acc_ref)
 
     for t in range(FR_DEV):
@@ -172,10 +169,18 @@
             lhs = x_ref[frame, pl.ds(tap_high, HR)].reshape(HR * WCOL, -1)
             acc_ref[t] += jnp.dot(lhs, w_ref[0], preferred_element_type=jnp.float32)
 
-
-def own_conv(validity, wide, weights):
-    frames = wide.shape[0]
-    channels = weights.shape[-1]
+    @pl.when((tap_time == 2) & (tap_high == 2))
+    def _():
+        fetch.wait()
+        for t in range(FR_DEV):
+            total = (f_ref[t] + acc_ref[t].reshape(HR, WCOL, -1)) + b_ref[...]
+            if t < 2:
+                early_ref[t] = total
+            else:
+                o_ref[t] = total.astype(o_ref.dtype)
+
+
+def own_conv(validity, wide, weights, features, bias):
     return pl.pallas_call(
         own_kernel,
         grid_spec=pltpu.PrefetchScalarGridSpec(
@@ -184,23 +189,37 @@
             in_specs=[
                 pl.BlockSpec(wide.shape, lambda a, b, v: (0, 0, 0, 0), pipeline_mode=pl.Buffered(1)),
                 pl.BlockSpec((1,) + weights.shape[1:], lambda a, b, v: (a * 3 + b, 0, 0)),
-            ],
-            out_specs=pl.BlockSpec((frames, HR * WCOL, channels), lambda a, b, v: (0, 0, 0)),
-        ),
-        out_shape=jax.ShapeDtypeStruct((frames, HR * WCOL, channels), jnp.float32),
+                pl.BlockSpec(bias.shape, lambda a, b, v: (0, 0), pipeline_mode=pl.Buffered(1)),
+                pl.BlockSpec(memory_space=pl.ANY),
+            ],
+            out_specs=[
+                pl.BlockSpec(features.shape, lambda a, b, v: (0, 0, 0, 0)),
+                pl.BlockSpec((2,) + features.shape[1:], lambda a, b, v: (0, 0, 0, 0)),
+            ],
+            scratch_shapes=[
+                pltpu.VMEM(features.shape, jnp.float32),
+                pltpu.VMEM((features.shape[0], HR * WCOL, features.shape[-1]), jnp.float32),
+                pltpu.SemaphoreType.DMA(()),
+            ],
+        ),
+        out_shape=[
+            jax.ShapeDtypeStruct(features.shape, jnp.bfloat16),
+            jax.ShapeDtypeStruct((2,) + features.shape[1:], jnp.float32),
+        ],
         compiler_params=pltpu.CompilerParams(
             dimension_semantics=("arbitrary", "arbitrary"), vmem_limit_bytes=60 * 1024 * 1024
         ),
-    )(validity, wide, weights)
-
-
-def prev_kernel(valid_ref, x_ref, w_ref, part_ref, f_ref, b_ref, o_ref, acc_ref):
+    )(validity, wide, weights, bias, features)
+
+
+def prev_kernel(valid_ref, x_ref, w_ref, early_ref, whole_ref, o_ref, acc_ref):
+    del whole_ref
     tap_time = pl.program_id(0)
     tap_high = pl.program_id(1)
 
     @pl.when((tap_time == 0) & (tap_high == 0))
     def _():
-        acc_ref[...] = part_ref[...]
+        acc_ref[...] = jnp.zeros_like(acc_ref)
 
     for t in range(2):
 
@@ -212,34 +231,32 @@
 
     @pl.when((tap_time == 1) & (tap_high == 2))
     def _():
-        conv_sum = acc_ref[...].reshape(o_ref.shape)
-        o_ref[...] = ((f_ref[...] + conv_sum) + b_ref[...]).astype(o_ref.dtype)
-
-
-def prev_conv(validity, wide, weights, partial_sum, features, bias):
-    whole = lambda shape: pl.BlockSpec(
-        shape, lambda a, b, v: (0,) * len(shape), pipeline_mode=pl.Buffered(1)
-    )
+        for t in range(2):
+            total = early_ref[t] + acc_ref[t].reshape(HR, WCOL, -1)
+            o_ref[t] = total.astype(o_ref.dtype)
+
+
+def prev_conv(validity, wide, weights, early, decoded):
     return pl.pallas_call(
         prev_kernel,
         grid_spec=pltpu.PrefetchScalarGridSpec(
             num_scalar_prefetch=1,
             grid=(2, 3),
             in_specs=[
-                whole(wide.shape),
+                pl.BlockSpec(wide.shape, lambda a, b, v: (0, 0, 0, 0), pipeline_mode=pl.Buffered(1)),
                 pl.BlockSpec((1,) + weights.shape[1:], lambda a, b, v: (a * 3 + b, 0, 0)),
-                whole(partial_sum.shape),
-                whole(features.shape),
-                whole(bias.shape),
-            ],
-            out_specs=pl.BlockSpec(features.shape, lambda a, b, v: (0, 0, 0, 0)),
-            scratch_shapes=[pltpu.VMEM(partial_sum.shape, jnp.float32)],
-        ),
-        out_shape=jax.ShapeDtypeStruct(features.shape, jnp.bfloat16),
+                pl.BlockSpec(early.shape, lambda a, b, v: (0, 0, 0, 0), pipeline_mode=pl.Buffered(1)),
+                pl.BlockSpec(memory_space=pl.ANY),
+            ],
+            out_specs=pl.BlockSpec(early.shape, lambda a, b, v: (0, 0, 0, 0)),
+            scratch_shapes=[pltpu.VMEM((2, HR * WCOL, early.shape[-1]), jnp.float32)],
+        ),
+        out_shape=jax.ShapeDtypeStruct(decoded.shape, decoded.dtype),
+        input_output_aliases={4: 0},
         compiler_params=pltpu.CompilerParams(
             dimension_semantics=("arbitrary", "arbitrary"), vmem_limit_bytes=60 * 1024 * 1024
         ),
-    )(validity, wide, weights, partial_sum, features, bias)
+    )(validity, wide, weights, early, decoded)
 
 
 def solution(mesh):

time: 200 us -> 187 us (0.935)
  local copies, waits for them, and re-layouts: 45.7 us -> 32.4 us
  Pallas kernels: 41.4 us -> 39.4 us
    dynamic_update_slice x4 -> x0, local copies, waits for them, and re-layouts: 12 us -> none  [the longest x2 6.35 us: widen(): wide = lax.dynamic_update_slice(wide, left, (0, 0, 0, 0))]
    pallas_call x1, Pallas kernels: 9.65 us -> 7.43 us  [prev_conv(): pl.pallas_call(prev_kernel, grid_spec=pltpu.PrefetchScalarGridSpec(num_sc...]
  transfers between devices with their start and end apart: 6 -> 6, of which waited for: 3 -> 3; matrix products, arithmetic and copies ran while one was open for 9% -> 4% of each run, Pallas kernels for 16% -> 17%
where the time goes in v3:
time: 187 us; the launch traced here: 185 us
  waiting for transfers between devices  60.5 us (32%)
  Pallas kernels  39.4 us (21%)
  local copies, waits for them, and re-layouts  32.4 us (17%)
  other arithmetic  27.4 us (15%)
  starting transfers between devices  23.3 us (12%)
    all_to_all x1, waiting for transfers between devices, shards(): lax.all_to_all(payload, ('src', 'frame', 'tile'), split_axis=0, concat_ax...  52.3 us
    pallas_call x1, Pallas kernels, own_conv(): pl.pallas_call(own_kernel, grid_spec=pltpu.PrefetchScalarGridSpec(num_sca...  32 us
    all_to_all x1, starting transfers between devices, shards(): lax.all_to_all(payload, ('src', 'frame', 'tile'), split_axis=0, concat_ax...  12 us
    gather x1, local copies, waits for them, and re-layouts, shards(): payload = feats[pick.reshape(-1)].reshape(devices, block, channels)  8.92 us
    gather x1, local copies, waits for them, and re-layouts, shards(): arrived.reshape(-1, channels)[gather_rows]  7.93 us
    pallas_call x1, Pallas kernels, prev_conv(): pl.pallas_call(prev_kernel, grid_spec=pltpu.PrefetchScalarGridSpec(num_sc...  7.43 us
    dynamic_update_slice x1, local copies, waits for them, and re-layouts, shards(): lax.dynamic_update_slice(payload, info[:, None, :], (0, per_pair, 0))  6.35 us
    concatenate x2, other arithmetic, widen(): return jnp.concatenate([shifted_in, block, shifted_out], axis=-1)  5.53 us
  transfers between devices with their start and end apart: 6, of which 3 were waited for; matrix products, arithmetic and copies ran while one was open for 4% of the time, Pallas kernels for 17%

profile of v3, /device:TPU:1, one launch (start us, length us, event | category | flops | bytes accessed | tf_op | source)
XLA Modules:
  0.0 185.0 jit_solution(14313794976720511094)
XLA Ops:
  0.0 0.7 fusion.16
  0.7 1.2 fusion.45
  1.9 3.3 %multiply_reduce_fusion.2 = f32[4,512]{1,0:T(4,128)S(1)} fusion(f32[4,1536]{1,0:T(4,128)S(1)} %bitcast.32, f32[1536,512]{1,0:T(8,128)} %param.7), kind=kLoop, calls=%fused_computation.4 | loop fusion | flops 6289408 | bytes 3178496 | tf_op jit(solution)/shard_map/reduce_sum | solution.py:60
  5.8 1.3 multiply_reduce_fusion.1
  7.1 0.8 subtract_multiply_fusion
  7.9 1.1 multiply_reduce_fusion
  9.3 5.1 %sort.44 = (s32[1536]{0:T(1024)}, s32[1536]{0:T(1024)S(1)}, s32[1536]{0:T(1024)S(1)}) sort(s32[1536]{0:T(1024)S(1)} %get-tuple-element.33, s32[1536]{0:T(1024)S(1)} %get-tuple-element.34, s32[1536]{0:T(1024)S(1)} %iota.28), dimensions={0}, to_apply=%region_0.1 | sort | flops 16896 | bytes 36864 | tf_op jit(solution)/shard_map/sort | solution.py:73
  15.2 8.9 %gather_fusion = f32[2048,512]{1,0:T(8,128)} fusion(f32[1536,512]{1,0:T(8,128)S(1)} %copy-done, s32[2048]{0:T(1024)S(1)} %broadcast_clamp_fusion), kind=kCustom, calls=%fused_computation | custom fusion | bytes 8396800 | tf_op jit(solution)/shard_map/gather | solution.py:87
  24.1 6.4 %dynamic_update_slice.3 = f32[128,16,512]{2,1,0:T(8,128)} dynamic-update-slice(f32[128,16,512]{2,1,0:T(8,128)} %bitcast.27, f32[128,1,512]{2,1,0:T(1,128)S(1)} %broadcast_in_dim.18, s32[]{:T(128)} %constant.86.clone.1, s32[]{:T(128)} %constant.97.clone.1, s32[]{:T(128)} %constant.86.clone.1) | dynamic-update-slice | bytes 524292 | tf_op jit(solution)/shard_map/dynamic_update_slice | solution.py:88
  30.4 12.0 %all-to-all-start = ((f32[128,16,512]{2,1,0:T(8,128)}), f32[128,16,512]{2,1,0:T(8,128)}, u32[]{:S(2)}, u32[]{:S(2)}) async-start(f32[128,16,512]{2,1,0:T(8,128)} %dynamic_update_slice.3), calls=%async_computation | async-start | bytes 8388608 | tf_op jit(solution)/shard_map/all_to_all | solution.py:89
  42.7 52.3 %all-to-all-done = f32[128,16,512]{2,1,0:T(8,128)} async-done(((f32[128,16,512]{2,1,0:T(8,128)}), f32[128,16,512]{2,1,0:T(8,128)}, u32[]{:S(2)}, u32[]{:S(2)}) %all-to-all-start) | async-done | bytes 4194336 | tf_op jit(solution)/shard_map/all_to_all | solution.py:89
  95.1 1.9 %slice.99 = f32[128,1,512]{2,1,0:T(1,128)S(1)} slice(f32[128,16,512]{2,1,0:T(8,128)} %all-to-all-done), slice={[0:128], [12:13], [0:512]} | slice | bytes 524288 | tf_op jit(solution)/shard_map/slice | solution.py:93
  98.9 5.1 %sort.45 = (s32[1536]{0:T(1024)}, s32[1536]{0:T(1024)S(1)}, s32[1536]{0:T(1024)}) sort(s32[1536]{0:T(1024)S(1)} %convert_element_type.22, s32[1536]{0:T(1024)S(1)} %fusion.12, s32[1536]{0:T(1024)S(1)} %iota.30), dimensions={0}, to_apply=%region_7.8 | sort | flops 16896 | bytes 36864 | tf_op jit(solution)/shard_map/sort | solution.py:109
  104.0 7.9 %gather_fusion.1 = f32[1536,512]{1,0:T(8,128)} fusion(f32[2048,512]{1,0:T(8,128)} %bitcast.5, s32[2048]{0:T(1024)S(1)} %pad_clamp_fusion), kind=kCustom, calls=%fused_computation.1 | custom fusion | bytes 6297600 | tf_op jit(solution)/shard_map/gather | solution.py:110
  111.9 2.9 %multiply_convert_fusion = bf16[6,8,32,512]{3,2,1,0:T(8,128)(2,1)S(1)} fusion(f32[6,8,32,512]{3,2,1,0:T(8,128)} %bitcast.25, f32[512]{0:T(512)S(1)} %copy-done.1, f32[512]{0:T(512)S(1)} %copy-done.2, f32[6,512]{1,0:T(8,128)S(1)} %mul.122, f32[6,512]{1,0:T(8,128)S(1)} %sub.49), kind=kLoop, calls=%fused_computation.6 | loop fusion | flops 7077888 | bytes 4747264 | tf_op jit(solution)/shard_map/convert_element_type | solution.py:123
  114.9 3.6 %collective-permute-start = (bf16[6,1,32,512]{3,2,1,0:T(8,128)(2,1)S(1)}, bf16[6,1,32,512]{3,2,1,0:T(8,128)(2,1)S(1)}, u32[]{:S(2)}, u32[]{:S(2)}) collective-permute-start(bf16[6,1,32,512]{3,2,1,0:T(8,128)(2,1)S(1)} %get-tuple-element.23), channel_id=1, source_target_pairs={{0,1},{1,2},{2,3},{4,5},{5,6},{6,7},{8,9},{9,10},{10,11},{12,13},{... | collective-permute-start | bytes 589832 | tf_op jit(solution)/shard_map/ppermute | solution.py:29
  118.5 1.9 %collective-permute-start.1 = (bf16[6,1,32,512]{3,2,1,0:T(8,128)(2,1)S(1)}, bf16[6,1,32,512]{3,2,1,0:T(8,128)(2,1)S(1)}, u32[]{:S(2)}, u32[]{:S(2)}) collective-permute-start(bf16[6,1,32,512]{3,2,1,0:T(8,128)(2,1)S(1)} %get-tuple-element.24), channel_id=1, source_target_pairs={{1,0},{2,1},{3,2},{5,4},{6,5},{7,6},{9,8},{10,9},{11,10},{13,12},{... | collective-permute-start | bytes 589832 | tf_op jit(solution)/shard_map/ppermute | solution.py:30
  120.5 0.6 select_n.68.valid_ref
  121.1 0.6 reshape.121.valid_ref
  121.7 5.3 %collective-permute-done.1 = bf16[6,1,32,512]{3,2,1,0:T(8,128)(2,1)S(1)} collective-permute-done((bf16[6,1,32,512]{3,2,1,0:T(8,128)(2,1)S(1)}, bf16[6,1,32,512]{3,2,1,0:T(8,128)(2,1)S(1)}, u32[]{:S(2)}, u32[]{:S(2)}) %collective-permute-start.1) | collective-permute-done | bytes 196640 | tf_op jit(solution)/shard_map/ppermute | solution.py:30
  127.2 1.5 collective-permute-start.2
  128.7 1.5 collective-permute-start.3
  130.4 1.3 fusion.40
  131.8 2.8 %collective-permute-done.3 = bf16[6,10,1,512]{3,2,1,0:T(2,128)(2,1)S(1)} collective-permute-done((bf16[6,10,1,512]{3,2,1,0:T(2,128)(2,1)S(1)}, bf16[6,10,1,512]{3,2,1,0:T(2,128)(2,1)S(1)}, u32[]{:S(2)}, u32[]{:S(2)}) %collective-permute-start.3) | collective-permute-done | bytes 61472 | tf_op jit(solution)/shard_map/ppermute | solution.py:128
  134.8 0.7 copy.23
  135.5 2.9 %collective-permute-start.4 = (bf16[2,10,34,512]{3,0,2,1:T(2,128)(2,1)S(1)}, bf16[2,10,34,512]{3,0,2,1:T(2,128)(2,1)S(1)}, u32[]{:S(2)}, u32[]{:S(2)}) collective-permute-start(bf16[2,10,34,512]{3,0,2,1:T(2,128)(2,1)S(1)} %copy.23), channel_id=1, source_target_pairs={{0,4},{4,8},{8,12},{12,16},{16,20},{20,24},{24,28},{1,5},{5,9},{9,... | collective-permute-start | bytes 2088968 | tf_op jit(solution)/shard_map/ppermute | solution.py:19
  138.4 3.8 %maximum_maximum_fusion.x_ref = bf16[6,10,32,1536]{3,2,1,0:T(8,128)(2,1)} fusion(bf16[6,10,1,512]{3,2,1,0:T(2,128)(2,1)S(1)} %collective-permute-done.3, bf16[6,10,31,512]{3,2,1,0:T(8,128)(2,1)S(1)} %get-tuple-element.20, bf16[6,1,32,512]{3,2,1,0:T(8,128)(2,1)S(1)} %collective-permute-done.1, bf16[6,8,32,512]{3,2,1,0:T(8,128)(2,1)S(1)} %multiply_convert_fusion, ...), kind=kLoop, calls=%fused_computation.5 | loop fusion | flops 41287680 | bytes 11796480 | tf_op jit(solution)/shard_map/concatenate | solution.py:151
  142.3 32.0 %shard_map.73 = (bf16[6,8,32,512]{3,2,1,0:T(8,128)(2,1)}, f32[2,8,32,512]{3,2,1,0:T(8,128)}) custom-call(s32[18]{0:T(128)} %select_n.68.valid_ref, bf16[6,10,32,1536]{3,2,1,0:T(8,128)(2,1)} %maximum_maximum_fusion.x_ref, bf16[9,1536,512]{2,1,0:T(8,128)(2,1)} %bitcast.23, f32[1,512]{1,0:T(1,128)} %bitcast.36, f32[6,8,32,512]{3,2,1,0:T(8,128)} %bitcast.26), custom_call_target="tpu_custom_call" | custom-call | tf_op jit(solution)/shard_map/pallas_call | solution.py:184
  174.3 0.7 fusion.43
  175.2 0.5 slice.111
  175.9 1.7 maximum_maximum_fusion.1.x_ref
  177.6 7.4 %shard_map.74 = bf16[6,8,32,512]{3,2,1,0:T(8,128)(2,1)} custom-call(s32[4]{0:T(128)} %reshape.121.valid_ref, bf16[2,10,32,1536]{3,2,1,0:T(8,128)(2,1)} %maximum_maximum_fusion.1.x_ref, bf16[9,1536,512]{2,1,0:T(8,128)(2,1)} %bitcast.24, f32[2,8,32,512]{3,2,1,0:T(8,128)} %get-tuple-element.15.early_ref, ...), custom_call_target="tpu_custom_call", output_to_operand_aliasing={{}: (4, {})} | custom-call | tf_op jit(solution)/shard_map/pallas_call | solution.py:240
  (76 shorter events, 4.9 us)
Async XLA Ops:
  1.9 5.2 %copy-start = (f32[1536,512]{1,0:T(8,128)S(1)}, f32[1536,512]{1,0:T(8,128)}, u32[]{:S(2)}) copy-start(f32[1536,512]{1,0:T(8,128)} %param.7) | copy-start | bytes 9437188
  30.4 12.0 %copy-start.3 = (s32[48]{0:T(128)S(1)}, s32[48]{0:T(128)}, u32[]{:S(2)}) copy-start(s32[48]{0:T(128)} %param.9) | copy-start | bytes 580
  30.4 64.6 %all-to-all-start = ((f32[128,16,512]{2,1,0:T(8,128)}), f32[128,16,512]{2,1,0:T(8,128)}, u32[]{:S(2)}, u32[]{:S(2)}) async-start(f32[128,16,512]{2,1,0:T(8,128)} %dynamic_update_slice.3), calls=%async_computation | async-start | bytes 8388608 | tf_op jit(solution)/shard_map/all_to_all | solution.py:89
  104.0 8.0 %copy-start.1 = (f32[512]{0:T(512)S(1)}, f32[512]{0:T(512)}, u32[]{:S(2)}) copy-start(f32[512]{0:T(512)} %param.11) | copy-start | bytes 6148
  104.0 7.9 %copy-start.2 = (f32[512]{0:T(512)S(1)}, f32[512]{0:T(512)}, u32[]{:S(2)}) copy-start(f32[512]{0:T(512)} %param.10) | copy-start | bytes 6148
  114.9 6.8 %collective-permute-start = (bf16[6,1,32,512]{3,2,1,0:T(8,128)(2,1)S(1)}, bf16[6,1,32,512]{3,2,1,0:T(8,128)(2,1)S(1)}, u32[]{:S(2)}, u32[]{:S(2)}) collective-permute-start(bf16[6,1,32,512]{3,2,1,0:T(8,128)(2,1)S(1)} %get-tuple-element.23), channel_id=1, source_target_pairs={{0,1},{1,2},{2,3},{4,5},{5,6},{6,7},{8,9},{9,10},{10,11},{12,13},{... | collective-permute-start | bytes 589832 | tf_op jit(solution)/shard_map/ppermute | solution.py:29
  118.5 8.5 %collective-permute-start.1 = (bf16[6,1,32,512]{3,2,1,0:T(8,128)(2,1)S(1)}, bf16[6,1,32,512]{3,2,1,0:T(8,128)(2,1)S(1)}, u32[]{:S(2)}, u32[]{:S(2)}) collective-permute-start(bf16[6,1,32,512]{3,2,1,0:T(8,128)(2,1)S(1)} %get-tuple-element.24), channel_id=1, source_target_pairs={{1,0},{2,1},{3,2},{5,4},{6,5},{7,6},{9,8},{10,9},{11,10},{13,12},{... | collective-permute-start | bytes 589832 | tf_op jit(solution)/shard_map/ppermute | solution.py:30
  127.2 4.5 %collective-permute-start.2 = (bf16[6,10,1,512]{3,2,1,0:T(2,128)(2,1)S(1)}, bf16[6,10,1,512]{3,2,1,0:T(2,128)(2,1)S(1)}, u32[]{:S(2)}, u32[]{:S(2)}) collective-permute-start(bf16[6,10,1,512]{3,2,1,0:T(2,128)(2,1)S(1)} %get-tuple-element.21), channel_id=1, source_target_pairs={{0,32},{32,64},{64,96},{1,33},{33,65},{65,97},{2,34},{34,66},{66,9... | collective-permute-start | bytes 184328 | tf_op jit(solution)/shard_map/ppermute | solution.py:127
  128.7 6.0 %collective-permute-start.3 = (bf16[6,10,1,512]{3,2,1,0:T(2,128)(2,1)S(1)}, bf16[6,10,1,512]{3,2,1,0:T(2,128)(2,1)S(1)}, u32[]{:S(2)}, u32[]{:S(2)}) collective-permute-start(bf16[6,10,1,512]{3,2,1,0:T(2,128)(2,1)S(1)} %get-tuple-element.22), channel_id=1, source_target_pairs={{32,0},{64,32},{96,64},{33,1},{65,33},{97,65},{34,2},{66,34},{98,6... | collective-permute-start | bytes 184328 | tf_op jit(solution)/shard_map/ppermute | solution.py:128
  135.5 38.7 %collective-permute-start.4 = (bf16[2,10,34,512]{3,0,2,1:T(2,128)(2,1)S(1)}, bf16[2,10,34,512]{3,0,2,1:T(2,128)(2,1)S(1)}, u32[]{:S(2)}, u32[]{:S(2)}) collective-permute-start(bf16[2,10,34,512]{3,0,2,1:T(2,128)(2,1)S(1)} %copy.23), channel_id=1, source_target_pairs={{0,4},{4,8},{8,12},{12,16},{16,20},{20,24},{24,28},{1,5},{5,9},{9,... | collective-permute-start | bytes 2088968 | tf_op jit(solution)/shard_map/ppermute | solution.py:19

commit v4 on v3

--- a/solution.py
+++ b/solution.py
@@ -161,13 +161,17 @@
         fetch.start()
         acc_ref[...] = jnp.zeros_like(acc_ref)
 
-    for t in range(FR_DEV):
-
-        @pl.when(valid_ref[tap_time * FR_DEV + t] != 0)
+    for a in range(3):
+
+        @pl.when(tap_time == a)
         def _():
-            frame = jnp.maximum(tap_time + t - 2, 0)
-            lhs = x_ref[frame, pl.ds(tap_high, HR)].reshape(HR * WCOL, -1)
-            acc_ref[t] += jnp.dot(lhs, w_ref[0], preferred_element_type=jnp.float32)
+            reach = FR_DEV - 2 + a
+            lhs = x_ref[:reach, pl.ds(tap_high, HR)].reshape(reach * HR * WCOL, -1)
+            part = jnp.dot(lhs, w_ref[0], preferred_element_type=jnp.float32)
+            for j in range(reach):
+                t = j + 2 - a
+                keep = valid_ref[a * FR_DEV + t].astype(jnp.float32)
+                acc_ref[t] += part[j * HR * WCOL : (j + 1) * HR * WCOL] * keep
 
     @pl.when((tap_time == 2) & (tap_high == 2))
     def _():

time: 187 us -> 181 us (0.968)
  Pallas kernels: 39.4 us -> 33.5 us
    pallas_call x1, Pallas kernels: 32 us -> 26.1 us  [own_conv(): pl.pallas_call(own_kernel, grid_spec=pltpu.PrefetchScalarGridSpec(num_sca...]
  transfers between devices with their start and end apart: 6 -> 6, of which waited for: 3 -> 3; matrix products, arithmetic and copies ran while one was open for 4% -> 4% of each run, Pallas kernels for 17% -> 15%
where the time goes in v4:
time: 181 us; the launch traced here: 179 us
  waiting for transfers between devices  60.5 us (33%)
  Pallas kernels  33.5 us (19%)
  local copies, waits for them, and re-layouts  32.4 us (18%)
  other arithmetic  27.4 us (15%)
  starting transfers between devices  23.3 us (13%)
    all_to_all x1, waiting for transfers between devices, shards(): lax.all_to_all(payload, ('src', 'frame', 'tile'), split_axis=0, concat_ax...  52.3 us
    pallas_call x1, Pallas kernels, own_conv(): pl.pallas_call(own_kernel, grid_spec=pltpu.PrefetchScalarGridSpec(num_sca...  26.1 us
    all_to_all x1, starting transfers between devices, shards(): lax.all_to_all(payload, ('src', 'frame', 'tile'), split_axis=0, concat_ax...  12 us
    gather x1, local copies, waits for them, and re-layouts, shards(): payload = feats[pick.reshape(-1)].reshape(devices, block, channels)  8.92 us
    gather x1, local copies, waits for them, and re-layouts, shards(): arrived.reshape(-1, channels)[gather_rows]  7.93 us
    pallas_call x1, Pallas kernels, prev_conv(): pl.pallas_call(prev_kernel, grid_spec=pltpu.PrefetchScalarGridSpec(num_sc...  7.43 us
    dynamic_update_slice x1, local copies, waits for them, and re-layouts, shards(): lax.dynamic_update_slice(payload, info[:, None, :], (0, per_pair, 0))  6.35 us
    concatenate x2, other arithmetic, widen(): return jnp.concatenate([shifted_in, block, shifted_out], axis=-1)  5.53 us
  transfers between devices with their start and end apart: 6, of which 3 were waited for; matrix products, arithmetic and copies ran while one was open for 4% of the time, Pallas kernels for 15%

profile of v4, /device:TPU:1, one launch (start us, length us, event | category | flops | bytes accessed | tf_op | source)
XLA Modules:
  0.0 179.1 jit_solution(8065214511866675721)
XLA Ops:
  0.0 0.7 fusion.16
  0.7 1.2 fusion.45
  1.9 3.3 %multiply_reduce_fusion.2 = f32[4,512]{1,0:T(4,128)S(1)} fusion(f32[4,1536]{1,0:T(4,128)S(1)} %bitcast.32, f32[1536,512]{1,0:T(8,128)} %param.7), kind=kLoop, calls=%fused_computation.4 | loop fusion | flops 6289408 | bytes 3178496 | tf_op jit(solution)/shard_map/reduce_sum | solution.py:60
  5.8 1.3 multiply_reduce_fusion.1
  7.1 0.8 subtract_multiply_fusion
  7.9 1.1 multiply_reduce_fusion
  9.3 5.1 %sort.44 = (s32[1536]{0:T(1024)}, s32[1536]{0:T(1024)S(1)}, s32[1536]{0:T(1024)S(1)}) sort(s32[1536]{0:T(1024)S(1)} %get-tuple-element.33, s32[1536]{0:T(1024)S(1)} %get-tuple-element.34, s32[1536]{0:T(1024)S(1)} %iota.28), dimensions={0}, to_apply=%region_0.1 | sort | flops 16896 | bytes 36864 | tf_op jit(solution)/shard_map/sort | solution.py:73
  15.2 8.9 %gather_fusion = f32[2048,512]{1,0:T(8,128)} fusion(f32[1536,512]{1,0:T(8,128)S(1)} %copy-done, s32[2048]{0:T(1024)S(1)} %broadcast_clamp_fusion), kind=kCustom, calls=%fused_computation | custom fusion | bytes 8396800 | tf_op jit(solution)/shard_map/gather | solution.py:87
  24.1 6.4 %dynamic_update_slice.3 = f32[128,16,512]{2,1,0:T(8,128)} dynamic-update-slice(f32[128,16,512]{2,1,0:T(8,128)} %bitcast.27, f32[128,1,512]{2,1,0:T(1,128)S(1)} %broadcast_in_dim.18, s32[]{:T(128)} %constant.86.clone.1, s32[]{:T(128)} %constant.97.clone.1, s32[]{:T(128)} %constant.86.clone.1) | dynamic-update-slice | bytes 524292 | tf_op jit(solution)/shard_map/dynamic_update_slice | solution.py:88
  30.4 12.0 %all-to-all-start = ((f32[128,16,512]{2,1,0:T(8,128)}), f32[128,16,512]{2,1,0:T(8,128)}, u32[]{:S(2)}, u32[]{:S(2)}) async-start(f32[128,16,512]{2,1,0:T(8,128)} %dynamic_update_slice.3), calls=%async_computation | async-start | bytes 8388608 | tf_op jit(solution)/shard_map/all_to_all | solution.py:89
  42.7 52.3 %all-to-all-done = f32[128,16,512]{2,1,0:T(8,128)} async-done(((f32[128,16,512]{2,1,0:T(8,128)}), f32[128,16,512]{2,1,0:T(8,128)}, u32[]{:S(2)}, u32[]{:S(2)}) %all-to-all-start) | async-done | bytes 4194336 | tf_op jit(solution)/shard_map/all_to_all | solution.py:89
  95.1 1.9 %slice.99 = f32[128,1,512]{2,1,0:T(1,128)S(1)} slice(f32[128,16,512]{2,1,0:T(8,128)} %all-to-all-done), slice={[0:128], [12:13], [0:512]} | slice | bytes 524288 | tf_op jit(solution)/shard_map/slice | solution.py:93
  98.9 5.1 %sort.45 = (s32[1536]{0:T(1024)}, s32[1536]{0:T(1024)S(1)}, s32[1536]{0:T(1024)}) sort(s32[1536]{0:T(1024)S(1)} %convert_element_type.22, s32[1536]{0:T(1024)S(1)} %fusion.12, s32[1536]{0:T(1024)S(1)} %iota.30), dimensions={0}, to_apply=%region_7.8 | sort | flops 16896 | bytes 36864 | tf_op jit(solution)/shard_map/sort | solution.py:109
  104.0 7.9 %gather_fusion.1 = f32[1536,512]{1,0:T(8,128)} fusion(f32[2048,512]{1,0:T(8,128)} %bitcast.5, s32[2048]{0:T(1024)S(1)} %pad_clamp_fusion), kind=kCustom, calls=%fused_computation.1 | custom fusion | bytes 6297600 | tf_op jit(solution)/shard_map/gather | solution.py:110
  111.9 2.9 %multiply_convert_fusion = bf16[6,8,32,512]{3,2,1,0:T(8,128)(2,1)S(1)} fusion(f32[6,8,32,512]{3,2,1,0:T(8,128)} %bitcast.25, f32[512]{0:T(512)S(1)} %copy-done.1, f32[512]{0:T(512)S(1)} %copy-done.2, f32[6,512]{1,0:T(8,128)S(1)} %mul.122, f32[6,512]{1,0:T(8,128)S(1)} %sub.49), kind=kLoop, calls=%fused_computation.6 | loop fusion | flops 7077888 | bytes 4747264 | tf_op jit(solution)/shard_map/convert_element_type | solution.py:123
  114.9 3.6 %collective-permute-start = (bf16[6,1,32,512]{3,2,1,0:T(8,128)(2,1)S(1)}, bf16[6,1,32,512]{3,2,1,0:T(8,128)(2,1)S(1)}, u32[]{:S(2)}, u32[]{:S(2)}) collective-permute-start(bf16[6,1,32,512]{3,2,1,0:T(8,128)(2,1)S(1)} %get-tuple-element.23), channel_id=1, source_target_pairs={{0,1},{1,2},{2,3},{4,5},{5,6},{6,7},{8,9},{9,10},{10,11},{12,13},{... | collective-permute-start | bytes 589832 | tf_op jit(solution)/shard_map/ppermute | solution.py:29
  118.5 1.9 %collective-permute-start.1 = (bf16[6,1,32,512]{3,2,1,0:T(8,128)(2,1)S(1)}, bf16[6,1,32,512]{3,2,1,0:T(8,128)(2,1)S(1)}, u32[]{:S(2)}, u32[]{:S(2)}) collective-permute-start(bf16[6,1,32,512]{3,2,1,0:T(8,128)(2,1)S(1)} %get-tuple-element.24), channel_id=1, source_target_pairs={{1,0},{2,1},{3,2},{5,4},{6,5},{7,6},{9,8},{10,9},{11,10},{13,12},{... | collective-permute-start | bytes 589832 | tf_op jit(solution)/shard_map/ppermute | solution.py:30
  120.5 0.6 select_n.68.valid_ref
  121.1 0.6 reshape.121.valid_ref
  121.7 5.3 %collective-permute-done.1 = bf16[6,1,32,512]{3,2,1,0:T(8,128)(2,1)S(1)} collective-permute-done((bf16[6,1,32,512]{3,2,1,0:T(8,128)(2,1)S(1)}, bf16[6,1,32,512]{3,2,1,0:T(8,128)(2,1)S(1)}, u32[]{:S(2)}, u32[]{:S(2)}) %collective-permute-start.1) | collective-permute-done | bytes 196640 | tf_op jit(solution)/shard_map/ppermute | solution.py:30
  127.2 1.5 collective-permute-start.2
  128.7 1.5 collective-permute-start.3
  130.4 1.3 fusion.40
  131.8 2.8 %collective-permute-done.3 = bf16[6,10,1,512]{3,2,1,0:T(2,128)(2,1)S(1)} collective-permute-done((bf16[6,10,1,512]{3,2,1,0:T(2,128)(2,1)S(1)}, bf16[6,10,1,512]{3,2,1,0:T(2,128)(2,1)S(1)}, u32[]{:S(2)}, u32[]{:S(2)}) %collective-permute-start.3) | collective-permute-done | bytes 61472 | tf_op jit(solution)/shard_map/ppermute | solution.py:128
  134.8 0.7 copy.23
  135.5 2.9 %collective-permute-start.4 = (bf16[2,10,34,512]{3,0,2,1:T(2,128)(2,1)S(1)}, bf16[2,10,34,512]{3,0,2,1:T(2,128)(2,1)S(1)}, u32[]{:S(2)}, u32[]{:S(2)}) collective-permute-start(bf16[2,10,34,512]{3,0,2,1:T(2,128)(2,1)S(1)} %copy.23), channel_id=1, source_target_pairs={{0,4},{4,8},{8,12},{12,16},{16,20},{20,24},{24,28},{1,5},{5,9},{9,... | collective-permute-start | bytes 2088968 | tf_op jit(solution)/shard_map/ppermute | solution.py:19
  138.4 3.8 %maximum_maximum_fusion.x_ref = bf16[6,10,32,1536]{3,2,1,0:T(8,128)(2,1)} fusion(bf16[6,10,1,512]{3,2,1,0:T(2,128)(2,1)S(1)} %collective-permute-done.3, bf16[6,10,31,512]{3,2,1,0:T(8,128)(2,1)S(1)} %get-tuple-element.20, bf16[6,1,32,512]{3,2,1,0:T(8,128)(2,1)S(1)} %collective-permute-done.1, bf16[6,8,32,512]{3,2,1,0:T(8,128)(2,1)S(1)} %multiply_convert_fusion, ...), kind=kLoop, calls=%fused_computation.5 | loop fusion | flops 41287680 | bytes 11796480 | tf_op jit(solution)/shard_map/concatenate | solution.py:151
  142.3 26.1 %shard_map.73 = (bf16[6,8,32,512]{3,2,1,0:T(8,128)(2,1)}, f32[2,8,32,512]{3,2,1,0:T(8,128)}) custom-call(s32[18]{0:T(128)} %select_n.68.valid_ref, bf16[6,10,32,1536]{3,2,1,0:T(8,128)(2,1)} %maximum_maximum_fusion.x_ref, bf16[9,1536,512]{2,1,0:T(8,128)(2,1)} %bitcast.23, f32[1,512]{1,0:T(1,128)} %bitcast.36, f32[6,8,32,512]{3,2,1,0:T(8,128)} %bitcast.26), custom_call_target="tpu_custom_call" | custom-call | tf_op jit(solution)/shard_map/pallas_call | solution.py:188
  168.3 0.7 fusion.43
  169.2 0.5 slice.111
  170.0 1.7 maximum_maximum_fusion.1.x_ref
  171.7 7.4 %shard_map.74 = bf16[6,8,32,512]{3,2,1,0:T(8,128)(2,1)} custom-call(s32[4]{0:T(128)} %reshape.121.valid_ref, bf16[2,10,32,1536]{3,2,1,0:T(8,128)(2,1)} %maximum_maximum_fusion.1.x_ref, bf16[9,1536,512]{2,1,0:T(8,128)(2,1)} %bitcast.24, f32[2,8,32,512]{3,2,1,0:T(8,128)} %get-tuple-element.15.early_ref, ...), custom_call_target="tpu_custom_call", output_to_operand_aliasing={{}: (4, {})} | custom-call | tf_op jit(solution)/shard_map/pallas_call | solution.py:244
  (76 shorter events, 4.9 us)
Async XLA Ops:
  1.9 5.2 %copy-start = (f32[1536,512]{1,0:T(8,128)S(1)}, f32[1536,512]{1,0:T(8,128)}, u32[]{:S(2)}) copy-start(f32[1536,512]{1,0:T(8,128)} %param.7) | copy-start | bytes 9437188
  30.4 12.0 %copy-start.3 = (s32[48]{0:T(128)S(1)}, s32[48]{0:T(128)}, u32[]{:S(2)}) copy-start(s32[48]{0:T(128)} %param.9) | copy-start | bytes 580
  30.4 64.6 %all-to-all-start = ((f32[128,16,512]{2,1,0:T(8,128)}), f32[128,16,512]{2,1,0:T(8,128)}, u32[]{:S(2)}, u32[]{:S(2)}) async-start(f32[128,16,512]{2,1,0:T(8,128)} %dynamic_update_slice.3), calls=%async_computation | async-start | bytes 8388608 | tf_op jit(solution)/shard_map/all_to_all | solution.py:89
  104.0 8.0 %copy-start.1 = (f32[512]{0:T(512)S(1)}, f32[512]{0:T(512)}, u32[]{:S(2)}) copy-start(f32[512]{0:T(512)} %param.11) | copy-start | bytes 6148
  104.0 7.9 %copy-start.2 = (f32[512]{0:T(512)S(1)}, f32[512]{0:T(512)}, u32[]{:S(2)}) copy-start(f32[512]{0:T(512)} %param.10) | copy-start | bytes 6148
  114.9 6.8 %collective-permute-start = (bf16[6,1,32,512]{3,2,1,0:T(8,128)(2,1)S(1)}, bf16[6,1,32,512]{3,2,1,0:T(8,128)(2,1)S(1)}, u32[]{:S(2)}, u32[]{:S(2)}) collective-permute-start(bf16[6,1,32,512]{3,2,1,0:T(8,128)(2,1)S(1)} %get-tuple-element.23), channel_id=1, source_target_pairs={{0,1},{1,2},{2,3},{4,5},{5,6},{6,7},{8,9},{9,10},{10,11},{12,13},{... | collective-permute-start | bytes 589832 | tf_op jit(solution)/shard_map/ppermute | solution.py:29
  118.5 8.5 %collective-permute-start.1 = (bf16[6,1,32,512]{3,2,1,0:T(8,128)(2,1)S(1)}, bf16[6,1,32,512]{3,2,1,0:T(8,128)(2,1)S(1)}, u32[]{:S(2)}, u32[]{:S(2)}) collective-permute-start(bf16[6,1,32,512]{3,2,1,0:T(8,128)(2,1)S(1)} %get-tuple-element.24), channel_id=1, source_target_pairs={{1,0},{2,1},{3,2},{5,4},{6,5},{7,6},{9,8},{10,9},{11,10},{13,12},{... | collective-permute-start | bytes 589832 | tf_op jit(solution)/shard_map/ppermute | solution.py:30
  127.2 4.5 %collective-permute-start.2 = (bf16[6,10,1,512]{3,2,1,0:T(2,128)(2,1)S(1)}, bf16[6,10,1,512]{3,2,1,0:T(2,128)(2,1)S(1)}, u32[]{:S(2)}, u32[]{:S(2)}) collective-permute-start(bf16[6,10,1,512]{3,2,1,0:T(2,128)(2,1)S(1)} %get-tuple-element.21), channel_id=1, source_target_pairs={{0,32},{32,64},{64,96},{1,33},{33,65},{65,97},{2,34},{34,66},{66,9... | collective-permute-start | bytes 184328 | tf_op jit(solution)/shard_map/ppermute | solution.py:127
  128.7 6.0 %collective-permute-start.3 = (bf16[6,10,1,512]{3,2,1,0:T(2,128)(2,1)S(1)}, bf16[6,10,1,512]{3,2,1,0:T(2,128)(2,1)S(1)}, u32[]{:S(2)}, u32[]{:S(2)}) collective-permute-start(bf16[6,10,1,512]{3,2,1,0:T(2,128)(2,1)S(1)} %get-tuple-element.22), channel_id=1, source_target_pairs={{32,0},{64,32},{96,64},{33,1},{65,33},{97,65},{34,2},{66,34},{98,6... | collective-permute-start | bytes 184328 | tf_op jit(solution)/shard_map/ppermute | solution.py:128
  135.5 32.8 %collective-permute-start.4 = (bf16[2,10,34,512]{3,0,2,1:T(2,128)(2,1)S(1)}, bf16[2,10,34,512]{3,0,2,1:T(2,128)(2,1)S(1)}, u32[]{:S(2)}, u32[]{:S(2)}) collective-permute-start(bf16[2,10,34,512]{3,0,2,1:T(2,128)(2,1)S(1)} %copy.23), channel_id=1, source_target_pairs={{0,4},{4,8},{8,12},{12,16},{16,20},{20,24},{24,28},{1,5},{5,9},{9,... | collective-permute-start | bytes 2088968 | tf_op jit(solution)/shard_map/ppermute | solution.py:19

commit v5 on v4

--- a/solution.py
+++ b/solution.py
@@ -68,7 +68,6 @@
         axis=2,
     )
 
-    block = 16
     iota = lax.iota(jnp.int32, local_rows)
     _, sent_slots, ordering = lax.sort((owners, slot_ids, iota), num_keys=1, is_stable=True)
     stats = jnp.concatenate([local_n, local_s.reshape(-1), local_m2.reshape(-1)])
@@ -80,17 +79,13 @@
         ],
         axis=1,
     )
-    pick = jnp.concatenate(
-        [ordering.reshape(devices, per_pair), jnp.zeros((devices, block - per_pair), jnp.int32)],
-        axis=1,
-    )
-    payload = feats[pick.reshape(-1)].reshape(devices, block, channels)
-    payload = lax.dynamic_update_slice(payload, info[:, None, :], (0, per_pair, 0))
+    gathered = feats[ordering].reshape(devices, per_pair, channels)
+    payload = jnp.concatenate([gathered, info[:, None, :]], axis=1).reshape(devices, -1)
     arrived = lax.all_to_all(
         payload, ("src", "frame", "tile"), split_axis=0, concat_axis=0, tiled=True
     )
 
-    info = arrived[:, per_pair, :]
+    info = arrived[:, per_pair * channels :]
     targets = info[:, :per_pair].reshape(-1).astype(jnp.int32)
     part_n = info[:, per_pair : per_pair + CLIPS]
     base = per_pair + CLIPS
@@ -105,9 +100,9 @@
     clip_m2 = jnp.sum(part_m2, axis=0) + jnp.sum(part_n[:, :, None] * spread * spread, axis=0)
     clip_var = clip_m2 / total_n[:, None]
 
-    arrival_row = (iota // per_pair) * block + iota % per_pair
-    _, gather_rows = lax.sort((targets, arrival_row), num_keys=1)
-    features = arrived.reshape(-1, channels)[gather_rows].reshape(FR_DEV, HR, WCOL, channels)
+    _, gather_rows = lax.sort((targets, iota), num_keys=1)
+    rows = arrived[:, : per_pair * channels].reshape(-1, channels)
+    features = rows[gather_rows].reshape(FR_DEV, HR, WCOL, channels)
 
     first_frame = lax.axis_index("frame") * FR_DEV
     padded_ids = jnp.concatenate([jnp.full((2,), -1, jnp.int32), clip_ids])

time: 181 us -> 191 us (1.055)
  local copies, waits for them, and re-layouts: 32.4 us -> 44.4 us
  waiting for transfers between devices: 60.5 us -> 52 us
  other arithmetic: 27.4 us -> 35.3 us
    all_to_all x0 -> x2, local copies, waits for them, and re-layouts: none -> 12 us  [shards(): lax.all_to_all(payload, ('src', 'frame', 'tile'), split_axis=0, concat_ax...]
    all_to_all x1, waiting for transfers between devices: 52.3 us -> 44.2 us  [shards(): lax.all_to_all(payload, ('src', 'frame', 'tile'), split_axis=0, concat_ax...]
    reshape x2, local copies, waits for them, and re-layouts: 0.19 us -> 7.5 us  [the longest x1 4.5 us: shards(): gathered = feats[ordering].reshape(devices, per_pair, channels)]
    gather x2, local copies, waits for them, and re-layouts: 16.8 us -> 9.92 us  [the longest x1 4.96 us: shards(): gathered = feats[ordering].reshape(devices, per_pair, channels)]
    dynamic_update_slice x1 -> x0, local copies, waits for them, and re-layouts: 6.35 us -> none  [shards(): lax.dynamic_update_slice(payload, info[:, None, :], (0, per_pair, 0))]
    concatenate x0 -> x1, other arithmetic: none -> 4.96 us  [shards(): jnp.concatenate([gathered, info[:, None, :]], axis=1).reshape(devices, -1)]
    concatenate x1, local copies, waits for them, and re-layouts: 0.01 us -> 3.51 us  [shards(): jnp.concatenate([gathered, info[:, None, :]], axis=1).reshape(devices, -1)]
    slice x1 -> x2, local copies, waits for them, and re-layouts: 1.85 us -> 4.44 us  [shards(): rows = arrived[:, :per_pair * channels].reshape(-1, channels)]
  transfers between devices with their start and end apart: 6 -> 6, of which waited for: 3 -> 3; matrix products, arithmetic and copies ran while one was open for 4% -> 4% of each run, Pallas kernels for 15% -> 14%
where the time goes in v5:
time: 191 us; the launch traced here: 190 us
  waiting for transfers between devices  52 us (27%)
  local copies, waits for them, and re-layouts  44.4 us (23%)
  other arithmetic  35.3 us (18%)
  Pallas kernels  33.5 us (18%)
  starting transfers between devices  23 us (12%)
    all_to_all x1, waiting for transfers between devices, shards(): lax.all_to_all(payload, ('src', 'frame', 'tile'), split_axis=0, concat_ax...  44.2 us
    pallas_call x1, Pallas kernels, own_conv(): pl.pallas_call(own_kernel, grid_spec=pltpu.PrefetchScalarGridSpec(num_sca...  26.1 us
    all_to_all x2, local copies, waits for them, and re-layouts, shards(): lax.all_to_all(payload, ('src', 'frame', 'tile'), split_axis=0, concat_ax...  12 us
    all_to_all x1, starting transfers between devices, shards(): lax.all_to_all(payload, ('src', 'frame', 'tile'), split_axis=0, concat_ax...  11.5 us
    pallas_call x1, Pallas kernels, prev_conv(): pl.pallas_call(prev_kernel, grid_spec=pltpu.PrefetchScalarGridSpec(num_sc...  7.43 us
    concatenate x2, other arithmetic, widen(): return jnp.concatenate([shifted_in, block, shifted_out], axis=-1)  5.53 us
    ppermute x1, waiting for transfers between devices, with_halo(): after = lax.ppermute(leading, axis, down)  5.32 us
    sort x1, other arithmetic, shards(): lax.sort((owners, slot_ids, iota), num_keys=1, is_stable=True)  5.13 us
  transfers between devices with their start and end apart: 6, of which 3 were waited for; matrix products, arithmetic and copies ran while one was open for 4% of the time, Pallas kernels for 14%

profile of v5, /device:TPU:1, one launch (start us, length us, event | category | flops | bytes accessed | tf_op | source)
XLA Modules:
  0.0 190.3 jit_solution(6784895913596403997)
XLA Ops:
  0.7 1.2 fusion.36
  1.9 3.3 %multiply_reduce_fusion.2 = f32[4,512]{1,0:T(4,128)S(1)} fusion(f32[4,1536]{1,0:T(4,128)S(1)} %bitcast.31, f32[1536,512]{1,0:T(8,128)} %param.7), kind=kLoop, calls=%fused_computation.4 | loop fusion | flops 6289408 | bytes 3178496 | tf_op jit(solution)/shard_map/reduce_sum | solution.py:60
  5.8 1.3 multiply_reduce_fusion.1
  7.9 1.1 multiply_reduce_fusion
  9.3 5.1 %sort.36 = (s32[1536]{0:T(1024)}, s32[1536]{0:T(1024)S(1)}, s32[1536]{0:T(1024)S(1)}) sort(s32[1536]{0:T(1024)S(1)} %get-tuple-element.31, s32[1536]{0:T(1024)S(1)} %get-tuple-element.32, s32[1536]{0:T(1024)S(1)} %iota.25), dimensions={0}, to_apply=%region_0.1 | sort | flops 16896 | bytes 36864 | tf_op jit(solution)/shard_map/sort | solution.py:72
  14.9 5.0 %gather_fusion = f32[1536,512]{1,0:T(8,128)} fusion(f32[1536,512]{1,0:T(8,128)S(1)} %copy-done, s32[2048]{0:T(1024)S(1)} %pad_clamp_fusion.1), kind=kCustom, calls=%fused_computation | custom fusion | bytes 6297600 | tf_op jit(solution)/shard_map/gather | solution.py:82
  19.9 4.5 %reshape.92 = f32[128,12,512]{2,1,0:T(8,128)} reshape(f32[1536,512]{1,0:T(8,128)} %gather_fusion) | data formatting | bytes 6291456 | tf_op jit(solution)/shard_map/reshape | solution.py:82
  24.4 5.0 %pad_maximum_fusion = f32[128,13,512]{2,1,0:T(8,128)} fusion(f32[128,1,512]{2,1,0:T(1,128)S(1)} %broadcast_in_dim.21, f32[128,12,512]{2,1,0:T(8,128)} %reshape.92), kind=kLoop, calls=%fused_computation.6 | loop fusion | flops 851968 | bytes 6815744 | tf_op jit(solution)/shard_map/concatenate | solution.py:83
  29.4 3.5 %copy.23 = f32[128,13,512]{0,2,1:T(8,128)S(1)} copy(f32[128,13,512]{2,1,0:T(8,128)} %pad_maximum_fusion) | data formatting | bytes 6815744 | tf_op jit(solution)/shard_map/concatenate | solution.py:83
  32.9 6.3 %copy.24 = f32[128,1,6656]{2,1,0:T(1,128)} copy(f32[128,1,6656]{0,2,1:T(8,128)S(1)} %bitcast.25) | data formatting | bytes 6815744 | tf_op jit(solution)/shard_map/all_to_all | solution.py:84
  39.2 11.5 %all-to-all-start = ((f32[128,1,6656]{2,1,0:T(1,128)}), f32[128,1,6656]{2,1,0:T(1,128)S(1)}, u32[]{:S(2)}, u32[]{:S(2)}) async-start(f32[128,1,6656]{2,1,0:T(1,128)} %copy.24), calls=%async_computation | async-start | bytes 6815744 | tf_op jit(solution)/shard_map/all_to_all | solution.py:84
  51.0 44.2 %all-to-all-done = f32[128,1,6656]{2,1,0:T(1,128)S(1)} async-done(((f32[128,1,6656]{2,1,0:T(1,128)}), f32[128,1,6656]{2,1,0:T(1,128)S(1)}, u32[]{:S(2)}, u32[]{:S(2)}) %all-to-all-start) | async-done | bytes 3407904 | tf_op jit(solution)/shard_map/all_to_all | solution.py:84
  95.2 5.7 %copy.25 = f32[128,1,6656]{0,2,1:T(8,128)} copy(f32[128,1,6656]{2,1,0:T(1,128)S(1)} %all-to-all-done) | data formatting | bytes 6815744 | tf_op jit(solution)/shard_map/all_to_all | solution.py:84
  102.7 2.1 %slice.104 = f32[128,6144]{0,1:T(8,128)S(1)} slice(f32[128,6656]{0,1:T(8,128)} %bitcast.28), slice={[0:128], [0:6144]} | slice | bytes 6291456 | tf_op jit(solution)/shard_map/slice | solution.py:104
  105.7 1.1 fusion.2
  107.7 2.3 %copy.26 = f32[128,6144]{1,0:T(8,128)} copy(f32[128,6144]{0,1:T(8,128)S(1)} %slice.104) | data formatting | bytes 6291456 | tf_op jit(solution)/shard_map/slice | solution.py:104
  110.1 3.0 %reshape.98 = f32[1536,512]{1,0:T(8,128)S(1)} reshape(f32[128,6144]{1,0:T(8,128)} %copy.26) | data formatting | bytes 6291456 | tf_op jit(solution)/shard_map/reshape | solution.py:104
  113.3 5.0 %sort.37 = (s32[1536]{0:T(1024)}, s32[1536]{0:T(1024)S(1)}) sort(s32[1536]{0:T(1024)S(1)} %convert_element_type.22, s32[1536]{0:T(1024)S(1)} %iota.26), dimensions={0}, to_apply=%region_7.8 | sort | flops 16896 | bytes 24576 | tf_op jit(solution)/shard_map/sort | solution.py:103
  118.4 5.0 %gather_fusion.1 = f32[1536,512]{1,0:T(8,128)} fusion(f32[1536,512]{1,0:T(8,128)S(1)} %reshape.98, s32[2048]{0:T(1024)S(1)} %pad_clamp_fusion), kind=kCustom, calls=%fused_computation.1 | custom fusion | bytes 6297600 | tf_op jit(solution)/shard_map/gather | solution.py:105
  123.3 2.9 %multiply_convert_fusion = bf16[6,8,32,512]{3,2,1,0:T(8,128)(2,1)S(1)} fusion(f32[6,8,32,512]{3,2,1,0:T(8,128)} %bitcast.23, f32[512]{0:T(512)S(1)} %copy-done.1, f32[512]{0:T(512)S(1)} %copy-done.2, f32[6,512]{1,0:T(8,128)S(1)} %mul.114, f32[6,512]{1,0:T(8,128)S(1)} %sub.44), kind=kLoop, calls=%fused_computation.7 | loop fusion | flops 7077888 | bytes 4747264 | tf_op jit(solution)/shard_map/convert_element_type | solution.py:118
  126.2 3.6 %collective-permute-start = (bf16[6,1,32,512]{3,2,1,0:T(8,128)(2,1)S(1)}, bf16[6,1,32,512]{3,2,1,0:T(8,128)(2,1)S(1)}, u32[]{:S(2)}, u32[]{:S(2)}) collective-permute-start(bf16[6,1,32,512]{3,2,1,0:T(8,128)(2,1)S(1)} %get-tuple-element.24), channel_id=1, source_target_pairs={{0,1},{1,2},{2,3},{4,5},{5,6},{6,7},{8,9},{9,10},{10,11},{12,13},{... | collective-permute-start | bytes 589832 | tf_op jit(solution)/shard_map/ppermute | solution.py:29
  129.9 1.9 %collective-permute-start.1 = (bf16[6,1,32,512]{3,2,1,0:T(8,128)(2,1)S(1)}, bf16[6,1,32,512]{3,2,1,0:T(8,128)(2,1)S(1)}, u32[]{:S(2)}, u32[]{:S(2)}) collective-permute-start(bf16[6,1,32,512]{3,2,1,0:T(8,128)(2,1)S(1)} %get-tuple-element.25), channel_id=1, source_target_pairs={{1,0},{2,1},{3,2},{5,4},{6,5},{7,6},{9,8},{10,9},{11,10},{13,12},{... | collective-permute-start | bytes 589832 | tf_op jit(solution)/shard_map/ppermute | solution.py:30
  133.1 5.3 %collective-permute-done.1 = bf16[6,1,32,512]{3,2,1,0:T(8,128)(2,1)S(1)} collective-permute-done((bf16[6,1,32,512]{3,2,1,0:T(8,128)(2,1)S(1)}, bf16[6,1,32,512]{3,2,1,0:T(8,128)(2,1)S(1)}, u32[]{:S(2)}, u32[]{:S(2)}) %collective-permute-start.1) | collective-permute-done | bytes 196640 | tf_op jit(solution)/shard_map/ppermute | solution.py:30
  138.6 1.4 collective-permute-start.2
  140.0 1.5 collective-permute-start.3
  141.7 1.3 fusion.32
  143.1 2.5 %collective-permute-done.3 = bf16[6,10,1,512]{3,2,1,0:T(2,128)(2,1)S(1)} collective-permute-done((bf16[6,10,1,512]{3,2,1,0:T(2,128)(2,1)S(1)}, bf16[6,10,1,512]{3,2,1,0:T(2,128)(2,1)S(1)}, u32[]{:S(2)}, u32[]{:S(2)}) %collective-permute-start.3) | collective-permute-done | bytes 61472 | tf_op jit(solution)/shard_map/ppermute | solution.py:123
  146.5 3.1 %collective-permute-start.4 = (bf16[2,10,34,512]{3,0,2,1:T(2,128)(2,1)S(1)}, bf16[2,10,34,512]{3,0,2,1:T(2,128)(2,1)S(1)}, u32[]{:S(2)}, u32[]{:S(2)}) collective-permute-start(bf16[2,10,34,512]{3,0,2,1:T(2,128)(2,1)S(1)} %copy.28), channel_id=1, source_target_pairs={{0,4},{4,8},{8,12},{12,16},{16,20},{20,24},{24,28},{1,5},{5,9},{9,... | collective-permute-start | bytes 2088968 | tf_op jit(solution)/shard_map/ppermute | solution.py:19
  149.6 3.8 %maximum_maximum_fusion.x_ref = bf16[6,10,32,1536]{3,2,1,0:T(8,128)(2,1)} fusion(bf16[6,10,1,512]{3,2,1,0:T(2,128)(2,1)S(1)} %collective-permute-done.3, bf16[6,10,31,512]{3,2,1,0:T(8,128)(2,1)S(1)} %get-tuple-element.21, bf16[6,1,32,512]{3,2,1,0:T(8,128)(2,1)S(1)} %collective-permute-done.1, bf16[6,8,32,512]{3,2,1,0:T(8,128)(2,1)S(1)} %multiply_convert_fusion, ...), kind=kLoop, calls=%fused_computation.5 | loop fusion | flops 41287680 | bytes 11796480 | tf_op jit(solution)/shard_map/concatenate | solution.py:146
  153.4 26.1 %shard_map.73 = (bf16[6,8,32,512]{3,2,1,0:T(8,128)(2,1)}, f32[2,8,32,512]{3,2,1,0:T(8,128)}) custom-call(s32[18]{0:T(128)} %select_n.52.valid_ref, bf16[6,10,32,1536]{3,2,1,0:T(8,128)(2,1)} %maximum_maximum_fusion.x_ref, bf16[9,1536,512]{2,1,0:T(8,128)(2,1)} %bitcast.21, f32[1,512]{1,0:T(1,128)} %bitcast.34, f32[6,8,32,512]{3,2,1,0:T(8,128)} %bitcast.24), custom_call_target="tpu_custom_call" | custom-call | tf_op jit(solution)/shard_map/pallas_call | solution.py:183
  181.1 1.7 maximum_maximum_fusion.1.x_ref
  182.8 7.4 %shard_map.74 = bf16[6,8,32,512]{3,2,1,0:T(8,128)(2,1)} custom-call(s32[4]{0:T(128)} %reshape.91.valid_ref, bf16[2,10,32,1536]{3,2,1,0:T(8,128)(2,1)} %maximum_maximum_fusion.1.x_ref, bf16[9,1536,512]{2,1,0:T(8,128)(2,1)} %bitcast.22, f32[2,8,32,512]{3,2,1,0:T(8,128)} %get-tuple-element.13.early_ref, ...), custom_call_target="tpu_custom_call", output_to_operand_aliasing={{}: (4, {})} | custom-call | tf_op jit(solution)/shard_map/pallas_call | solution.py:239
  (77 shorter events, 11.1 us)
Async XLA Ops:
  1.9 5.2 %copy-start = (f32[1536,512]{1,0:T(8,128)S(1)}, f32[1536,512]{1,0:T(8,128)}, u32[]{:S(2)}) copy-start(f32[1536,512]{1,0:T(8,128)} %param.7) | copy-start | bytes 9437188
  39.2 11.5 %copy-start.3 = (s32[48]{0:T(128)S(1)}, s32[48]{0:T(128)}, u32[]{:S(2)}) copy-start(s32[48]{0:T(128)} %param.9) | copy-start | bytes 580
  39.2 56.1 %all-to-all-start = ((f32[128,1,6656]{2,1,0:T(1,128)}), f32[128,1,6656]{2,1,0:T(1,128)S(1)}, u32[]{:S(2)}, u32[]{:S(2)}) async-start(f32[128,1,6656]{2,1,0:T(1,128)} %copy.24), calls=%async_computation | async-start | bytes 6815744 | tf_op jit(solution)/shard_map/all_to_all | solution.py:84
  118.3 5.0 %copy-start.1 = (f32[512]{0:T(512)S(1)}, f32[512]{0:T(512)}, u32[]{:S(2)}) copy-start(f32[512]{0:T(512)} %param.11) | copy-start | bytes 6148
  118.3 5.0 %copy-start.2 = (f32[512]{0:T(512)S(1)}, f32[512]{0:T(512)}, u32[]{:S(2)}) copy-start(f32[512]{0:T(512)} %param.10) | copy-start | bytes 6148
  126.2 6.8 %collective-permute-start = (bf16[6,1,32,512]{3,2,1,0:T(8,128)(2,1)S(1)}, bf16[6,1,32,512]{3,2,1,0:T(8,128)(2,1)S(1)}, u32[]{:S(2)}, u32[]{:S(2)}) collective-permute-start(bf16[6,1,32,512]{3,2,1,0:T(8,128)(2,1)S(1)} %get-tuple-element.24), channel_id=1, source_target_pairs={{0,1},{1,2},{2,3},{4,5},{5,6},{6,7},{8,9},{9,10},{10,11},{12,13},{... | collective-permute-start | bytes 589832 | tf_op jit(solution)/shard_map/ppermute | solution.py:29
  129.9 8.5 %collective-permute-start.1 = (bf16[6,1,32,512]{3,2,1,0:T(8,128)(2,1)S(1)}, bf16[6,1,32,512]{3,2,1,0:T(8,128)(2,1)S(1)}, u32[]{:S(2)}, u32[]{:S(2)}) collective-permute-start(bf16[6,1,32,512]{3,2,1,0:T(8,128)(2,1)S(1)} %get-tuple-element.25), channel_id=1, source_target_pairs={{1,0},{2,1},{3,2},{5,4},{6,5},{7,6},{9,8},{10,9},{11,10},{13,12},{... | collective-permute-start | bytes 589832 | tf_op jit(solution)/shard_map/ppermute | solution.py:30
  138.6 4.5 %collective-permute-start.2 = (bf16[6,10,1,512]{3,2,1,0:T(2,128)(2,1)S(1)}, bf16[6,10,1,512]{3,2,1,0:T(2,128)(2,1)S(1)}, u32[]{:S(2)}, u32[]{:S(2)}) collective-permute-start(bf16[6,10,1,512]{3,2,1,0:T(2,128)(2,1)S(1)} %get-tuple-element.22), channel_id=1, source_target_pairs={{0,32},{32,64},{64,96},{1,33},{33,65},{65,97},{2,34},{34,66},{66,9... | collective-permute-start | bytes 184328 | tf_op jit(solution)/shard_map/ppermute | solution.py:122
  140.0 5.6 %collective-permute-start.3 = (bf16[6,10,1,512]{3,2,1,0:T(2,128)(2,1)S(1)}, bf16[6,10,1,512]{3,2,1,0:T(2,128)(2,1)S(1)}, u32[]{:S(2)}, u32[]{:S(2)}) collective-permute-start(bf16[6,10,1,512]{3,2,1,0:T(2,128)(2,1)S(1)} %get-tuple-element.23), channel_id=1, source_target_pairs={{32,0},{64,32},{96,64},{33,1},{65,33},{97,65},{34,2},{66,34},{98,6... | collective-permute-start | bytes 184328 | tf_op jit(solution)/shard_map/ppermute | solution.py:123
  146.5 33.0 %collective-permute-start.4 = (bf16[2,10,34,512]{3,0,2,1:T(2,128)(2,1)S(1)}, bf16[2,10,34,512]{3,0,2,1:T(2,128)(2,1)S(1)}, u32[]{:S(2)}, u32[]{:S(2)}) collective-permute-start(bf16[2,10,34,512]{3,0,2,1:T(2,128)(2,1)S(1)} %copy.28), channel_id=1, source_target_pairs={{0,4},{4,8},{8,12},{12,16},{16,20},{20,24},{24,28},{1,5},{5,9},{9,... | collective-permute-start | bytes 2088968 | tf_op jit(solution)/shard_map/ppermute | solution.py:19

commit v6 on v4

--- a/solution.py
+++ b/solution.py
@@ -80,12 +80,14 @@
         ],
         axis=1,
     )
-    pick = jnp.concatenate(
-        [ordering.reshape(devices, per_pair), jnp.zeros((devices, block - per_pair), jnp.int32)],
+    payload = jnp.concatenate(
+        [
+            feats[ordering.reshape(devices, per_pair)],
+            info[:, None, :],
+            jnp.zeros((devices, block - per_pair - 1, channels), jnp.float32),
+        ],
         axis=1,
     )
-    payload = feats[pick.reshape(-1)].reshape(devices, block, channels)
-    payload = lax.dynamic_update_slice(payload, info[:, None, :], (0, per_pair, 0))
     arrived = lax.all_to_all(
         payload, ("src", "frame", "tile"), split_axis=0, concat_axis=0, tiled=True
     )
@@ -106,7 +108,10 @@
     clip_var = clip_m2 / total_n[:, None]
 
     arrival_row = (iota // per_pair) * block + iota % per_pair
-    _, gather_rows = lax.sort((targets, arrival_row), num_keys=1)
+    digits = jnp.stack([arrival_row // 64, arrival_row % 64], axis=1).astype(jnp.bfloat16)
+    chooser = (targets[None, :] == iota[:, None]).astype(jnp.bfloat16)
+    found = jnp.dot(chooser, digits, preferred_element_type=jnp.float32).astype(jnp.int32)
+    gather_rows = found[:, 0] * 64 + found[:, 1]
     features = arrived.reshape(-1, channels)[gather_rows].reshape(FR_DEV, HR, WCOL, channels)
 
     first_frame = lax.axis_index("frame") * FR_DEV

time: 181 us -> 177 us (0.978)
  local copies, waits for them, and re-layouts: 32.4 us -> 26.6 us
    dynamic_update_slice x1 -> x0, local copies, waits for them, and re-layouts: 6.35 us -> none  [shards(): lax.dynamic_update_slice(payload, info[:, None, :], (0, per_pair, 0))]
    concatenate x0 -> x1, other arithmetic: none -> 5.2 us  [shards(): jnp.concatenate([feats[ordering.reshape(devices, per_pair)], info[:, None...]
    sort x1 -> x0, other arithmetic: 5.12 us -> none  [shards(): _, gather_rows = lax.sort((targets, arrival_row), num_keys=1)]
    gather x1 -> x2, local copies, waits for them, and re-layouts: 8.92 us -> 9.46 us  [shards(): feats[ordering.reshape(devices, per_pair)]]
where the time goes in v6:
time: 177 us; the launch traced here: 175 us
  waiting for transfers between devices  60.4 us (34%)
  Pallas kernels  33.5 us (19%)
  other arithmetic  27.6 us (16%)
  local copies, waits for them, and re-layouts  26.6 us (15%)
  starting transfers between devices  23.3 us (13%)
  matrix products  3.23 us (2%)
    all_to_all x1, waiting for transfers between devices, shards(): lax.all_to_all(payload, ('src', 'frame', 'tile'), split_axis=0, concat_ax...  52.2 us
    pallas_call x1, Pallas kernels, own_conv(): pl.pallas_call(own_kernel, grid_spec=pltpu.PrefetchScalarGridSpec(num_sca...  26.1 us
    all_to_all x1, starting transfers between devices, shards(): lax.all_to_all(payload, ('src', 'frame', 'tile'), split_axis=0, concat_ax...  12 us
    gather x2, local copies, waits for them, and re-layouts, shards(): feats[ordering.reshape(devices, per_pair)]  9.46 us
    gather x1, local copies, waits for them, and re-layouts, shards(): arrived.reshape(-1, channels)[gather_rows]  7.93 us
    pallas_call x1, Pallas kernels, prev_conv(): pl.pallas_call(prev_kernel, grid_spec=pltpu.PrefetchScalarGridSpec(num_sc...  7.43 us
    concatenate x2, other arithmetic, widen(): return jnp.concatenate([shifted_in, block, shifted_out], axis=-1)  5.53 us
    ppermute x1, waiting for transfers between devices, with_halo(): after = lax.ppermute(leading, axis, down)  5.32 us
  transfers between devices with their start and end apart: 6, of which 3 were waited for; matrix products, arithmetic and copies ran while one was open for 4% of the time, Pallas kernels for 15%

profile of v6, /device:TPU:1, one launch (start us, length us, event | category | flops | bytes accessed | tf_op | source)
XLA Modules:
  0.0 175.1 jit_solution(11893994593730609118)
XLA Ops:
  0.0 0.7 fusion.11
  0.7 1.2 fusion.48
  1.9 3.3 %multiply_reduce_fusion.2 = f32[4,512]{1,0:T(4,128)S(1)} fusion(f32[4,1536]{1,0:T(4,128)S(1)} %bitcast.31, f32[1536,512]{1,0:T(8,128)} %param.7), kind=kLoop, calls=%fused_computation.4 | loop fusion | flops 6289408 | bytes 3178496 | tf_op jit(solution)/shard_map/reduce_sum | solution.py:60
  5.8 1.3 multiply_reduce_fusion.1
  7.1 0.8 subtract_multiply_fusion
  7.9 1.1 multiply_reduce_fusion
  9.3 5.1 %sort.21 = (s32[1536]{0:T(1024)}, s32[1536]{0:T(1024)S(1)}, s32[1536]{0:T(1024)S(1)}) sort(s32[1536]{0:T(1024)S(1)} %get-tuple-element.29, s32[1536]{0:T(1024)S(1)} %get-tuple-element.30, s32[1536]{0:T(1024)S(1)} %iota.32), dimensions={0}, to_apply=%region_0.1 | sort | flops 16896 | bytes 36864 | tf_op jit(solution)/shard_map/sort | solution.py:73
  15.2 5.0 %gather_fusion = f32[1536,512]{1,0:T(8,128)} fusion(f32[1536,512]{1,0:T(8,128)S(1)} %copy-done, s32[2048]{0:T(1024)S(1)} %pad_clamp_fusion.1), kind=kCustom, calls=%fused_computation | custom fusion | bytes 6297600 | tf_op jit(solution)/shard_map/gather | solution.py:85
  20.1 4.5 %reshape.250 = f32[128,12,512]{2,1,0:T(8,128)} reshape(f32[1536,512]{1,0:T(8,128)} %gather_fusion) | data formatting | bytes 6291456 | tf_op jit(solution)/shard_map/gather | solution.py:85
  24.7 5.2 %maximum_maximum_fusion.1 = f32[128,16,512]{2,1,0:T(8,128)} fusion(f32[128,1,512]{2,1,0:T(1,128)S(1)} %broadcast_in_dim.18, f32[128,12,512]{2,1,0:T(8,128)} %reshape.250, f32[16]{0:T(128)S(1)} %pad.23.clone), kind=kLoop, calls=%fused_computation.9 | loop fusion | flops 2097152 | bytes 7602240 | tf_op jit(solution)/shard_map/concatenate | solution.py:83
  29.9 12.0 %all-to-all-start = ((f32[128,16,512]{2,1,0:T(8,128)}), f32[128,16,512]{2,1,0:T(8,128)}, u32[]{:S(2)}, u32[]{:S(2)}) async-start(f32[128,16,512]{2,1,0:T(8,128)} %maximum_maximum_fusion.1), calls=%async_computation | async-start | bytes 8388608 | tf_op jit(solution)/shard_map/all_to_all | solution.py:91
  42.3 52.2 %all-to-all-done = f32[128,16,512]{2,1,0:T(8,128)} async-done(((f32[128,16,512]{2,1,0:T(8,128)}), f32[128,16,512]{2,1,0:T(8,128)}, u32[]{:S(2)}, u32[]{:S(2)}) %all-to-all-start) | async-done | bytes 4194336 | tf_op jit(solution)/shard_map/all_to_all | solution.py:91
  94.5 1.9 %slice.107 = f32[128,1,512]{2,1,0:T(1,128)S(1)} slice(f32[128,16,512]{2,1,0:T(8,128)} %all-to-all-done), slice={[0:128], [12:13], [0:512]} | slice | bytes 524288 | tf_op jit(solution)/shard_map/slice | solution.py:95
  98.3 1.7 fusion.2
  100.1 7.9 %gather_fusion.1 = f32[1536,512]{1,0:T(8,128)} fusion(f32[2048,512]{1,0:T(8,128)} %bitcast.3, s32[2048]{0:T(1024)S(1)} %pad_clamp_fusion), kind=kCustom, calls=%fused_computation.1 | custom fusion | bytes 6297600 | tf_op jit(solution)/shard_map/gather | solution.py:115
  108.0 2.9 %multiply_convert_fusion = bf16[6,8,32,512]{3,2,1,0:T(8,128)(2,1)S(1)} fusion(f32[6,8,32,512]{3,2,1,0:T(8,128)} %bitcast.25, f32[512]{0:T(512)S(1)} %copy-done.1, f32[512]{0:T(512)S(1)} %copy-done.2, f32[6,512]{1,0:T(8,128)S(1)} %mul.141, f32[6,512]{1,0:T(8,128)S(1)} %sub.56), kind=kLoop, calls=%fused_computation.10 | loop fusion | flops 7077888 | bytes 4747264 | tf_op jit(solution)/shard_map/convert_element_type | solution.py:128
  110.9 3.6 %collective-permute-start = (bf16[6,1,32,512]{3,2,1,0:T(8,128)(2,1)S(1)}, bf16[6,1,32,512]{3,2,1,0:T(8,128)(2,1)S(1)}, u32[]{:S(2)}, u32[]{:S(2)}) collective-permute-start(bf16[6,1,32,512]{3,2,1,0:T(8,128)(2,1)S(1)} %get-tuple-element.19), channel_id=1, source_target_pairs={{0,1},{1,2},{2,3},{4,5},{5,6},{6,7},{8,9},{9,10},{10,11},{12,13},{... | collective-permute-start | bytes 589832 | tf_op jit(solution)/shard_map/ppermute | solution.py:29
  114.6 1.9 %collective-permute-start.1 = (bf16[6,1,32,512]{3,2,1,0:T(8,128)(2,1)S(1)}, bf16[6,1,32,512]{3,2,1,0:T(8,128)(2,1)S(1)}, u32[]{:S(2)}, u32[]{:S(2)}) collective-permute-start(bf16[6,1,32,512]{3,2,1,0:T(8,128)(2,1)S(1)} %get-tuple-element.20), channel_id=1, source_target_pairs={{1,0},{2,1},{3,2},{5,4},{6,5},{7,6},{9,8},{10,9},{11,10},{13,12},{... | collective-permute-start | bytes 589832 | tf_op jit(solution)/shard_map/ppermute | solution.py:30
  116.6 0.6 select_n.118.valid_ref
  117.2 0.6 reshape.237.valid_ref
  117.7 5.3 %collective-permute-done.1 = bf16[6,1,32,512]{3,2,1,0:T(8,128)(2,1)S(1)} collective-permute-done((bf16[6,1,32,512]{3,2,1,0:T(8,128)(2,1)S(1)}, bf16[6,1,32,512]{3,2,1,0:T(8,128)(2,1)S(1)}, u32[]{:S(2)}, u32[]{:S(2)}) %collective-permute-start.1) | collective-permute-done | bytes 196640 | tf_op jit(solution)/shard_map/ppermute | solution.py:30
  123.2 1.5 collective-permute-start.2
  124.7 1.5 collective-permute-start.3
  126.4 1.3 fusion.43
  127.9 2.8 %collective-permute-done.3 = bf16[6,10,1,512]{3,2,1,0:T(2,128)(2,1)S(1)} collective-permute-done((bf16[6,10,1,512]{3,2,1,0:T(2,128)(2,1)S(1)}, bf16[6,10,1,512]{3,2,1,0:T(2,128)(2,1)S(1)}, u32[]{:S(2)}, u32[]{:S(2)}) %collective-permute-start.3) | collective-permute-done | bytes 61472 | tf_op jit(solution)/shard_map/ppermute | solution.py:133
  130.9 0.7 copy.54
  131.6 2.9 %collective-permute-start.4 = (bf16[2,10,34,512]{3,0,2,1:T(2,128)(2,1)S(1)}, bf16[2,10,34,512]{3,0,2,1:T(2,128)(2,1)S(1)}, u32[]{:S(2)}, u32[]{:S(2)}) collective-permute-start(bf16[2,10,34,512]{3,0,2,1:T(2,128)(2,1)S(1)} %copy.54), channel_id=1, source_target_pairs={{0,4},{4,8},{8,12},{12,16},{16,20},{20,24},{24,28},{1,5},{5,9},{9,... | collective-permute-start | bytes 2088968 | tf_op jit(solution)/shard_map/ppermute | solution.py:19
  134.5 3.8 %maximum_maximum_fusion.x_ref = bf16[6,10,32,1536]{3,2,1,0:T(8,128)(2,1)} fusion(bf16[6,10,1,512]{3,2,1,0:T(2,128)(2,1)S(1)} %collective-permute-done.3, bf16[6,10,31,512]{3,2,1,0:T(8,128)(2,1)S(1)} %get-tuple-element.16, bf16[6,1,32,512]{3,2,1,0:T(8,128)(2,1)S(1)} %collective-permute-done.1, bf16[6,8,32,512]{3,2,1,0:T(8,128)(2,1)S(1)} %multiply_convert_fusion, ...), kind=kLoop, calls=%fused_computation.7 | loop fusion | flops 41287680 | bytes 11796480 | tf_op jit(solution)/shard_map/concatenate | solution.py:156
  138.3 26.1 %shard_map.73 = (bf16[6,8,32,512]{3,2,1,0:T(8,128)(2,1)}, f32[2,8,32,512]{3,2,1,0:T(8,128)}) custom-call(s32[18]{0:T(128)} %select_n.118.valid_ref, bf16[6,10,32,1536]{3,2,1,0:T(8,128)(2,1)} %maximum_maximum_fusion.x_ref, bf16[9,1536,512]{2,1,0:T(8,128)(2,1)} %bitcast.23, f32[1,512]{1,0:T(1,128)} %bitcast.34, f32[6,8,32,512]{3,2,1,0:T(8,128)} %bitcast.26), custom_call_target="tpu_custom_call" | custom-call | tf_op jit(solution)/shard_map/pallas_call | solution.py:193
  164.4 0.7 fusion.46
  166.0 1.7 maximum_maximum_fusion.2.x_ref
  167.7 7.4 %shard_map.74 = bf16[6,8,32,512]{3,2,1,0:T(8,128)(2,1)} custom-call(s32[4]{0:T(128)} %reshape.237.valid_ref, bf16[2,10,32,1536]{3,2,1,0:T(8,128)(2,1)} %maximum_maximum_fusion.2.x_ref, bf16[9,1536,512]{2,1,0:T(8,128)(2,1)} %bitcast.24, f32[2,8,32,512]{3,2,1,0:T(8,128)} %get-tuple-element.11.early_ref, ...), custom_call_target="tpu_custom_call", output_to_operand_aliasing={{}: (4, {})} | custom-call | tf_op jit(solution)/shard_map/pallas_call | solution.py:249
  (77 shorter events, 5.6 us)
Async XLA Ops:
  1.9 5.2 %copy-start = (f32[1536,512]{1,0:T(8,128)S(1)}, f32[1536,512]{1,0:T(8,128)}, u32[]{:S(2)}) copy-start(f32[1536,512]{1,0:T(8,128)} %param.7) | copy-start | bytes 9437188
  29.9 12.0 %copy-start.3 = (s32[48]{0:T(128)S(1)}, s32[48]{0:T(128)}, u32[]{:S(2)}) copy-start(s32[48]{0:T(128)} %param.9) | copy-start | bytes 580
  29.9 64.6 %all-to-all-start = ((f32[128,16,512]{2,1,0:T(8,128)}), f32[128,16,512]{2,1,0:T(8,128)}, u32[]{:S(2)}, u32[]{:S(2)}) async-start(f32[128,16,512]{2,1,0:T(8,128)} %maximum_maximum_fusion.1), calls=%async_computation | async-start | bytes 8388608 | tf_op jit(solution)/shard_map/all_to_all | solution.py:91
  100.0 8.0 %copy-start.1 = (f32[512]{0:T(512)S(1)}, f32[512]{0:T(512)}, u32[]{:S(2)}) copy-start(f32[512]{0:T(512)} %param.11) | copy-start | bytes 6148
  100.0 7.9 %copy-start.2 = (f32[512]{0:T(512)S(1)}, f32[512]{0:T(512)}, u32[]{:S(2)}) copy-start(f32[512]{0:T(512)} %param.10) | copy-start | bytes 6148
  110.9 6.8 %collective-permute-start = (bf16[6,1,32,512]{3,2,1,0:T(8,128)(2,1)S(1)}, bf16[6,1,32,512]{3,2,1,0:T(8,128)(2,1)S(1)}, u32[]{:S(2)}, u32[]{:S(2)}) collective-permute-start(bf16[6,1,32,512]{3,2,1,0:T(8,128)(2,1)S(1)} %get-tuple-element.19), channel_id=1, source_target_pairs={{0,1},{1,2},{2,3},{4,5},{5,6},{6,7},{8,9},{9,10},{10,11},{12,13},{... | collective-permute-start | bytes 589832 | tf_op jit(solution)/shard_map/ppermute | solution.py:29
  114.6 8.5 %collective-permute-start.1 = (bf16[6,1,32,512]{3,2,1,0:T(8,128)(2,1)S(1)}, bf16[6,1,32,512]{3,2,1,0:T(8,128)(2,1)S(1)}, u32[]{:S(2)}, u32[]{:S(2)}) collective-permute-start(bf16[6,1,32,512]{3,2,1,0:T(8,128)(2,1)S(1)} %get-tuple-element.20), channel_id=1, source_target_pairs={{1,0},{2,1},{3,2},{5,4},{6,5},{7,6},{9,8},{10,9},{11,10},{13,12},{... | collective-permute-start | bytes 589832 | tf_op jit(solution)/shard_map/ppermute | solution.py:30
  123.2 4.5 %collective-permute-start.2 = (bf16[6,10,1,512]{3,2,1,0:T(2,128)(2,1)S(1)}, bf16[6,10,1,512]{3,2,1,0:T(2,128)(2,1)S(1)}, u32[]{:S(2)}, u32[]{:S(2)}) collective-permute-start(bf16[6,10,1,512]{3,2,1,0:T(2,128)(2,1)S(1)} %get-tuple-element.17), channel_id=1, source_target_pairs={{0,32},{32,64},{64,96},{1,33},{33,65},{65,97},{2,34},{34,66},{66,9... | collective-permute-start | bytes 184328 | tf_op jit(solution)/shard_map/ppermute | solution.py:132
  124.7 6.0 %collective-permute-start.3 = (bf16[6,10,1,512]{3,2,1,0:T(2,128)(2,1)S(1)}, bf16[6,10,1,512]{3,2,1,0:T(2,128)(2,1)S(1)}, u32[]{:S(2)}, u32[]{:S(2)}) collective-permute-start(bf16[6,10,1,512]{3,2,1,0:T(2,128)(2,1)S(1)} %get-tuple-element.18), channel_id=1, source_target_pairs={{32,0},{64,32},{96,64},{33,1},{65,33},{97,65},{34,2},{66,34},{98,6... | collective-permute-start | bytes 184328 | tf_op jit(solution)/shard_map/ppermute | solution.py:133
  131.6 32.8 %collective-permute-start.4 = (bf16[2,10,34,512]{3,0,2,1:T(2,128)(2,1)S(1)}, bf16[2,10,34,512]{3,0,2,1:T(2,128)(2,1)S(1)}, u32[]{:S(2)}, u32[]{:S(2)}) collective-permute-start(bf16[2,10,34,512]{3,0,2,1:T(2,128)(2,1)S(1)} %copy.54), channel_id=1, source_target_pairs={{0,4},{4,8},{8,12},{12,16},{16,20},{20,24},{24,28},{1,5},{5,9},{9,... | collective-permute-start | bytes 2088968 | tf_op jit(solution)/shard_map/ppermute | solution.py:19

commit v7 on v6

--- a/solution.py
+++ b/solution.py
@@ -70,24 +70,39 @@
 
     block = 16
     iota = lax.iota(jnp.int32, local_rows)
-    _, sent_slots, ordering = lax.sort((owners, slot_ids, iota), num_keys=1, is_stable=True)
+    owner_onehot = (owners[:, None] == jnp.arange(devices, dtype=jnp.int32)[None, :]).astype(
+        jnp.bfloat16
+    )
+    earlier = (iota[:, None] > iota[None, :]).astype(jnp.bfloat16)
+    before = jnp.dot(earlier, owner_onehot, preferred_element_type=jnp.float32)
+    rank = jnp.sum(before * owner_onehot.astype(jnp.float32), axis=1).astype(jnp.int32)
+    position = owners * block + rank
+    slots = lax.iota(jnp.int32, devices * block)
+    placer = (position[None, :] == slots[:, None]).astype(jnp.bfloat16)
+
+    high = lax.reduce_precision(feats, exponent_bits=8, mantissa_bits=7)
+    rest = feats - high
+    middle = lax.reduce_precision(rest, exponent_bits=8, mantissa_bits=7)
+    low = rest - middle
+    pieces = jnp.concatenate([high, middle, low], axis=1).astype(jnp.bfloat16)
+    placed = jnp.dot(placer, pieces, preferred_element_type=jnp.float32)
+    digits = jnp.stack([slot_ids // 64, slot_ids % 64], axis=1).astype(jnp.bfloat16)
+    slot_digits = jnp.dot(placer, digits, preferred_element_type=jnp.float32)
+    sent_slots = (slot_digits[:, 0] * 64 + slot_digits[:, 1]).reshape(devices, block)[:, :per_pair]
+
     stats = jnp.concatenate([local_n, local_s.reshape(-1), local_m2.reshape(-1)])
     info = jnp.concatenate(
         [
-            sent_slots.astype(jnp.float32).reshape(devices, per_pair),
+            sent_slots,
             jnp.broadcast_to(stats, (devices, stats.shape[0])),
             jnp.zeros((devices, channels - per_pair - stats.shape[0]), jnp.float32),
         ],
         axis=1,
     )
-    payload = jnp.concatenate(
-        [
-            feats[ordering.reshape(devices, per_pair)],
-            info[:, None, :],
-            jnp.zeros((devices, block - per_pair - 1, channels), jnp.float32),
-        ],
-        axis=1,
-    )
+    rows = (placed[:, :channels] + placed[:, channels : 2 * channels]) + placed[:, 2 * channels :]
+    rows = rows.reshape(devices, block, channels)
+    is_info = (jnp.arange(block) == per_pair)[None, :, None]
+    payload = jnp.where(is_info, info[:, None, :], rows)
     arrived = lax.all_to_all(
         payload, ("src", "frame", "tile"), split_axis=0, concat_axis=0, tiled=True
     )

time: 177 us -> 177 us (level)
  matrix products: 3.23 us -> 18.1 us
  local copies, waits for them, and re-layouts: 26.6 us -> 17 us
  other arithmetic: 27.6 us -> 22.3 us
    dot_general x0 -> x3, matrix products: none -> 15.5 us  [the longest x1 12.2 us: shards(): placed = jnp.dot(placer, pieces, preferred_element_type=jnp.float32)]
    gather x2 -> x0, local copies, waits for them, and re-layouts: 9.46 us -> none  [shards(): feats[ordering.reshape(devices, per_pair)]]
    concatenate x2 -> x1, other arithmetic: 5.23 us -> 0.03 us  [shards(): jnp.concatenate([sent_slots, jnp.broadcast_to(stats, (devices, stats.shap...]
    sort x1 -> x0, other arithmetic: 5.13 us -> none  [shards(): lax.sort((owners, slot_ids, iota), num_keys=1, is_stable=True)]
    select_n x1 -> x2, other arithmetic: 0.01 us -> 3.47 us  [the longest x1 2.76 us: shards(): payload = jnp.where(is_info, info[:, None, :], rows)]
    mul x1, other arithmetic: 0.76 us -> 3.55 us  [shards(): dev * dev]
    reduce_sum x1, other arithmetic: 3.33 us -> 1.09 us  [shards(): jnp.sum(feats[None] * clip_mask, axis=1).reshape(CLIPS, GROUPS, group_width)]
where the time goes in v7:
time: 177 us; the launch traced here: 175 us
  waiting for transfers between devices  60.6 us (34%)
  Pallas kernels  33.5 us (19%)
  starting transfers between devices  23.4 us (13%)
  other arithmetic  22.3 us (13%)
  matrix products  18.1 us (10%)
  local copies, waits for them, and re-layouts  17 us (10%)
    all_to_all x1, waiting for transfers between devices, shards(): lax.all_to_all(payload, ('src', 'frame', 'tile'), split_axis=0, concat_ax...  52.3 us
    pallas_call x1, Pallas kernels, own_conv(): pl.pallas_call(own_kernel, grid_spec=pltpu.PrefetchScalarGridSpec(num_sca...  26.1 us
    dot_general x1, matrix products, shards(): placed = jnp.dot(placer, pieces, preferred_element_type=jnp.float32)  12.2 us
    all_to_all x1, starting transfers between devices, shards(): lax.all_to_all(payload, ('src', 'frame', 'tile'), split_axis=0, concat_ax...  12 us
    gather x1, local copies, waits for them, and re-layouts, shards(): arrived.reshape(-1, channels)[gather_rows]  7.93 us
    pallas_call x1, Pallas kernels, prev_conv(): pl.pallas_call(prev_kernel, grid_spec=pltpu.PrefetchScalarGridSpec(num_sc...  7.43 us
    concatenate x2, other arithmetic, widen(): return jnp.concatenate([shifted_in, block, shifted_out], axis=-1)  5.53 us
    ppermute x1, waiting for transfers between devices, with_halo(): after = lax.ppermute(leading, axis, down)  5.32 us
  transfers between devices with their start and end apart: 6, of which 3 were waited for; matrix products, arithmetic and copies ran while one was open for 4% of the time, Pallas kernels for 15%

profile of v7, /device:TPU:1, one launch (start us, length us, event | category | flops | bytes accessed | tf_op | source)
XLA Modules:
  0.0 175.5 jit_solution(977385008113105059)
XLA Ops:
  0.0 0.7 add_select_fusion.6
  0.7 1.2 fusion.15
  2.0 2.2 %fusion.1 = f32[2048,2]{0,1:T(2,128)S(1)} fusion(s32[1536]{0:T(1024)S(1)} %get-tuple-element.29, bf16[1536,1]{0,1:T(2,128)(2,1)S(1)} %stack.40, bf16[1536,1]{0,1:T(2,128)(2,1)S(1)} %stack.39), kind=kOutput, calls=%fused_computation.6 | convolution fusion | flops 15740928 | bytes 28672 | tf_op jit(solution)/shard_map/dot_general | solution.py:90
  4.8 1.1 multiply_reduce_fusion.2
  6.5 1.3 multiply_reduce_fusion.1
  7.8 3.5 %subtract_multiply_fusion = (f32[1536,512]{1,0:T(8,128)S(1)}, bf16[1536,512]{1,0:T(8,128)(2,1)}, bf16[1536,512]{1,0:T(8,128)(2,1)}, bf16[1536,512]{1,0:T(8,128)(2,1)}) fusion(f32[1536,512]{1,0:T(8,128)S(1)} %copy-done, f32[1536,512]{1,0:T(8,128)S(1)} %multiply_reduce_fusion.1), kind=kLoop, calls=%fused_computation.28 | loop fusion | flops 7077888 | bytes 14155776 | tf_op jit(solution)/shard_map/mul | solution.py:67
  11.4 1.3 multiply_reduce_fusion
  13.3 12.2 %fusion = f32[2048,1536]{1,0:T(8,128)S(1)} fusion(s32[1536]{0:T(1024)S(1)} %get-tuple-element.29, bf16[1536,512]{1,0:T(8,128)(2,1)S(1)} %copy-done.1, bf16[1536,512]{1,0:T(8,128)(2,1)S(1)} %copy-done.2, bf16[1536,512]{1,0:T(8,128)(2,1)} %get-tuple-element.14), kind=kOutput, calls=%fused_computation.5 | convolution fusion | flops 9680977920 | bytes 17307648 | tf_op jit(solution)/shard_map/dot_general | solution.py:88
  25.4 1.6 slice_add_fusion
  27.2 2.8 %broadcast_select_fusion = f32[128,16,512]{2,1,0:T(8,128)} fusion(f32[128,16,512]{2,1,0:T(8,128)S(1)} %bitcast.27, f32[128,512]{1,0:T(8,128)S(1)} %maximum_maximum_fusion.2, pred[16]{0:T(512)(128)(4,1)S(1)} %iota_compare_fusion.22), kind=kLoop, calls=%fused_computation.31 | loop fusion | flops 1048576 | bytes 8650768 | tf_op jit(solution)/shard_map/jit(_where)/select_n | solution.py:105
  30.0 12.0 %all-to-all-start = ((f32[128,16,512]{2,1,0:T(8,128)}), f32[128,16,512]{2,1,0:T(8,128)}, u32[]{:S(2)}, u32[]{:S(2)}) async-start(f32[128,16,512]{2,1,0:T(8,128)} %broadcast_select_fusion), calls=%async_computation | async-start | bytes 8388608 | tf_op jit(solution)/shard_map/all_to_all | solution.py:106
  42.3 52.3 %all-to-all-done = f32[128,16,512]{2,1,0:T(8,128)} async-done(((f32[128,16,512]{2,1,0:T(8,128)}), f32[128,16,512]{2,1,0:T(8,128)}, u32[]{:S(2)}, u32[]{:S(2)}) %all-to-all-start) | async-done | bytes 4194336 | tf_op jit(solution)/shard_map/all_to_all | solution.py:106
  94.6 1.9 %slice.135 = f32[128,1,512]{2,1,0:T(1,128)S(1)} slice(f32[128,16,512]{2,1,0:T(8,128)} %all-to-all-done), slice={[0:128], [12:13], [0:512]} | slice | bytes 524288 | tf_op jit(solution)/shard_map/slice | solution.py:110
  98.0 1.7 fusion.14
  100.1 7.9 %gather_fusion = f32[1536,512]{1,0:T(8,128)} fusion(f32[2048,512]{1,0:T(8,128)} %bitcast.4, s32[2048]{0:T(1024)S(1)} %pad_clamp_fusion), kind=kCustom, calls=%fused_computation | custom fusion | bytes 6297600 | tf_op jit(solution)/shard_map/gather | solution.py:130
  108.0 2.9 %multiply_convert_fusion = bf16[6,8,32,512]{3,2,1,0:T(8,128)(2,1)S(1)} fusion(f32[6,8,32,512]{3,2,1,0:T(8,128)} %bitcast.25, f32[512]{0:T(512)S(1)} %copy-done.4, f32[512]{0:T(512)S(1)} %copy-done.5, f32[6,512]{1,0:T(8,128)S(1)} %mul.152, f32[6,512]{1,0:T(8,128)S(1)} %sub.69), kind=kLoop, calls=%fused_computation.27 | loop fusion | flops 7077888 | bytes 4747264 | tf_op jit(solution)/shard_map/convert_element_type | solution.py:143
  111.0 3.6 %collective-permute-start = (bf16[6,1,32,512]{3,2,1,0:T(8,128)(2,1)S(1)}, bf16[6,1,32,512]{3,2,1,0:T(8,128)(2,1)S(1)}, u32[]{:S(2)}, u32[]{:S(2)}) collective-permute-start(bf16[6,1,32,512]{3,2,1,0:T(8,128)(2,1)S(1)} %get-tuple-element.19), channel_id=1, source_target_pairs={{0,1},{1,2},{2,3},{4,5},{5,6},{6,7},{8,9},{9,10},{10,11},{12,13},{... | collective-permute-start | bytes 589832 | tf_op jit(solution)/shard_map/ppermute | solution.py:29
  114.6 1.9 %collective-permute-start.1 = (bf16[6,1,32,512]{3,2,1,0:T(8,128)(2,1)S(1)}, bf16[6,1,32,512]{3,2,1,0:T(8,128)(2,1)S(1)}, u32[]{:S(2)}, u32[]{:S(2)}) collective-permute-start(bf16[6,1,32,512]{3,2,1,0:T(8,128)(2,1)S(1)} %get-tuple-element.20), channel_id=1, source_target_pairs={{1,0},{2,1},{3,2},{5,4},{6,5},{7,6},{9,8},{10,9},{11,10},{13,12},{... | collective-permute-start | bytes 589832 | tf_op jit(solution)/shard_map/ppermute | solution.py:30
  116.6 0.6 select_n.121.valid_ref
  117.2 0.6 reshape.219.valid_ref
  117.8 5.3 %collective-permute-done.1 = bf16[6,1,32,512]{3,2,1,0:T(8,128)(2,1)S(1)} collective-permute-done((bf16[6,1,32,512]{3,2,1,0:T(8,128)(2,1)S(1)}, bf16[6,1,32,512]{3,2,1,0:T(8,128)(2,1)S(1)}, u32[]{:S(2)}, u32[]{:S(2)}) %collective-permute-start.1) | collective-permute-done | bytes 196640 | tf_op jit(solution)/shard_map/ppermute | solution.py:30
  123.3 1.5 collective-permute-start.2
  124.8 1.3 collective-permute-start.3
  126.3 1.3 fusion.67
  127.7 3.0 %collective-permute-done.3 = bf16[6,10,1,512]{3,2,1,0:T(2,128)(2,1)S(1)} collective-permute-done((bf16[6,10,1,512]{3,2,1,0:T(2,128)(2,1)S(1)}, bf16[6,10,1,512]{3,2,1,0:T(2,128)(2,1)S(1)}, u32[]{:S(2)}, u32[]{:S(2)}) %collective-permute-start.3) | collective-permute-done | bytes 61472 | tf_op jit(solution)/shard_map/ppermute | solution.py:148
  130.9 0.7 copy.23
  131.7 3.1 %collective-permute-start.4 = (bf16[2,10,34,512]{3,0,2,1:T(2,128)(2,1)S(1)}, bf16[2,10,34,512]{3,0,2,1:T(2,128)(2,1)S(1)}, u32[]{:S(2)}, u32[]{:S(2)}) collective-permute-start(bf16[2,10,34,512]{3,0,2,1:T(2,128)(2,1)S(1)} %copy.23), channel_id=1, source_target_pairs={{0,4},{4,8},{8,12},{12,16},{16,20},{20,24},{24,28},{1,5},{5,9},{9,... | collective-permute-start | bytes 2088968 | tf_op jit(solution)/shard_map/ppermute | solution.py:19
  134.8 3.8 %maximum_maximum_fusion.x_ref = bf16[6,10,32,1536]{3,2,1,0:T(8,128)(2,1)} fusion(bf16[6,10,1,512]{3,2,1,0:T(2,128)(2,1)S(1)} %collective-permute-done.3, bf16[6,10,31,512]{3,2,1,0:T(8,128)(2,1)S(1)} %get-tuple-element.16, bf16[6,1,32,512]{3,2,1,0:T(8,128)(2,1)S(1)} %collective-permute-done.1, bf16[6,8,32,512]{3,2,1,0:T(8,128)(2,1)S(1)} %multiply_convert_fusion, ...), kind=kLoop, calls=%fused_computation.13 | loop fusion | flops 41287680 | bytes 11796480 | tf_op jit(solution)/shard_map/concatenate | solution.py:171
  138.6 26.1 %shard_map.73 = (bf16[6,8,32,512]{3,2,1,0:T(8,128)(2,1)}, f32[2,8,32,512]{3,2,1,0:T(8,128)}) custom-call(s32[18]{0:T(128)} %select_n.121.valid_ref, bf16[6,10,32,1536]{3,2,1,0:T(8,128)(2,1)} %maximum_maximum_fusion.x_ref, bf16[9,1536,512]{2,1,0:T(8,128)(2,1)} %bitcast.23, f32[1,512]{1,0:T(1,128)} %bitcast.36, f32[6,8,32,512]{3,2,1,0:T(8,128)} %bitcast.26), custom_call_target="tpu_custom_call" | custom-call | tf_op jit(solution)/shard_map/pallas_call | solution.py:208
  165.5 0.7 fusion.70
  166.3 1.7 maximum_maximum_fusion.1.x_ref
  168.0 7.4 %shard_map.74 = bf16[6,8,32,512]{3,2,1,0:T(8,128)(2,1)} custom-call(s32[4]{0:T(128)} %reshape.219.valid_ref, bf16[2,10,32,1536]{3,2,1,0:T(8,128)(2,1)} %maximum_maximum_fusion.1.x_ref, bf16[9,1536,512]{2,1,0:T(8,128)(2,1)} %bitcast.24, f32[2,8,32,512]{3,2,1,0:T(8,128)} %get-tuple-element.7.early_ref, ...), custom_call_target="tpu_custom_call", output_to_operand_aliasing={{}: (4, {})} | custom-call | tf_op jit(solution)/shard_map/pallas_call | solution.py:264
  (80 shorter events, 6.0 us)
Async XLA Ops:
  0.7 1.2 copy-start.3
  1.9 2.3 %copy-start.6 = (s32[48]{0:T(128)S(1)}, s32[48]{0:T(128)}, u32[]{:S(2)}) copy-start(s32[48]{0:T(128)} %param.9) | copy-start | bytes 580
  1.9 2.8 %copy-start = (f32[1536,512]{1,0:T(8,128)S(1)}, f32[1536,512]{1,0:T(8,128)}, u32[]{:S(2)}) copy-start(f32[1536,512]{1,0:T(8,128)} %param.7) | copy-start | bytes 9437188
  11.4 1.5 copy-start.1
  11.4 1.9 %copy-start.2 = (bf16[1536,512]{1,0:T(8,128)(2,1)S(1)}, bf16[1536,512]{1,0:T(8,128)(2,1)}, u32[]{:S(2)}) copy-start(bf16[1536,512]{1,0:T(8,128)(2,1)} %get-tuple-element.13) | copy-start | bytes 4718596
  30.0 64.6 %all-to-all-start = ((f32[128,16,512]{2,1,0:T(8,128)}), f32[128,16,512]{2,1,0:T(8,128)}, u32[]{:S(2)}, u32[]{:S(2)}) async-start(f32[128,16,512]{2,1,0:T(8,128)} %broadcast_select_fusion), calls=%async_computation | async-start | bytes 8388608 | tf_op jit(solution)/shard_map/all_to_all | solution.py:106
  100.1 8.0 %copy-start.4 = (f32[512]{0:T(512)S(1)}, f32[512]{0:T(512)}, u32[]{:S(2)}) copy-start(f32[512]{0:T(512)} %param.11) | copy-start | bytes 6148
  100.1 7.9 %copy-start.5 = (f32[512]{0:T(512)S(1)}, f32[512]{0:T(512)}, u32[]{:S(2)}) copy-start(f32[512]{0:T(512)} %param.10) | copy-start | bytes 6148
  111.0 6.8 %collective-permute-start = (bf16[6,1,32,512]{3,2,1,0:T(8,128)(2,1)S(1)}, bf16[6,1,32,512]{3,2,1,0:T(8,128)(2,1)S(1)}, u32[]{:S(2)}, u32[]{:S(2)}) collective-permute-start(bf16[6,1,32,512]{3,2,1,0:T(8,128)(2,1)S(1)} %get-tuple-element.19), channel_id=1, source_target_pairs={{0,1},{1,2},{2,3},{4,5},{5,6},{6,7},{8,9},{9,10},{10,11},{12,13},{... | collective-permute-start | bytes 589832 | tf_op jit(solution)/shard_map/ppermute | solution.py:29
  114.6 8.5 %collective-permute-start.1 = (bf16[6,1,32,512]{3,2,1,0:T(8,128)(2,1)S(1)}, bf16[6,1,32,512]{3,2,1,0:T(8,128)(2,1)S(1)}, u32[]{:S(2)}, u32[]{:S(2)}) collective-permute-start(bf16[6,1,32,512]{3,2,1,0:T(8,128)(2,1)S(1)} %get-tuple-element.20), channel_id=1, source_target_pairs={{1,0},{2,1},{3,2},{5,4},{6,5},{7,6},{9,8},{10,9},{11,10},{13,12},{... | collective-permute-start | bytes 589832 | tf_op jit(solution)/shard_map/ppermute | solution.py:30
  123.3 4.4 %collective-permute-start.2 = (bf16[6,10,1,512]{3,2,1,0:T(2,128)(2,1)S(1)}, bf16[6,10,1,512]{3,2,1,0:T(2,128)(2,1)S(1)}, u32[]{:S(2)}, u32[]{:S(2)}) collective-permute-start(bf16[6,10,1,512]{3,2,1,0:T(2,128)(2,1)S(1)} %get-tuple-element.17), channel_id=1, source_target_pairs={{0,32},{32,64},{64,96},{1,33},{33,65},{65,97},{2,34},{34,66},{66,9... | collective-permute-start | bytes 184328 | tf_op jit(solution)/shard_map/ppermute | solution.py:147
  124.8 6.0 %collective-permute-start.3 = (bf16[6,10,1,512]{3,2,1,0:T(2,128)(2,1)S(1)}, bf16[6,10,1,512]{3,2,1,0:T(2,128)(2,1)S(1)}, u32[]{:S(2)}, u32[]{:S(2)}) collective-permute-start(bf16[6,10,1,512]{3,2,1,0:T(2,128)(2,1)S(1)} %get-tuple-element.18), channel_id=1, source_target_pairs={{32,0},{64,32},{96,64},{33,1},{65,33},{97,65},{34,2},{66,34},{98,6... | collective-permute-start | bytes 184328 | tf_op jit(solution)/shard_map/ppermute | solution.py:148
  131.7 33.0 %collective-permute-start.4 = (bf16[2,10,34,512]{3,0,2,1:T(2,128)(2,1)S(1)}, bf16[2,10,34,512]{3,0,2,1:T(2,128)(2,1)S(1)}, u32[]{:S(2)}, u32[]{:S(2)}) collective-permute-start(bf16[2,10,34,512]{3,0,2,1:T(2,128)(2,1)S(1)} %copy.23), channel_id=1, source_target_pairs={{0,4},{4,8},{8,12},{12,16},{16,20},{20,24},{24,28},{1,5},{5,9},{9,... | collective-permute-start | bytes 2088968 | tf_op jit(solution)/shard_map/ppermute | solution.py:19

commit v8 on v6

--- a/solution.py
+++ b/solution.py
@@ -71,12 +71,10 @@
     block = 16
     iota = lax.iota(jnp.int32, local_rows)
     _, sent_slots, ordering = lax.sort((owners, slot_ids, iota), num_keys=1, is_stable=True)
-    stats = jnp.concatenate([local_n, local_s.reshape(-1), local_m2.reshape(-1)])
     info = jnp.concatenate(
         [
             sent_slots.astype(jnp.float32).reshape(devices, per_pair),
-            jnp.broadcast_to(stats, (devices, stats.shape[0])),
-            jnp.zeros((devices, channels - per_pair - stats.shape[0]), jnp.float32),
+            jnp.zeros((devices, channels - per_pair), jnp.float32),
         ],
         axis=1,
     )
@@ -94,12 +92,11 @@
 
     info = arrived[:, per_pair, :]
     targets = info[:, :per_pair].reshape(-1).astype(jnp.int32)
-    part_n = info[:, per_pair : per_pair + CLIPS]
-    base = per_pair + CLIPS
-    part_s = info[:, base : base + CLIPS * GROUPS].reshape(devices, CLIPS, GROUPS)
-    part_m2 = info[:, base + CLIPS * GROUPS : base + 2 * CLIPS * GROUPS].reshape(
-        devices, CLIPS, GROUPS
-    )
+    stats = jnp.concatenate([local_n, local_s.reshape(-1), local_m2.reshape(-1)])
+    everyone = lax.all_gather(stats, ("src", "frame", "tile"))
+    part_n = everyone[:, :CLIPS]
+    part_s = everyone[:, CLIPS : CLIPS + CLIPS * GROUPS].reshape(devices, CLIPS, GROUPS)
+    part_m2 = everyone[:, CLIPS + CLIPS * GROUPS :].reshape(devices, CLIPS, GROUPS)
     total_n = jnp.sum(part_n, axis=0)
     clip_mean = jnp.sum(part_s, axis=0) / total_n[:, None]
     part_m = part_s / jnp.maximum(part_n, 1.0)[:, :, None]

time: 177 us -> 307 us (1.73)
  waiting for transfers between devices: 60.4 us -> 176 us
  between operations: 0.47 us -> 13.9 us
    unnamed x0 -> x2, waiting for transfers between devices: none -> 169 us
    all_to_all x1, waiting for transfers between devices: 52.2 us -> 0.01 us  [shards(): lax.all_to_all(payload, ('src', 'frame', 'tile'), split_axis=0, concat_ax...]
  transfers between devices with their start and end apart: 6 -> 7, of which waited for: 3 -> 3; matrix products, arithmetic and copies ran while one was open for 4% -> 5% of each run, Pallas kernels for 15% -> 9%
where the time goes in v8:
time: 307 us; the launch traced here: 305 us
  waiting for transfers between devices  176 us (57%)
  Pallas kernels  33.5 us (11%)
  local copies, waits for them, and re-layouts  27.9 us (9%)
  other arithmetic  25.3 us (8%)
  starting transfers between devices  25.2 us (8%)
  between operations  13.9 us (5%)
    unnamed x2, waiting for transfers between devices  169 us
    pallas_call x1, Pallas kernels, own_conv(): pl.pallas_call(own_kernel, grid_spec=pltpu.PrefetchScalarGridSpec(num_sca...  26.1 us
    all_to_all x1, starting transfers between devices, shards(): lax.all_to_all(payload, ('src', 'frame', 'tile'), split_axis=0, concat_ax...  12 us
    gather x2, local copies, waits for them, and re-layouts, shards(): feats[ordering.reshape(devices, per_pair)]  9 us
    gather x1, local copies, waits for them, and re-layouts, shards(): arrived.reshape(-1, channels)[gather_rows]  7.93 us
    pallas_call x1, Pallas kernels, prev_conv(): pl.pallas_call(prev_kernel, grid_spec=pltpu.PrefetchScalarGridSpec(num_sc...  7.43 us
  transfers between devices with their start and end apart: 7, of which 3 were waited for; matrix products, arithmetic and copies ran while one was open for 5% of the time, Pallas kernels for 9%

profile of v8, /device:TPU:1, one launch (start us, length us, event | category | flops | bytes accessed | tf_op | source)
XLA Modules:
  0.0 304.7 jit_solution(3398442285846839078)
XLA Ops:
  6.5 0.7 fusion.10
  7.3 5.1 %sort.21 = (s32[1536]{0:T(1024)}, s32[1536]{0:T(1024)S(1)}, s32[1536]{0:T(1024)S(1)}) sort(s32[1536]{0:T(1024)S(1)} %get-tuple-element.28, s32[1536]{0:T(1024)S(1)} %get-tuple-element.29, s32[1536]{0:T(1024)S(1)} %iota.32), dimensions={0}, to_apply=%region_0.1 | sort | flops 16896 | bytes 36864 | tf_op jit(solution)/shard_map/sort | solution.py:73
  12.6 6.9 %gather_fusion = f32[1536,512]{1,0:T(8,128)S(1)} fusion(f32[1536,512]{1,0:T(8,128)} %param.7, s32[2048]{0:T(1024)S(1)} %pad_clamp_fusion.1), kind=kCustom, calls=%fused_computation | custom fusion | bytes 6297600 | tf_op jit(solution)/shard_map/gather | solution.py:83
  19.5 2.1 reshape.250
  22.1 5.2 %maximum_maximum_fusion.1 = f32[128,16,512]{2,1,0:T(8,128)} fusion(f32[128,1,512]{2,1,0:T(1,128)S(1)} %broadcast_in_dim.11, f32[128,12,512]{2,1,0:T(8,128)} %reshape.250, f32[16]{0:T(128)S(1)} %pad.27.clone), kind=kLoop, calls=%fused_computation.9 | loop fusion | flops 2097152 | bytes 7602240 | tf_op jit(solution)/shard_map/concatenate | solution.py:81
  27.3 12.0 %all-to-all-start = ((f32[128,16,512]{2,1,0:T(8,128)}), f32[128,16,512]{2,1,0:T(8,128)}, u32[]{:S(2)}, u32[]{:S(2)}) async-start(f32[128,16,512]{2,1,0:T(8,128)} %maximum_maximum_fusion.1), calls=%async_computation | async-start | bytes 8388608 | tf_op jit(solution)/shard_map/all_to_all | solution.py:89
  39.8 1.1 multiply_reduce_fusion.2
  41.5 1.3 multiply_reduce_fusion.1
  42.8 0.8 subtract_multiply_fusion
  43.6 1.1 multiply_reduce_fusion
  45.2 0.7 copy-done.1
  46.2 168.5 %all-reduce.5.cloned.1.call-done = f32[33280]{0:T(1024)} async-done(((f32[33280]{0:T(1024)}), f32[33280]{0:T(1024)}) %all-reduce.5.cloned.1.call-update) | async-done | bytes 133136
  214.8 1.1 reshape.265
  217.6 1.9 slice.107
  219.6 1.7 fusion.2
  221.3 7.9 %gather_fusion.1 = f32[1536,512]{1,0:T(8,128)} fusion(f32[2048,512]{1,0:T(8,128)} %bitcast.2, s32[2048]{0:T(1024)S(1)} %pad_clamp_fusion), kind=kCustom, calls=%fused_computation.1 | custom fusion | bytes 6297600 | tf_op jit(solution)/shard_map/gather | solution.py:112
  229.3 2.9 multiply_convert_fusion
  232.2 4.5 %collective-permute-start = (bf16[6,1,32,512]{3,2,1,0:T(8,128)(2,1)S(1)}, bf16[6,1,32,512]{3,2,1,0:T(8,128)(2,1)S(1)}, u32[]{:S(2)}, u32[]{:S(2)}) collective-permute-start(bf16[6,1,32,512]{3,2,1,0:T(8,128)(2,1)S(1)} %get-tuple-element.19), channel_id=1, source_target_pairs={{0,1},{1,2},{2,3},{4,5},{5,6},{6,7},{8,9},{9,10},{10,11},{12,13},{... | collective-permute-start | bytes 589832 | tf_op jit(solution)/shard_map/ppermute | solution.py:29
  236.6 2.1 collective-permute-start.1
  238.8 0.6 select_n.118.valid_ref
  240.0 5.1 %collective-permute-done.1 = bf16[6,1,32,512]{3,2,1,0:T(8,128)(2,1)S(1)} collective-permute-done((bf16[6,1,32,512]{3,2,1,0:T(8,128)(2,1)S(1)}, bf16[6,1,32,512]{3,2,1,0:T(8,128)(2,1)S(1)}, u32[]{:S(2)}, u32[]{:S(2)}) %collective-permute-start.1) | collective-permute-done | bytes 196640 | tf_op jit(solution)/shard_map/ppermute | solution.py:30
  245.3 2.8 collective-permute-start.2
  248.2 1.3 collective-permute-start.3
  249.7 1.3 fusion.42
  251.1 2.7 collective-permute-done.3
  254.0 0.7 copy.36
  254.7 2.5 collective-permute-start.4
  257.2 3.8 %maximum_maximum_fusion.x_ref = bf16[6,10,32,1536]{3,2,1,0:T(8,128)(2,1)} fusion(bf16[6,10,1,512]{3,2,1,0:T(2,128)(2,1)S(1)} %collective-permute-done.3, bf16[6,10,31,512]{3,2,1,0:T(8,128)(2,1)S(1)} %get-tuple-element.16, bf16[6,1,32,512]{3,2,1,0:T(8,128)(2,1)S(1)} %collective-permute-done.1, bf16[6,8,32,512]{3,2,1,0:T(8,128)(2,1)S(1)} %multiply_convert_fusion, ...), kind=kLoop, calls=%fused_computation.7 | loop fusion | flops 41287680 | bytes 11796480 | tf_op jit(solution)/shard_map/concatenate | solution.py:153
  261.0 26.1 %shard_map.73 = (bf16[6,8,32,512]{3,2,1,0:T(8,128)(2,1)}, f32[2,8,32,512]{3,2,1,0:T(8,128)}) custom-call(s32[18]{0:T(128)} %select_n.118.valid_ref, bf16[6,10,32,1536]{3,2,1,0:T(8,128)(2,1)} %maximum_maximum_fusion.x_ref, bf16[9,1536,512]{2,1,0:T(8,128)(2,1)} %bitcast.19, f32[1,512]{1,0:T(1,128)} %bitcast.29, f32[6,8,32,512]{3,2,1,0:T(8,128)} %bitcast.22), custom_call_target="tpu_custom_call" | custom-call | tf_op jit(solution)/shard_map/pallas_call | solution.py:190
  287.1 0.7 fusion.45
  288.7 1.7 maximum_maximum_fusion.2.x_ref
  290.4 7.4 %shard_map.74 = bf16[6,8,32,512]{3,2,1,0:T(8,128)(2,1)} custom-call(s32[4]{0:T(128)} %reshape.237.valid_ref, bf16[2,10,32,1536]{3,2,1,0:T(8,128)(2,1)} %maximum_maximum_fusion.2.x_ref, bf16[9,1536,512]{2,1,0:T(8,128)(2,1)} %bitcast.20, f32[2,8,32,512]{3,2,1,0:T(8,128)} %get-tuple-element.11.early_ref, ...), custom_call_target="tpu_custom_call", output_to_operand_aliasing={{}: (4, {})} | custom-call | tf_op jit(solution)/shard_map/pallas_call | solution.py:246
  (87 shorter events, 6.7 us)
Async XLA Ops:
  27.3 12.0 %copy-start.4 = (s32[48]{0:T(128)S(1)}, s32[48]{0:T(128)}, u32[]{:S(2)}) copy-start(s32[48]{0:T(128)} %param.9) | copy-start | bytes 580
  27.3 12.6 %copy-start = (f32[1536,512]{1,0:T(8,128)S(1)}, f32[1536,512]{1,0:T(8,128)}, u32[]{:S(2)}) copy-start(f32[1536,512]{1,0:T(8,128)} %param.7) | copy-start | bytes 9437188
  27.3 190.3 %all-to-all-start = ((f32[128,16,512]{2,1,0:T(8,128)}), f32[128,16,512]{2,1,0:T(8,128)}, u32[]{:S(2)}, u32[]{:S(2)}) async-start(f32[128,16,512]{2,1,0:T(8,128)} %maximum_maximum_fusion.1), calls=%async_computation | async-start | bytes 8388608 | tf_op jit(solution)/shard_map/all_to_all | solution.py:89
  39.2 175.5 %all-reduce.5.cloned.1.call-start = ((), (), s32[]{:S(2)}) async-start(), calls=%async_computation.1 | async-start | bytes 270336
  45.2 0.7 copy-start.1
  221.3 8.0 %copy-start.2 = (f32[512]{0:T(512)S(1)}, f32[512]{0:T(512)}, u32[]{:S(2)}) copy-start(f32[512]{0:T(512)} %param.11) | copy-start | bytes 6148
  221.3 7.9 %copy-start.3 = (f32[512]{0:T(512)S(1)}, f32[512]{0:T(512)}, u32[]{:S(2)}) copy-start(f32[512]{0:T(512)} %param.10) | copy-start | bytes 6148
  232.2 7.8 %collective-permute-start = (bf16[6,1,32,512]{3,2,1,0:T(8,128)(2,1)S(1)}, bf16[6,1,32,512]{3,2,1,0:T(8,128)(2,1)S(1)}, u32[]{:S(2)}, u32[]{:S(2)}) collective-permute-start(bf16[6,1,32,512]{3,2,1,0:T(8,128)(2,1)S(1)} %get-tuple-element.19), channel_id=1, source_target_pairs={{0,1},{1,2},{2,3},{4,5},{5,6},{6,7},{8,9},{9,10},{10,11},{12,13},{... | collective-permute-start | bytes 589832 | tf_op jit(solution)/shard_map/ppermute | solution.py:29
  236.6 8.5 %collective-permute-start.1 = (bf16[6,1,32,512]{3,2,1,0:T(8,128)(2,1)S(1)}, bf16[6,1,32,512]{3,2,1,0:T(8,128)(2,1)S(1)}, u32[]{:S(2)}, u32[]{:S(2)}) collective-permute-start(bf16[6,1,32,512]{3,2,1,0:T(8,128)(2,1)S(1)} %get-tuple-element.20), channel_id=1, source_target_pairs={{1,0},{2,1},{3,2},{5,4},{6,5},{7,6},{9,8},{10,9},{11,10},{13,12},{... | collective-permute-start | bytes 589832 | tf_op jit(solution)/shard_map/ppermute | solution.py:30
  245.3 5.7 %collective-permute-start.2 = (bf16[6,10,1,512]{3,2,1,0:T(2,128)(2,1)S(1)}, bf16[6,10,1,512]{3,2,1,0:T(2,128)(2,1)S(1)}, u32[]{:S(2)}, u32[]{:S(2)}) collective-permute-start(bf16[6,10,1,512]{3,2,1,0:T(2,128)(2,1)S(1)} %get-tuple-element.17), channel_id=1, source_target_pairs={{0,32},{32,64},{64,96},{1,33},{33,65},{65,97},{2,34},{34,66},{66,9... | collective-permute-start | bytes 184328 | tf_op jit(solution)/shard_map/ppermute | solution.py:129
  248.2 5.6 %collective-permute-start.3 = (bf16[6,10,1,512]{3,2,1,0:T(2,128)(2,1)S(1)}, bf16[6,10,1,512]{3,2,1,0:T(2,128)(2,1)S(1)}, u32[]{:S(2)}, u32[]{:S(2)}) collective-permute-start(bf16[6,10,1,512]{3,2,1,0:T(2,128)(2,1)S(1)} %get-tuple-element.18), channel_id=1, source_target_pairs={{32,0},{64,32},{96,64},{33,1},{65,33},{97,65},{34,2},{66,34},{98,6... | collective-permute-start | bytes 184328 | tf_op jit(solution)/shard_map/ppermute | solution.py:130
  254.7 32.4 %collective-permute-start.4 = (bf16[2,10,34,512]{3,0,2,1:T(2,128)(2,1)S(1)}, bf16[2,10,34,512]{3,0,2,1:T(2,128)(2,1)S(1)}, u32[]{:S(2)}, u32[]{:S(2)}) collective-permute-start(bf16[2,10,34,512]{3,0,2,1:T(2,128)(2,1)S(1)} %copy.36), channel_id=1, source_target_pairs={{0,4},{4,8},{8,12},{12,16},{16,20},{20,24},{24,28},{1,5},{5,9},{9,... | collective-permute-start | bytes 2088968 | tf_op jit(solution)/shard_map/ppermute | solution.py:19
Sparse Core Ops, SparseCore 0:
  46.0 168.7 all-reduce.4

commit v9 on v6

--- a/solution.py
+++ b/solution.py
@@ -119,18 +119,39 @@
     window_ids = lax.dynamic_slice_in_dim(padded_ids, first_frame, FR_DEV + 2)
     own_ids = window_ids[2:]
     onehot = (own_ids[:, None] == jnp.arange(CLIPS, dtype=jnp.int32)[None, :]).astype(jnp.float32)
-    shaped = features.reshape(FR_DEV, per_frame, GROUPS, group_width)
     frame_mean = jnp.dot(onehot, clip_mean, precision=HIGH)
-    centred = shaped - frame_mean[:, None, :, None]
     inverse_std = 1.0 / jnp.sqrt(clip_var + 1e-06)
     frame_inv = jnp.dot(onehot, inverse_std, precision=HIGH)
-    normed = (centred * frame_inv[:, None, :, None]).reshape(FR_DEV, HR, WCOL, channels)
-    activated = jax.nn.silu(normed * norm_gain + norm_bias).astype(jnp.bfloat16)
-    high_padded = with_halo(activated, (("tile", 1),), 1)
-    n_wide = lax.axis_size("src")
-    up = [(i, i + 1) for i in range(n_wide - 1)]
-    left = lax.ppermute(high_padded[:, :, WCOL - 1 :], "src", up)
-    right = lax.ppermute(high_padded[:, :, :1], "src", [(j, i) for i, j in up])
+
+    def activate(x):
+        grouped = x.reshape(FR_DEV, -1, GROUPS, group_width)
+        centred = grouped - frame_mean[:, None, :, None]
+        normed = (centred * frame_inv[:, None, :, None]).reshape(x.shape)
+        return jax.nn.silu(normed * norm_gain + norm_bias).astype(jnp.bfloat16)
+
+    grid_rows = gather_rows.reshape(FR_DEV, HR, WCOL)
+    edge_rows = jnp.concatenate(
+        [grid_rows[:, 0], grid_rows[:, HR - 1], grid_rows[:, :, 0], grid_rows[:, :, WCOL - 1]],
+        axis=1,
+    )
+    edges = activate(arrived.reshape(-1, channels)[edge_rows])
+    top_own = edges[:, :WCOL]
+    bottom_own = edges[:, WCOL : 2 * WCOL]
+    first_col = edges[:, 2 * WCOL : 2 * WCOL + HR]
+    last_col = edges[:, 2 * WCOL + HR :]
+    top_halo = passed_along(bottom_own, "tile", 1)
+    bottom_halo = passed_along(top_own, "tile", -1)
+    left = passed_along(
+        jnp.concatenate([top_halo[:, WCOL - 1 :], last_col, bottom_halo[:, WCOL - 1 :]], axis=1),
+        "src",
+        1,
+    )[:, :, None]
+    right = passed_along(
+        jnp.concatenate([top_halo[:, :1], first_col, bottom_halo[:, :1]], axis=1), "src", -1
+    )[:, :, None]
+
+    activated = activate(features)
+    high_padded = jnp.concatenate([top_halo[:, None], activated, bottom_halo[:, None]], axis=1)
     own_wide = widen(high_padded, left, right)
     sent_prev = jnp.concatenate(
         [high_padded[FR_DEV - 2 :], left[FR_DEV - 2 :], right[FR_DEV - 2 :]], axis=2

time: 177 us -> 182 us (1.028)
  local copies, waits for them, and re-layouts: 26.6 us -> 31.5 us
  waiting for transfers between devices: 60.4 us -> 57.9 us
  starting transfers between devices: 23.3 us -> 25.4 us
    ppermute x1 -> x5, starting transfers between devices: 2.86 us -> 13.5 us  [passed_along(): return lax.ppermute(x, axis, pairs)]
    ppermute x4 -> x0, starting transfers between devices: 8.5 us -> none  [the longest x1 3.65 us: with_halo(): before = lax.ppermute(last, axis, up)]
    ppermute x4 -> x0, waiting for transfers between devices: 8.16 us -> none  [the longest x1 5.32 us: with_halo(): after = lax.ppermute(leading, axis, down)]
    ppermute x1 -> x5, waiting for transfers between devices: 0.01 us -> 6.92 us  [passed_along(): return lax.ppermute(x, axis, pairs)]
    gather x0 -> x1, local copies, waits for them, and re-layouts: none -> 4.89 us  [shards(): edges = activate(arrived.reshape(-1, channels)[edge_rows])]
  transfers between devices with their start and end apart: 6 -> 6, of which waited for: 3 -> 3; matrix products, arithmetic and copies ran while one was open for 4% -> 4% of each run, Pallas kernels for 15% -> 14%
where the time goes in v9:
time: 182 us; the launch traced here: 180 us
  waiting for transfers between devices  57.9 us (32%)
  Pallas kernels  33.5 us (18%)
  local copies, waits for them, and re-layouts  31.5 us (17%)
  other arithmetic  28 us (15%)
  starting transfers between devices  25.4 us (14%)
  matrix products  3.25 us (2%)
    all_to_all x1, waiting for transfers between devices, shards(): lax.all_to_all(payload, ('src', 'frame', 'tile'), split_axis=0, concat_ax...  51 us
    pallas_call x1, Pallas kernels, own_conv(): pl.pallas_call(own_kernel, grid_spec=pltpu.PrefetchScalarGridSpec(num_sca...  26.1 us
    ppermute x5, starting transfers between devices, passed_along(): return lax.ppermute(x, axis, pairs)  13.5 us
    all_to_all x1, starting transfers between devices, shards(): lax.all_to_all(payload, ('src', 'frame', 'tile'), split_axis=0, concat_ax...  12 us
    gather x2, local copies, waits for them, and re-layouts, shards(): feats[ordering.reshape(devices, per_pair)]  9.48 us
    pallas_call x1, Pallas kernels, prev_conv(): pl.pallas_call(prev_kernel, grid_spec=pltpu.PrefetchScalarGridSpec(num_sc...  7.43 us
    gather x1, local copies, waits for them, and re-layouts, shards(): arrived.reshape(-1, channels)[gather_rows]  7.21 us
    ppermute x5, waiting for transfers between devices, passed_along(): return lax.ppermute(x, axis, pairs)  6.92 us
  transfers between devices with their start and end apart: 6, of which 3 were waited for; matrix products, arithmetic and copies ran while one was open for 4% of the time, Pallas kernels for 14%

profile of v9, /device:TPU:1, one launch (start us, length us, event | category | flops | bytes accessed | tf_op | source)
XLA Modules:
  0.0 180.1 jit_solution(13109170061596798274)
XLA Ops:
  0.2 0.7 fusion.11
  0.9 5.1 %sort.21 = (s32[1536]{0:T(1024)}, s32[1536]{0:T(1024)S(1)}, s32[1536]{0:T(1024)S(1)}) sort(s32[1536]{0:T(1024)S(1)} %get-tuple-element.39, s32[1536]{0:T(1024)S(1)} %get-tuple-element.40, s32[1536]{0:T(1024)S(1)} %iota.32), dimensions={0}, to_apply=%region_0.1 | sort | flops 16896 | bytes 36864 | tf_op jit(solution)/shard_map/sort | solution.py:73
  6.0 1.2 fusion.53
  7.2 3.3 %multiply_reduce_fusion.2 = f32[4,512]{1,0:T(4,128)S(1)} fusion(f32[4,1536]{1,0:T(4,128)S(1)} %bitcast.51, f32[1536,512]{1,0:T(8,128)} %param.7), kind=kLoop, calls=%fused_computation.5 | loop fusion | flops 6289408 | bytes 3178496 | tf_op jit(solution)/shard_map/reduce_sum | solution.py:60
  11.5 1.3 multiply_reduce_fusion.1
  12.8 0.8 subtract_multiply_fusion
  13.6 1.1 multiply_reduce_fusion
  15.2 5.0 %gather_fusion = f32[1536,512]{1,0:T(8,128)} fusion(f32[1536,512]{1,0:T(8,128)S(1)} %copy-done, s32[2048]{0:T(1024)S(1)} %pad_clamp_fusion.1), kind=kCustom, calls=%fused_computation | custom fusion | bytes 6297600 | tf_op jit(solution)/shard_map/gather | solution.py:85
  20.2 4.5 %reshape.408 = f32[128,12,512]{2,1,0:T(8,128)} reshape(f32[1536,512]{1,0:T(8,128)} %gather_fusion) | data formatting | bytes 6291456 | tf_op jit(solution)/shard_map/gather | solution.py:85
  24.7 5.2 %maximum_maximum_fusion.1 = f32[128,16,512]{2,1,0:T(8,128)} fusion(f32[128,1,512]{2,1,0:T(1,128)S(1)} %broadcast_in_dim.26, f32[128,12,512]{2,1,0:T(8,128)} %reshape.408, f32[16]{0:T(128)S(1)} %pad.33.clone), kind=kLoop, calls=%fused_computation.10 | loop fusion | flops 2097152 | bytes 7602240 | tf_op jit(solution)/shard_map/concatenate | solution.py:83
  29.9 12.0 %all-to-all-start = ((f32[128,16,512]{2,1,0:T(8,128)}), f32[128,16,512]{2,1,0:T(8,128)}, u32[]{:S(2)}, u32[]{:S(2)}) async-start(f32[128,16,512]{2,1,0:T(8,128)} %maximum_maximum_fusion.1), calls=%async_computation | async-start | bytes 8388608 | tf_op jit(solution)/shard_map/all_to_all | solution.py:91
  43.5 51.0 %all-to-all-done = f32[128,16,512]{2,1,0:T(8,128)} async-done(((f32[128,16,512]{2,1,0:T(8,128)}), f32[128,16,512]{2,1,0:T(8,128)}, u32[]{:S(2)}, u32[]{:S(2)}) %all-to-all-start) | async-done | bytes 4194336 | tf_op jit(solution)/shard_map/all_to_all | solution.py:91
  94.5 1.9 %slice.149 = f32[128,1,512]{2,1,0:T(1,128)S(1)} slice(f32[128,16,512]{2,1,0:T(8,128)} %all-to-all-done), slice={[0:128], [12:13], [0:512]} | slice | bytes 524288 | tf_op jit(solution)/shard_map/slice | solution.py:95
  96.9 1.7 fusion.2
  100.6 4.9 %gather_fusion.1 = f32[480,512]{1,0:T(8,128)} fusion(f32[2048,512]{1,0:T(8,128)} %bitcast.3, s32[1024]{0:T(1024)S(1)} %pad_clamp_fusion.2), kind=kCustom, calls=%fused_computation.1 | custom fusion | bytes 1968000 | tf_op jit(solution)/shard_map/gather | solution.py:137
  105.5 7.2 %gather_fusion.2 = f32[1536,512]{1,0:T(8,128)S(1)} fusion(f32[2048,512]{1,0:T(8,128)} %bitcast.3, s32[2048]{0:T(1024)S(1)} %pad_clamp_fusion), kind=kCustom, calls=%fused_computation.2 | custom fusion | bytes 6297600 | tf_op jit(solution)/shard_map/gather | solution.py:115
  112.7 2.3 %multiply_convert_fusion.1 = bf16[6,80,512]{2,1,0:T(8,128)(2,1)S(1)} fusion(f32[6,80,512]{2,1,0:T(8,128)} %bitcast.42, f32[512]{0:T(512)S(1)} %copy-done.2, f32[512]{0:T(512)S(1)} %copy-done.3, f32[6,512]{1,0:T(8,128)S(1)} %mul.164, f32[6,512]{1,0:T(8,128)S(1)} %sub.65), kind=kLoop, calls=%fused_computation.16 | loop fusion | flops 2211840 | bytes 1503232 | tf_op jit(solution)/shard_map/convert_element_type | solution.py:130
  115.0 3.6 %collective-permute-start = (bf16[6,32,512]{2,1,0:T(8,128)(2,1)S(1)}, bf16[6,32,512]{2,1,0:T(8,128)(2,1)S(1)}, u32[]{:S(2)}, u32[]{:S(2)}) collective-permute-start(bf16[6,32,512]{2,1,0:T(8,128)(2,1)S(1)} %get-tuple-element.25), channel_id=1, source_target_pairs={{0,1},{1,2},{2,3},{4,5},{5,6},{6,7},{8,9},{9,10},{10,11},{12,13},{... | collective-permute-start | bytes 589832 | tf_op jit(solution)/shard_map/ppermute | solution.py:19
  118.7 2.1 %collective-permute-start.1 = (bf16[6,32,512]{2,1,0:T(8,128)(2,1)S(1)}, bf16[6,32,512]{2,1,0:T(8,128)(2,1)S(1)}, u32[]{:S(2)}, u32[]{:S(2)}) collective-permute-start(bf16[6,32,512]{2,1,0:T(8,128)(2,1)S(1)} %get-tuple-element.26), channel_id=1, source_target_pairs={{1,0},{2,1},{3,2},{5,4},{6,5},{7,6},{9,8},{10,9},{11,10},{13,12},{... | collective-permute-start | bytes 589832 | tf_op jit(solution)/shard_map/ppermute | solution.py:19
  120.8 1.0 multiply_convert_fusion
  121.8 5.4 %collective-permute-done.1 = bf16[6,32,512]{2,1,0:T(8,128)(2,1)S(1)} collective-permute-done((bf16[6,32,512]{2,1,0:T(8,128)(2,1)S(1)}, bf16[6,32,512]{2,1,0:T(8,128)(2,1)S(1)}, u32[]{:S(2)}, u32[]{:S(2)}) %collective-permute-start.1) | collective-permute-done | bytes 196640 | tf_op jit(solution)/shard_map/ppermute | solution.py:19
  127.5 1.3 fusion.44
  128.9 1.3 collective-permute-start.3
  130.3 4.0 %collective-permute-start.2 = (bf16[6,10,512]{2,1,0:T(8,128)(2,1)S(1)}, bf16[6,10,512]{2,1,0:T(8,128)(2,1)S(1)}, u32[]{:S(2)}, u32[]{:S(2)}) collective-permute-start(bf16[6,10,512]{2,1,0:T(8,128)(2,1)S(1)} %pad_maximum_fusion.2), channel_id=1, source_target_pairs={{0,32},{32,64},{64,96},{1,33},{33,65},{65,97},{2,34},{34,66},{66,9... | collective-permute-start | bytes 184328 | tf_op jit(solution)/shard_map/ppermute | solution.py:19
  134.3 1.6 collective-permute-done.2
  136.2 0.7 copy.162
  137.0 2.4 %collective-permute-start.4 = (bf16[2,10,34,512]{3,0,2,1:T(2,128)(2,1)S(1)}, bf16[2,10,34,512]{3,0,2,1:T(2,128)(2,1)S(1)}, u32[]{:S(2)}, u32[]{:S(2)}) collective-permute-start(bf16[2,10,34,512]{3,0,2,1:T(2,128)(2,1)S(1)} %copy.162), channel_id=1, source_target_pairs={{0,4},{4,8},{8,12},{12,16},{16,20},{20,24},{24,28},{1,5},{5,9},{9,... | collective-permute-start | bytes 2088968 | tf_op jit(solution)/shard_map/ppermute | solution.py:19
  139.4 3.8 %maximum_maximum_fusion.x_ref = bf16[6,10,32,1536]{3,2,1,0:T(8,128)(2,1)} fusion(bf16[6,10,1,512]{3,2,1,0:T(2,128)(2,1)S(1)} %copy.171, bf16[6,10,31,512]{3,2,1,0:T(8,128)(2,1)S(1)} %get-tuple-element.18, bf16[6,1,32,512]{3,2,1,0:T(8,128)(2,1)S(1)} %bitcast.46, bf16[6,8,32,512]{3,2,1,0:T(8,128)(2,1)S(1)} %multiply_convert_fusion, ...), kind=kLoop, calls=%fused_computation.8 | loop fusion | flops 41287680 | bytes 11796480 | tf_op jit(solution)/shard_map/concatenate | solution.py:177
  143.3 26.1 %shard_map.73 = (bf16[6,8,32,512]{3,2,1,0:T(8,128)(2,1)}, f32[2,8,32,512]{3,2,1,0:T(8,128)}) custom-call(s32[18]{0:T(128)} %select_n.129.valid_ref, bf16[6,10,32,1536]{3,2,1,0:T(8,128)(2,1)} %maximum_maximum_fusion.x_ref, bf16[9,1536,512]{2,1,0:T(8,128)(2,1)} %bitcast.38, f32[1,512]{1,0:T(1,128)} %bitcast.56, f32[6,8,32,512]{3,2,1,0:T(8,128)} %bitcast.41), custom_call_target="tpu_custom_call" | custom-call | tf_op jit(solution)/shard_map/pallas_call | solution.py:214
  170.1 0.7 fusion.46
  171.0 1.7 maximum_maximum_fusion.2.x_ref
  172.7 7.4 %shard_map.74 = bf16[6,8,32,512]{3,2,1,0:T(8,128)(2,1)} custom-call(s32[4]{0:T(128)} %reshape.395.valid_ref, bf16[2,10,32,1536]{3,2,1,0:T(8,128)(2,1)} %maximum_maximum_fusion.2.x_ref, bf16[9,1536,512]{2,1,0:T(8,128)(2,1)} %bitcast.39, f32[2,8,32,512]{3,2,1,0:T(8,128)} %get-tuple-element.11.early_ref, ...), custom_call_target="tpu_custom_call", output_to_operand_aliasing={{}: (4, {})} | custom-call | tf_op jit(solution)/shard_map/pallas_call | solution.py:270
  (97 shorter events, 7.5 us)
Async XLA Ops:
  7.2 5.6 %copy-start = (f32[1536,512]{1,0:T(8,128)S(1)}, f32[1536,512]{1,0:T(8,128)}, u32[]{:S(2)}) copy-start(f32[1536,512]{1,0:T(8,128)} %param.7) | copy-start | bytes 9437188
  29.9 12.0 %copy-start.4 = (s32[48]{0:T(128)S(1)}, s32[48]{0:T(128)}, u32[]{:S(2)}) copy-start(s32[48]{0:T(128)} %param.9) | copy-start | bytes 580
  29.9 64.6 %all-to-all-start = ((f32[128,16,512]{2,1,0:T(8,128)}), f32[128,16,512]{2,1,0:T(8,128)}, u32[]{:S(2)}, u32[]{:S(2)}) async-start(f32[128,16,512]{2,1,0:T(8,128)} %maximum_maximum_fusion.1), calls=%async_computation | async-start | bytes 8388608 | tf_op jit(solution)/shard_map/all_to_all | solution.py:91
  105.5 7.2 %copy-start.2 = (f32[512]{0:T(512)S(1)}, f32[512]{0:T(512)}, u32[]{:S(2)}) copy-start(f32[512]{0:T(512)} %param.11) | copy-start | bytes 6148
  105.5 7.2 %copy-start.3 = (f32[512]{0:T(512)S(1)}, f32[512]{0:T(512)}, u32[]{:S(2)}) copy-start(f32[512]{0:T(512)} %param.10) | copy-start | bytes 6148
  112.7 9.1 %copy-start.1 = (f32[1536,512]{1,0:T(8,128)}, f32[1536,512]{1,0:T(8,128)S(1)}, u32[]{:S(2)}) copy-start(f32[1536,512]{1,0:T(8,128)S(1)} %gather_fusion.2) | copy-start | bytes 9437188
  115.0 6.8 %collective-permute-start = (bf16[6,32,512]{2,1,0:T(8,128)(2,1)S(1)}, bf16[6,32,512]{2,1,0:T(8,128)(2,1)S(1)}, u32[]{:S(2)}, u32[]{:S(2)}) collective-permute-start(bf16[6,32,512]{2,1,0:T(8,128)(2,1)S(1)} %get-tuple-element.25), channel_id=1, source_target_pairs={{0,1},{1,2},{2,3},{4,5},{5,6},{6,7},{8,9},{9,10},{10,11},{12,13},{... | collective-permute-start | bytes 589832 | tf_op jit(solution)/shard_map/ppermute | solution.py:19
  118.7 8.5 %collective-permute-start.1 = (bf16[6,32,512]{2,1,0:T(8,128)(2,1)S(1)}, bf16[6,32,512]{2,1,0:T(8,128)(2,1)S(1)}, u32[]{:S(2)}, u32[]{:S(2)}) collective-permute-start(bf16[6,32,512]{2,1,0:T(8,128)(2,1)S(1)} %get-tuple-element.26), channel_id=1, source_target_pairs={{1,0},{2,1},{3,2},{5,4},{6,5},{7,6},{9,8},{10,9},{11,10},{13,12},{... | collective-permute-start | bytes 589832 | tf_op jit(solution)/shard_map/ppermute | solution.py:19
  128.9 5.4 %collective-permute-start.3 = (bf16[6,10,512]{2,1,0:T(8,128)(2,1)S(1)}, bf16[6,10,512]{2,1,0:T(8,128)(2,1)S(1)}, u32[]{:S(2)}, u32[]{:S(2)}) collective-permute-start(bf16[6,10,512]{2,1,0:T(8,128)(2,1)S(1)} %pad_maximum_fusion.3), channel_id=1, source_target_pairs={{32,0},{64,32},{96,64},{33,1},{65,33},{97,65},{34,2},{66,34},{98,6... | collective-permute-start | bytes 184328 | tf_op jit(solution)/shard_map/ppermute | solution.py:19
  130.3 5.6 %collective-permute-start.2 = (bf16[6,10,512]{2,1,0:T(8,128)(2,1)S(1)}, bf16[6,10,512]{2,1,0:T(8,128)(2,1)S(1)}, u32[]{:S(2)}, u32[]{:S(2)}) collective-permute-start(bf16[6,10,512]{2,1,0:T(8,128)(2,1)S(1)} %pad_maximum_fusion.2), channel_id=1, source_target_pairs={{0,32},{32,64},{64,96},{1,33},{33,65},{65,97},{2,34},{34,66},{66,9... | collective-permute-start | bytes 184328 | tf_op jit(solution)/shard_map/ppermute | solution.py:19
  137.0 32.4 %collective-permute-start.4 = (bf16[2,10,34,512]{3,0,2,1:T(2,128)(2,1)S(1)}, bf16[2,10,34,512]{3,0,2,1:T(2,128)(2,1)S(1)}, u32[]{:S(2)}, u32[]{:S(2)}) collective-permute-start(bf16[2,10,34,512]{3,0,2,1:T(2,128)(2,1)S(1)} %copy.162), channel_id=1, source_target_pairs={{0,4},{4,8},{8,12},{12,16},{16,20},{20,24},{24,28},{1,5},{5,9},{9,... | collective-permute-start | bytes 2088968 | tf_op jit(solution)/shard_map/ppermute | solution.py:19

commit v10 on v6

--- a/solution.py
+++ b/solution.py
@@ -132,11 +132,7 @@
     left = lax.ppermute(high_padded[:, :, WCOL - 1 :], "src", up)
     right = lax.ppermute(high_padded[:, :, :1], "src", [(j, i) for i, j in up])
     own_wide = widen(high_padded, left, right)
-    sent_prev = jnp.concatenate(
-        [high_padded[FR_DEV - 2 :], left[FR_DEV - 2 :], right[FR_DEV - 2 :]], axis=2
-    )
-    prev = passed_along(sent_prev, "frame", 1)
-    prev_wide = widen(prev[:, :, :WCOL], prev[:, :, WCOL : WCOL + 1], prev[:, :, WCOL + 1 :])
+    prev_wide = passed_along(own_wide[FR_DEV - 2 :], "frame", 1)
 
     validity = jnp.stack(
         [(window_ids[a : a + FR_DEV] == own_ids).astype(jnp.int32) for a in range(3)]

time: 177 us -> 189 us (1.068)
  waiting for transfers between devices: 60.4 us -> 73.6 us
  other arithmetic: 27.6 us -> 22.7 us
  local copies, waits for them, and re-layouts: 26.6 us -> 28.9 us
    ppermute x1, waiting for transfers between devices: 0.01 us -> 11.7 us  [passed_along(): return lax.ppermute(x, axis, pairs)]
    unnamed x14 -> x15, local copies, waits for them, and re-layouts: 0.49 us -> 3.94 us
    concatenate x2 -> x1, other arithmetic: 5.53 us -> 2.65 us  [widen(): return jnp.concatenate([shifted_in, block, shifted_out], axis=-1)]
  transfers between devices with their start and end apart: 6 -> 6, of which waited for: 3 -> 5; matrix products, arithmetic and copies ran while one was open for 4% -> 2% of each run, Pallas kernels for 15% -> 14%
where the time goes in v10:
time: 189 us; the launch traced here: 186 us
  waiting for transfers between devices  73.6 us (39%)
  Pallas kernels  33.5 us (18%)
  local copies, waits for them, and re-layouts  28.9 us (15%)
  starting transfers between devices  23.4 us (12%)
  other arithmetic  22.7 us (12%)
  matrix products  3.23 us (2%)
    all_to_all x1, waiting for transfers between devices, shards(): lax.all_to_all(payload, ('src', 'frame', 'tile'), split_axis=0, concat_ax...  52.4 us
    pallas_call x1, Pallas kernels, own_conv(): pl.pallas_call(own_kernel, grid_spec=pltpu.PrefetchScalarGridSpec(num_sca...  26.1 us
    all_to_all x1, starting transfers between devices, shards(): lax.all_to_all(payload, ('src', 'frame', 'tile'), split_axis=0, concat_ax...  12 us
    ppermute x1, waiting for transfers between devices, passed_along(): return lax.ppermute(x, axis, pairs)  11.7 us
    gather x2, local copies, waits for them, and re-layouts, shards(): feats[ordering.reshape(devices, per_pair)]  9.46 us
    pallas_call x1, Pallas kernels, prev_conv(): pl.pallas_call(prev_kernel, grid_spec=pltpu.PrefetchScalarGridSpec(num_sc...  7.43 us
    gather x1, local copies, waits for them, and re-layouts, shards(): arrived.reshape(-1, channels)[gather_rows]  7.19 us
    ppermute x1, waiting for transfers between devices, with_halo(): after = lax.ppermute(leading, axis, down)  5.9 us
  transfers between devices with their start and end apart: 6, of which 5 were waited for; matrix products, arithmetic and copies ran while one was open for 2% of the time, Pallas kernels for 14%

profile of v10, /device:TPU:1, one launch (start us, length us, event | category | flops | bytes accessed | tf_op | source)
XLA Modules:
  0.0 185.7 jit_solution(17157375664001879636)
XLA Ops:
  0.0 0.7 fusion.11
  0.7 1.2 fusion.46
  1.9 3.3 %multiply_reduce_fusion.2 = f32[4,512]{1,0:T(4,128)S(1)} fusion(f32[4,1536]{1,0:T(4,128)S(1)} %bitcast.31, f32[1536,512]{1,0:T(8,128)} %param.7), kind=kLoop, calls=%fused_computation.4 | loop fusion | flops 6289408 | bytes 3178496 | tf_op jit(solution)/shard_map/reduce_sum | solution.py:60
  5.8 1.3 multiply_reduce_fusion.1
  7.1 0.8 subtract_multiply_fusion
  7.9 1.1 multiply_reduce_fusion
  9.3 5.1 %sort.21 = (s32[1536]{0:T(1024)}, s32[1536]{0:T(1024)S(1)}, s32[1536]{0:T(1024)S(1)}) sort(s32[1536]{0:T(1024)S(1)} %get-tuple-element.25, s32[1536]{0:T(1024)S(1)} %get-tuple-element.26, s32[1536]{0:T(1024)S(1)} %iota.32), dimensions={0}, to_apply=%region_0.1 | sort | flops 16896 | bytes 36864 | tf_op jit(solution)/shard_map/sort | solution.py:73
  15.2 5.0 %gather_fusion = f32[1536,512]{1,0:T(8,128)} fusion(f32[1536,512]{1,0:T(8,128)S(1)} %copy-done, s32[2048]{0:T(1024)S(1)} %pad_clamp_fusion.1), kind=kCustom, calls=%fused_computation | custom fusion | bytes 6297600 | tf_op jit(solution)/shard_map/gather | solution.py:85
  20.1 4.5 %reshape.250 = f32[128,12,512]{2,1,0:T(8,128)} reshape(f32[1536,512]{1,0:T(8,128)} %gather_fusion) | data formatting | bytes 6291456 | tf_op jit(solution)/shard_map/gather | solution.py:85
  24.7 5.2 %maximum_maximum_fusion.1 = f32[128,16,512]{2,1,0:T(8,128)} fusion(f32[128,1,512]{2,1,0:T(1,128)S(1)} %broadcast_in_dim.18, f32[128,12,512]{2,1,0:T(8,128)} %reshape.250, f32[16]{0:T(128)S(1)} %pad.15.clone), kind=kLoop, calls=%fused_computation.9 | loop fusion | flops 2097152 | bytes 7602240 | tf_op jit(solution)/shard_map/concatenate | solution.py:83
  29.9 12.0 %all-to-all-start = ((f32[128,16,512]{2,1,0:T(8,128)}), f32[128,16,512]{2,1,0:T(8,128)}, u32[]{:S(2)}, u32[]{:S(2)}) async-start(f32[128,16,512]{2,1,0:T(8,128)} %maximum_maximum_fusion.1), calls=%async_computation | async-start | bytes 8388608 | tf_op jit(solution)/shard_map/all_to_all | solution.py:91
  42.1 52.4 %all-to-all-done = f32[128,16,512]{2,1,0:T(8,128)} async-done(((f32[128,16,512]{2,1,0:T(8,128)}), f32[128,16,512]{2,1,0:T(8,128)}, u32[]{:S(2)}, u32[]{:S(2)}) %all-to-all-start) | async-done | bytes 4194336 | tf_op jit(solution)/shard_map/all_to_all | solution.py:91
  94.5 1.9 slice.77
  98.3 1.7 fusion.2
  100.1 7.2 %gather_fusion.1 = f32[1536,512]{1,0:T(8,128)S(1)} fusion(f32[2048,512]{1,0:T(8,128)} %bitcast.3, s32[2048]{0:T(1024)S(1)} %pad_clamp_fusion), kind=kCustom, calls=%fused_computation.1 | custom fusion | bytes 6297600 | tf_op jit(solution)/shard_map/gather | solution.py:115
  107.3 1.0 multiply_convert_fusion
  108.3 3.6 %collective-permute-start = (bf16[6,1,32,512]{3,2,1,0:T(8,128)(2,1)S(1)}, bf16[6,1,32,512]{3,2,1,0:T(8,128)(2,1)S(1)}, u32[]{:S(2)}, u32[]{:S(2)}) collective-permute-start(bf16[6,1,32,512]{3,2,1,0:T(8,128)(2,1)S(1)} %get-tuple-element.19), channel_id=1, source_target_pairs={{0,1},{1,2},{2,3},{4,5},{5,6},{6,7},{8,9},{9,10},{10,11},{12,13},{... | collective-permute-start | bytes 589832 | tf_op jit(solution)/shard_map/ppermute | solution.py:29
  112.0 1.9 %collective-permute-start.1 = (bf16[6,1,32,512]{3,2,1,0:T(8,128)(2,1)S(1)}, bf16[6,1,32,512]{3,2,1,0:T(8,128)(2,1)S(1)}, u32[]{:S(2)}, u32[]{:S(2)}) collective-permute-start(bf16[6,1,32,512]{3,2,1,0:T(8,128)(2,1)S(1)} %get-tuple-element.20), channel_id=1, source_target_pairs={{1,0},{2,1},{3,2},{5,4},{6,5},{7,6},{9,8},{10,9},{11,10},{13,12},{... | collective-permute-start | bytes 589832 | tf_op jit(solution)/shard_map/ppermute | solution.py:30
  114.6 5.9 %collective-permute-done.1 = bf16[6,1,32,512]{3,2,1,0:T(8,128)(2,1)S(1)} collective-permute-done((bf16[6,1,32,512]{3,2,1,0:T(8,128)(2,1)S(1)}, bf16[6,1,32,512]{3,2,1,0:T(8,128)(2,1)S(1)}, u32[]{:S(2)}, u32[]{:S(2)}) %collective-permute-start.1) | collective-permute-done | bytes 196640 | tf_op jit(solution)/shard_map/ppermute | solution.py:30
  120.7 1.5 collective-permute-start.2
  122.1 1.5 collective-permute-start.3
  123.9 1.3 fusion.43
  125.2 2.9 %collective-permute-done.3 = bf16[6,10,1,512]{3,2,1,0:T(2,128)(2,1)S(1)} collective-permute-done((bf16[6,10,1,512]{3,2,1,0:T(2,128)(2,1)S(1)}, bf16[6,10,1,512]{3,2,1,0:T(2,128)(2,1)S(1)}, u32[]{:S(2)}, u32[]{:S(2)}) %collective-permute-start.3) | collective-permute-done | bytes 61472 | tf_op jit(solution)/shard_map/ppermute | solution.py:133
  128.1 2.6 %maximum_maximum_fusion.x_ref = bf16[6,10,32,1536]{3,2,1,0:T(8,128)(2,1)S(1)} fusion(bf16[6,10,1,512]{3,2,1,0:T(2,128)(2,1)S(1)} %collective-permute-done.3, bf16[6,10,31,512]{3,2,1,0:T(8,128)(2,1)S(1)} %get-tuple-element.18, bf16[6,1,32,512]{3,2,1,0:T(8,128)(2,1)S(1)} %collective-permute-done.1, bf16[6,8,32,512]{3,2,1,0:T(8,128)(2,1)S(1)} %multiply_convert_fusion, ...), kind=kLoop, calls=%fused_computation.7 | loop fusion | flops 41287680 | bytes 11796480 | tf_op jit(solution)/shard_map/concatenate | solution.py:152
  130.8 2.5 %copy-done.1 = bf16[6,10,32,1536]{3,2,1,0:T(8,128)(2,1)} copy-done((bf16[6,10,32,1536]{3,2,1,0:T(8,128)(2,1)}, bf16[6,10,32,1536]{3,2,1,0:T(8,128)(2,1)S(1)}, u32[]{:S(2)}) %copy-start.1) | copy-done | bytes 5898264
  133.3 1.4 slice.88
  134.7 2.9 %collective-permute-start.4 = (bf16[2,10,32,1536]{3,2,1,0:T(8,128)(2,1)}, bf16[2,10,32,1536]{3,2,1,0:T(8,128)(2,1)S(1)}, u32[]{:S(2)}, u32[]{:S(2)}) collective-permute-start(bf16[2,10,32,1536]{3,2,1,0:T(8,128)(2,1)} %slice.88), channel_id=1, source_target_pairs={{0,4},{4,8},{8,12},{12,16},{16,20},{20,24},{24,28},{1,5},{5,9},{9,... | collective-permute-start | bytes 5898248 | tf_op jit(solution)/shard_map/ppermute | solution.py:19
  138.6 0.7 reshape.237.valid_ref
  139.2 26.1 %shard_map.73 = (bf16[6,8,32,512]{3,2,1,0:T(8,128)(2,1)}, f32[2,8,32,512]{3,2,1,0:T(8,128)}) custom-call(s32[18]{0:T(128)} %select_n.118.valid_ref, bf16[6,10,32,1536]{3,2,1,0:T(8,128)(2,1)} %copy-done.1, bf16[9,1536,512]{2,1,0:T(8,128)(2,1)} %bitcast.23, f32[1,512]{1,0:T(1,128)} %bitcast.34, f32[6,8,32,512]{3,2,1,0:T(8,128)} %bitcast.26), custom_call_target="tpu_custom_call" | custom-call | tf_op jit(solution)/shard_map/pallas_call | solution.py:189
  165.3 11.7 %collective-permute-done.4.x_ref = bf16[2,10,32,1536]{3,2,1,0:T(8,128)(2,1)S(1)} collective-permute-done((bf16[2,10,32,1536]{3,2,1,0:T(8,128)(2,1)}, bf16[2,10,32,1536]{3,2,1,0:T(8,128)(2,1)S(1)}, u32[]{:S(2)}, u32[]{:S(2)}) %collective-permute-start.4) | collective-permute-done | bytes 1966112 | tf_op jit(solution)/shard_map/ppermute | solution.py:19
  177.0 1.3 copy-done.3
  178.3 7.4 %shard_map.74 = bf16[6,8,32,512]{3,2,1,0:T(8,128)(2,1)} custom-call(s32[4]{0:T(128)} %reshape.237.valid_ref, bf16[2,10,32,1536]{3,2,1,0:T(8,128)(2,1)} %copy-done.3, bf16[9,1536,512]{2,1,0:T(8,128)(2,1)} %bitcast.24, f32[2,8,32,512]{3,2,1,0:T(8,128)} %get-tuple-element.11.early_ref, ...), custom_call_target="tpu_custom_call", output_to_operand_aliasing={{}: (4, {})} | custom-call | tf_op jit(solution)/shard_map/pallas_call | solution.py:245
  (70 shorter events, 5.7 us)
Async XLA Ops:
  1.9 5.2 %copy-start = (f32[1536,512]{1,0:T(8,128)S(1)}, f32[1536,512]{1,0:T(8,128)}, u32[]{:S(2)}) copy-start(f32[1536,512]{1,0:T(8,128)} %param.7) | copy-start | bytes 9437188
  29.9 12.0 %copy-start.6 = (s32[48]{0:T(128)S(1)}, s32[48]{0:T(128)}, u32[]{:S(2)}) copy-start(s32[48]{0:T(128)} %param.9) | copy-start | bytes 580
  29.9 64.6 %all-to-all-start = ((f32[128,16,512]{2,1,0:T(8,128)}), f32[128,16,512]{2,1,0:T(8,128)}, u32[]{:S(2)}, u32[]{:S(2)}) async-start(f32[128,16,512]{2,1,0:T(8,128)} %maximum_maximum_fusion.1), calls=%async_computation | async-start | bytes 8388608 | tf_op jit(solution)/shard_map/all_to_all | solution.py:91
  100.0 7.2 %copy-start.4 = (f32[512]{0:T(512)S(1)}, f32[512]{0:T(512)}, u32[]{:S(2)}) copy-start(f32[512]{0:T(512)} %param.11) | copy-start | bytes 6148
  100.0 7.2 %copy-start.5 = (f32[512]{0:T(512)S(1)}, f32[512]{0:T(512)}, u32[]{:S(2)}) copy-start(f32[512]{0:T(512)} %param.10) | copy-start | bytes 6148
  107.2 13.4 %copy-start.2 = (f32[1536,512]{1,0:T(8,128)}, f32[1536,512]{1,0:T(8,128)S(1)}, u32[]{:S(2)}) copy-start(f32[1536,512]{1,0:T(8,128)S(1)} %gather_fusion.1) | copy-start | bytes 9437188
  108.3 6.2 %collective-permute-start = (bf16[6,1,32,512]{3,2,1,0:T(8,128)(2,1)S(1)}, bf16[6,1,32,512]{3,2,1,0:T(8,128)(2,1)S(1)}, u32[]{:S(2)}, u32[]{:S(2)}) collective-permute-start(bf16[6,1,32,512]{3,2,1,0:T(8,128)(2,1)S(1)} %get-tuple-element.19), channel_id=1, source_target_pairs={{0,1},{1,2},{2,3},{4,5},{5,6},{6,7},{8,9},{9,10},{10,11},{12,13},{... | collective-permute-start | bytes 589832 | tf_op jit(solution)/shard_map/ppermute | solution.py:29
  112.0 8.5 %collective-permute-start.1 = (bf16[6,1,32,512]{3,2,1,0:T(8,128)(2,1)S(1)}, bf16[6,1,32,512]{3,2,1,0:T(8,128)(2,1)S(1)}, u32[]{:S(2)}, u32[]{:S(2)}) collective-permute-start(bf16[6,1,32,512]{3,2,1,0:T(8,128)(2,1)S(1)} %get-tuple-element.20), channel_id=1, source_target_pairs={{1,0},{2,1},{3,2},{5,4},{6,5},{7,6},{9,8},{10,9},{11,10},{13,12},{... | collective-permute-start | bytes 589832 | tf_op jit(solution)/shard_map/ppermute | solution.py:30
  120.7 4.5 %collective-permute-start.2 = (bf16[6,10,1,512]{3,2,1,0:T(2,128)(2,1)S(1)}, bf16[6,10,1,512]{3,2,1,0:T(2,128)(2,1)S(1)}, u32[]{:S(2)}, u32[]{:S(2)}) collective-permute-start(bf16[6,10,1,512]{3,2,1,0:T(2,128)(2,1)S(1)} %get-tuple-element.15), channel_id=1, source_target_pairs={{0,32},{32,64},{64,96},{1,33},{33,65},{65,97},{2,34},{34,66},{66,9... | collective-permute-start | bytes 184328 | tf_op jit(solution)/shard_map/ppermute | solution.py:132
  122.1 6.0 %collective-permute-start.3 = (bf16[6,10,1,512]{3,2,1,0:T(2,128)(2,1)S(1)}, bf16[6,10,1,512]{3,2,1,0:T(2,128)(2,1)S(1)}, u32[]{:S(2)}, u32[]{:S(2)}) collective-permute-start(bf16[6,10,1,512]{3,2,1,0:T(2,128)(2,1)S(1)} %get-tuple-element.16), channel_id=1, source_target_pairs={{32,0},{64,32},{96,64},{33,1},{65,33},{97,65},{34,2},{66,34},{98,6... | collective-permute-start | bytes 184328 | tf_op jit(solution)/shard_map/ppermute | solution.py:133
  130.8 2.5 %copy-start.1 = (bf16[6,10,32,1536]{3,2,1,0:T(8,128)(2,1)}, bf16[6,10,32,1536]{3,2,1,0:T(8,128)(2,1)S(1)}, u32[]{:S(2)}) copy-start(bf16[6,10,32,1536]{3,2,1,0:T(8,128)(2,1)S(1)} %maximum_maximum_fusion.x_ref) | copy-start | bytes 17694724
  134.7 42.3 %collective-permute-start.4 = (bf16[2,10,32,1536]{3,2,1,0:T(8,128)(2,1)}, bf16[2,10,32,1536]{3,2,1,0:T(8,128)(2,1)S(1)}, u32[]{:S(2)}, u32[]{:S(2)}) collective-permute-start(bf16[2,10,32,1536]{3,2,1,0:T(8,128)(2,1)} %slice.88), channel_id=1, source_target_pairs={{0,4},{4,8},{8,12},{12,16},{16,20},{20,24},{24,28},{1,5},{5,9},{9,... | collective-permute-start | bytes 5898248 | tf_op jit(solution)/shard_map/ppermute | solution.py:19
  177.0 1.3 copy-start.3

commit v11 on v4

--- a/solution.py
+++ b/solution.py
@@ -84,8 +84,10 @@
         [ordering.reshape(devices, per_pair), jnp.zeros((devices, block - per_pair), jnp.int32)],
         axis=1,
     )
-    payload = feats[pick.reshape(-1)].reshape(devices, block, channels)
-    payload = lax.dynamic_update_slice(payload, info[:, None, :], (0, per_pair, 0))
+    is_info = (jnp.arange(block) == per_pair)[None, :, None]
+    payload = jnp.where(
+        is_info, info[:, None, :], feats[pick.reshape(-1)].reshape(devices, block, channels)
+    )
     arrived = lax.all_to_all(
         payload, ("src", "frame", "tile"), split_axis=0, concat_axis=0, tiled=True
     )
@@ -106,7 +108,10 @@
     clip_var = clip_m2 / total_n[:, None]
 
     arrival_row = (iota // per_pair) * block + iota % per_pair
-    _, gather_rows = lax.sort((targets, arrival_row), num_keys=1)
+    digits = jnp.stack([arrival_row // 64, arrival_row % 64], axis=1).astype(jnp.bfloat16)
+    chooser = (targets[None, :] == iota[:, None]).astype(jnp.bfloat16)
+    found = jnp.dot(chooser, digits, preferred_element_type=jnp.float32).astype(jnp.int32)
+    gather_rows = found[:, 0] * 64 + found[:, 1]
     features = arrived.reshape(-1, channels)[gather_rows].reshape(FR_DEV, HR, WCOL, channels)
 
     first_frame = lax.axis_index("frame") * FR_DEV

time: 181 us -> 176 us (0.972)
  local copies, waits for them, and re-layouts: 32.4 us -> 25.8 us
    dynamic_update_slice x1 -> x0, local copies, waits for them, and re-layouts: 6.35 us -> none  [shards(): lax.dynamic_update_slice(payload, info[:, None, :], (0, per_pair, 0))]
    select_n x1 -> x2, other arithmetic: 0.01 us -> 5.25 us  [the longest x1 5.23 us: shards(): jnp.where(is_info, info[:, None, :], feats[pick.reshape(-1)].reshape(devi...]
    sort x1 -> x0, other arithmetic: 5.12 us -> none  [shards(): _, gather_rows = lax.sort((targets, arrival_row), num_keys=1)]
where the time goes in v11:
time: 176 us; the launch traced here: 174 us
  waiting for transfers between devices  60.4 us (34%)
  Pallas kernels  33.5 us (19%)
  other arithmetic  27.6 us (16%)
  local copies, waits for them, and re-layouts  25.8 us (15%)
  starting transfers between devices  23.3 us (13%)
  matrix products  3.23 us (2%)
    all_to_all x1, waiting for transfers between devices, shards(): lax.all_to_all(payload, ('src', 'frame', 'tile'), split_axis=0, concat_ax...  52.2 us
    pallas_call x1, Pallas kernels, own_conv(): pl.pallas_call(own_kernel, grid_spec=pltpu.PrefetchScalarGridSpec(num_sca...  26.1 us
    all_to_all x1, starting transfers between devices, shards(): lax.all_to_all(payload, ('src', 'frame', 'tile'), split_axis=0, concat_ax...  12 us
    gather x1, local copies, waits for them, and re-layouts, shards(): feats[pick.reshape(-1)].reshape(devices, block, channels)  8.91 us
    gather x1, local copies, waits for them, and re-layouts, shards(): arrived.reshape(-1, channels)[gather_rows]  7.93 us
    pallas_call x1, Pallas kernels, prev_conv(): pl.pallas_call(prev_kernel, grid_spec=pltpu.PrefetchScalarGridSpec(num_sc...  7.43 us
    concatenate x2, other arithmetic, widen(): return jnp.concatenate([shifted_in, block, shifted_out], axis=-1)  5.53 us
    ppermute x1, waiting for transfers between devices, with_halo(): after = lax.ppermute(leading, axis, down)  5.32 us
  transfers between devices with their start and end apart: 6, of which 3 were waited for; matrix products, arithmetic and copies ran while one was open for 4% of the time, Pallas kernels for 15%

profile of v11, /device:TPU:1, one launch (start us, length us, event | category | flops | bytes accessed | tf_op | source)
XLA Modules:
  0.0 174.3 jit_solution(1694093252626563138)
XLA Ops:
  0.0 0.7 fusion.11
  0.7 1.2 fusion.48
  1.9 3.3 %multiply_reduce_fusion.2 = f32[4,512]{1,0:T(4,128)S(1)} fusion(f32[4,1536]{1,0:T(4,128)S(1)} %bitcast.32, f32[1536,512]{1,0:T(8,128)} %param.7), kind=kLoop, calls=%fused_computation.4 | loop fusion | flops 6289408 | bytes 3178496 | tf_op jit(solution)/shard_map/reduce_sum | solution.py:60
  5.8 1.3 multiply_reduce_fusion.1
  7.1 0.8 subtract_multiply_fusion
  7.9 1.1 multiply_reduce_fusion
  9.3 5.1 %sort.21 = (s32[1536]{0:T(1024)}, s32[1536]{0:T(1024)S(1)}, s32[1536]{0:T(1024)S(1)}) sort(s32[1536]{0:T(1024)S(1)} %get-tuple-element.29, s32[1536]{0:T(1024)S(1)} %get-tuple-element.30, s32[1536]{0:T(1024)S(1)} %iota.38), dimensions={0}, to_apply=%region_0.1 | sort | flops 16896 | bytes 36864 | tf_op jit(solution)/shard_map/sort | solution.py:73
  14.8 8.9 %gather_fusion = f32[2048,512]{1,0:T(8,128)} fusion(f32[1536,512]{1,0:T(8,128)S(1)} %copy-done, s32[2048]{0:T(1024)S(1)} %broadcast_clamp_fusion), kind=kCustom, calls=%fused_computation | custom fusion | bytes 8396800 | tf_op jit(solution)/shard_map/gather | solution.py:89
  23.9 5.2 %broadcast_select_fusion = f32[128,16,512]{2,1,0:T(8,128)} fusion(f32[128,16,512]{2,1,0:T(8,128)} %bitcast.27, f32[128,512]{1,0:T(8,128)S(1)} %maximum_maximum_fusion.2, pred[16]{0:T(512)(128)(4,1)S(1)} %iota_compare_fusion.11), kind=kLoop, calls=%fused_computation.12 | loop fusion | flops 1048576 | bytes 8650768 | tf_op jit(solution)/shard_map/jit(_where)/select_n | solution.py:88
  29.1 12.0 %all-to-all-start = ((f32[128,16,512]{2,1,0:T(8,128)}), f32[128,16,512]{2,1,0:T(8,128)}, u32[]{:S(2)}, u32[]{:S(2)}) async-start(f32[128,16,512]{2,1,0:T(8,128)} %broadcast_select_fusion), calls=%async_computation | async-start | bytes 8388608 | tf_op jit(solution)/shard_map/all_to_all | solution.py:91
  41.5 52.2 %all-to-all-done = f32[128,16,512]{2,1,0:T(8,128)} async-done(((f32[128,16,512]{2,1,0:T(8,128)}), f32[128,16,512]{2,1,0:T(8,128)}, u32[]{:S(2)}, u32[]{:S(2)}) %all-to-all-start) | async-done | bytes 4194336 | tf_op jit(solution)/shard_map/all_to_all | solution.py:91
  93.7 1.9 %slice.107 = f32[128,1,512]{2,1,0:T(1,128)S(1)} slice(f32[128,16,512]{2,1,0:T(8,128)} %all-to-all-done), slice={[0:128], [12:13], [0:512]} | slice | bytes 524288 | tf_op jit(solution)/shard_map/slice | solution.py:95
  97.5 1.7 fusion.2
  99.3 7.9 %gather_fusion.1 = f32[1536,512]{1,0:T(8,128)} fusion(f32[2048,512]{1,0:T(8,128)} %bitcast.5, s32[2048]{0:T(1024)S(1)} %pad_clamp_fusion), kind=kCustom, calls=%fused_computation.1 | custom fusion | bytes 6297600 | tf_op jit(solution)/shard_map/gather | solution.py:115
  107.2 2.9 %multiply_convert_fusion = bf16[6,8,32,512]{3,2,1,0:T(8,128)(2,1)S(1)} fusion(f32[6,8,32,512]{3,2,1,0:T(8,128)} %bitcast.25, f32[512]{0:T(512)S(1)} %copy-done.1, f32[512]{0:T(512)S(1)} %copy-done.2, f32[6,512]{1,0:T(8,128)S(1)} %mul.141, f32[6,512]{1,0:T(8,128)S(1)} %sub.56), kind=kLoop, calls=%fused_computation.9 | loop fusion | flops 7077888 | bytes 4747264 | tf_op jit(solution)/shard_map/convert_element_type | solution.py:128
  110.1 3.6 %collective-permute-start = (bf16[6,1,32,512]{3,2,1,0:T(8,128)(2,1)S(1)}, bf16[6,1,32,512]{3,2,1,0:T(8,128)(2,1)S(1)}, u32[]{:S(2)}, u32[]{:S(2)}) collective-permute-start(bf16[6,1,32,512]{3,2,1,0:T(8,128)(2,1)S(1)} %get-tuple-element.19), channel_id=1, source_target_pairs={{0,1},{1,2},{2,3},{4,5},{5,6},{6,7},{8,9},{9,10},{10,11},{12,13},{... | collective-permute-start | bytes 589832 | tf_op jit(solution)/shard_map/ppermute | solution.py:29
  113.8 1.9 %collective-permute-start.1 = (bf16[6,1,32,512]{3,2,1,0:T(8,128)(2,1)S(1)}, bf16[6,1,32,512]{3,2,1,0:T(8,128)(2,1)S(1)}, u32[]{:S(2)}, u32[]{:S(2)}) collective-permute-start(bf16[6,1,32,512]{3,2,1,0:T(8,128)(2,1)S(1)} %get-tuple-element.20), channel_id=1, source_target_pairs={{1,0},{2,1},{3,2},{5,4},{6,5},{7,6},{9,8},{10,9},{11,10},{13,12},{... | collective-permute-start | bytes 589832 | tf_op jit(solution)/shard_map/ppermute | solution.py:30
  115.8 0.6 select_n.123.valid_ref
  116.4 0.6 reshape.248.valid_ref
  116.9 5.3 %collective-permute-done.1 = bf16[6,1,32,512]{3,2,1,0:T(8,128)(2,1)S(1)} collective-permute-done((bf16[6,1,32,512]{3,2,1,0:T(8,128)(2,1)S(1)}, bf16[6,1,32,512]{3,2,1,0:T(8,128)(2,1)S(1)}, u32[]{:S(2)}, u32[]{:S(2)}) %collective-permute-start.1) | collective-permute-done | bytes 196640 | tf_op jit(solution)/shard_map/ppermute | solution.py:30
  122.5 1.5 collective-permute-start.2
  123.9 1.5 collective-permute-start.3
  125.7 1.3 fusion.43
  127.1 2.8 %collective-permute-done.3 = bf16[6,10,1,512]{3,2,1,0:T(2,128)(2,1)S(1)} collective-permute-done((bf16[6,10,1,512]{3,2,1,0:T(2,128)(2,1)S(1)}, bf16[6,10,1,512]{3,2,1,0:T(2,128)(2,1)S(1)}, u32[]{:S(2)}, u32[]{:S(2)}) %collective-permute-start.3) | collective-permute-done | bytes 61472 | tf_op jit(solution)/shard_map/ppermute | solution.py:133
  130.1 0.7 copy.23
  130.8 2.9 %collective-permute-start.4 = (bf16[2,10,34,512]{3,0,2,1:T(2,128)(2,1)S(1)}, bf16[2,10,34,512]{3,0,2,1:T(2,128)(2,1)S(1)}, u32[]{:S(2)}, u32[]{:S(2)}) collective-permute-start(bf16[2,10,34,512]{3,0,2,1:T(2,128)(2,1)S(1)} %copy.23), channel_id=1, source_target_pairs={{0,4},{4,8},{8,12},{12,16},{16,20},{20,24},{24,28},{1,5},{5,9},{9,... | collective-permute-start | bytes 2088968 | tf_op jit(solution)/shard_map/ppermute | solution.py:19
  133.7 3.8 %maximum_maximum_fusion.x_ref = bf16[6,10,32,1536]{3,2,1,0:T(8,128)(2,1)} fusion(bf16[6,10,1,512]{3,2,1,0:T(2,128)(2,1)S(1)} %collective-permute-done.3, bf16[6,10,31,512]{3,2,1,0:T(8,128)(2,1)S(1)} %get-tuple-element.16, bf16[6,1,32,512]{3,2,1,0:T(8,128)(2,1)S(1)} %collective-permute-done.1, bf16[6,8,32,512]{3,2,1,0:T(8,128)(2,1)S(1)} %multiply_convert_fusion, ...), kind=kLoop, calls=%fused_computation.7 | loop fusion | flops 41287680 | bytes 11796480 | tf_op jit(solution)/shard_map/concatenate | solution.py:156
  137.5 26.1 %shard_map.73 = (bf16[6,8,32,512]{3,2,1,0:T(8,128)(2,1)}, f32[2,8,32,512]{3,2,1,0:T(8,128)}) custom-call(s32[18]{0:T(128)} %select_n.123.valid_ref, bf16[6,10,32,1536]{3,2,1,0:T(8,128)(2,1)} %maximum_maximum_fusion.x_ref, bf16[9,1536,512]{2,1,0:T(8,128)(2,1)} %bitcast.23, f32[1,512]{1,0:T(1,128)} %bitcast.36, f32[6,8,32,512]{3,2,1,0:T(8,128)} %bitcast.26), custom_call_target="tpu_custom_call" | custom-call | tf_op jit(solution)/shard_map/pallas_call | solution.py:193
  163.6 0.7 fusion.46
  164.5 0.5 slice.121
  165.2 1.7 maximum_maximum_fusion.1.x_ref
  166.9 7.4 %shard_map.74 = bf16[6,8,32,512]{3,2,1,0:T(8,128)(2,1)} custom-call(s32[4]{0:T(128)} %reshape.248.valid_ref, bf16[2,10,32,1536]{3,2,1,0:T(8,128)(2,1)} %maximum_maximum_fusion.1.x_ref, bf16[9,1536,512]{2,1,0:T(8,128)(2,1)} %bitcast.24, f32[2,8,32,512]{3,2,1,0:T(8,128)} %get-tuple-element.11.early_ref, ...), custom_call_target="tpu_custom_call", output_to_operand_aliasing={{}: (4, {})} | custom-call | tf_op jit(solution)/shard_map/pallas_call | solution.py:249
  (75 shorter events, 4.8 us)
Async XLA Ops:
  1.9 5.2 %copy-start = (f32[1536,512]{1,0:T(8,128)S(1)}, f32[1536,512]{1,0:T(8,128)}, u32[]{:S(2)}) copy-start(f32[1536,512]{1,0:T(8,128)} %param.7) | copy-start | bytes 9437188
  29.1 12.0 %copy-start.3 = (s32[48]{0:T(128)S(1)}, s32[48]{0:T(128)}, u32[]{:S(2)}) copy-start(s32[48]{0:T(128)} %param.9) | copy-start | bytes 580
  29.1 64.6 %all-to-all-start = ((f32[128,16,512]{2,1,0:T(8,128)}), f32[128,16,512]{2,1,0:T(8,128)}, u32[]{:S(2)}, u32[]{:S(2)}) async-start(f32[128,16,512]{2,1,0:T(8,128)} %broadcast_select_fusion), calls=%async_computation | async-start | bytes 8388608 | tf_op jit(solution)/shard_map/all_to_all | solution.py:91
  99.2 8.0 %copy-start.1 = (f32[512]{0:T(512)S(1)}, f32[512]{0:T(512)}, u32[]{:S(2)}) copy-start(f32[512]{0:T(512)} %param.11) | copy-start | bytes 6148
  99.3 7.9 %copy-start.2 = (f32[512]{0:T(512)S(1)}, f32[512]{0:T(512)}, u32[]{:S(2)}) copy-start(f32[512]{0:T(512)} %param.10) | copy-start | bytes 6148
  110.1 6.8 %collective-permute-start = (bf16[6,1,32,512]{3,2,1,0:T(8,128)(2,1)S(1)}, bf16[6,1,32,512]{3,2,1,0:T(8,128)(2,1)S(1)}, u32[]{:S(2)}, u32[]{:S(2)}) collective-permute-start(bf16[6,1,32,512]{3,2,1,0:T(8,128)(2,1)S(1)} %get-tuple-element.19), channel_id=1, source_target_pairs={{0,1},{1,2},{2,3},{4,5},{5,6},{6,7},{8,9},{9,10},{10,11},{12,13},{... | collective-permute-start | bytes 589832 | tf_op jit(solution)/shard_map/ppermute | solution.py:29
  113.8 8.5 %collective-permute-start.1 = (bf16[6,1,32,512]{3,2,1,0:T(8,128)(2,1)S(1)}, bf16[6,1,32,512]{3,2,1,0:T(8,128)(2,1)S(1)}, u32[]{:S(2)}, u32[]{:S(2)}) collective-permute-start(bf16[6,1,32,512]{3,2,1,0:T(8,128)(2,1)S(1)} %get-tuple-element.20), channel_id=1, source_target_pairs={{1,0},{2,1},{3,2},{5,4},{6,5},{7,6},{9,8},{10,9},{11,10},{13,12},{... | collective-permute-start | bytes 589832 | tf_op jit(solution)/shard_map/ppermute | solution.py:30
  122.5 4.5 %collective-permute-start.2 = (bf16[6,10,1,512]{3,2,1,0:T(2,128)(2,1)S(1)}, bf16[6,10,1,512]{3,2,1,0:T(2,128)(2,1)S(1)}, u32[]{:S(2)}, u32[]{:S(2)}) collective-permute-start(bf16[6,10,1,512]{3,2,1,0:T(2,128)(2,1)S(1)} %get-tuple-element.17), channel_id=1, source_target_pairs={{0,32},{32,64},{64,96},{1,33},{33,65},{65,97},{2,34},{34,66},{66,9... | collective-permute-start | bytes 184328 | tf_op jit(solution)/shard_map/ppermute | solution.py:132
  123.9 6.0 %collective-permute-start.3 = (bf16[6,10,1,512]{3,2,1,0:T(2,128)(2,1)S(1)}, bf16[6,10,1,512]{3,2,1,0:T(2,128)(2,1)S(1)}, u32[]{:S(2)}, u32[]{:S(2)}) collective-permute-start(bf16[6,10,1,512]{3,2,1,0:T(2,128)(2,1)S(1)} %get-tuple-element.18), channel_id=1, source_target_pairs={{32,0},{64,32},{96,64},{33,1},{65,33},{97,65},{34,2},{66,34},{98,6... | collective-permute-start | bytes 184328 | tf_op jit(solution)/shard_map/ppermute | solution.py:133
  130.8 32.8 %collective-permute-start.4 = (bf16[2,10,34,512]{3,0,2,1:T(2,128)(2,1)S(1)}, bf16[2,10,34,512]{3,0,2,1:T(2,128)(2,1)S(1)}, u32[]{:S(2)}, u32[]{:S(2)}) collective-permute-start(bf16[2,10,34,512]{3,0,2,1:T(2,128)(2,1)S(1)} %copy.23), channel_id=1, source_target_pairs={{0,4},{4,8},{8,12},{12,16},{16,20},{20,24},{24,28},{1,5},{5,9},{9,... | collective-permute-start | bytes 2088968 | tf_op jit(solution)/shard_map/ppermute | solution.py:19

commit v12 on v11

--- a/solution.py
+++ b/solution.py
@@ -230,13 +230,16 @@
     def _():
         acc_ref[...] = jnp.zeros_like(acc_ref)
 
-    for t in range(2):
-
-        @pl.when(valid_ref[tap_time * 2 + t] != 0)
+    for a in range(2):
+
+        @pl.when(tap_time == a)
         def _():
-            frame = jnp.minimum(tap_time + t, 1)
-            lhs = x_ref[frame, pl.ds(tap_high, HR)].reshape(HR * WCOL, -1)
-            acc_ref[t] += jnp.dot(lhs, w_ref[0], preferred_element_type=jnp.float32)
+            reach = 2 - a
+            lhs = x_ref[a : a + reach, pl.ds(tap_high, HR)].reshape(reach * HR * WCOL, -1)
+            part = jnp.dot(lhs, w_ref[0], preferred_element_type=jnp.float32)
+            for t in range(reach):
+                keep = valid_ref[a * 2 + t].astype(jnp.float32)
+                acc_ref[t] += part[t * HR * WCOL : (t + 1) * HR * WCOL] * keep
 
     @pl.when((tap_time == 1) & (tap_high == 2))
     def _():

time: 176 us -> 178 us (1.011)
  Pallas kernels: 33.5 us -> 36.2 us
    pallas_call x1, Pallas kernels: 7.43 us -> 10.1 us  [prev_conv(): pl.pallas_call(prev_kernel, grid_spec=pltpu.PrefetchScalarGridSpec(num_sc...]
where the time goes in v12:
time: 178 us; the launch traced here: 177 us
  waiting for transfers between devices  60.4 us (34%)
  Pallas kernels  36.2 us (20%)
  other arithmetic  27.6 us (16%)
  local copies, waits for them, and re-layouts  25.8 us (14%)
  starting transfers between devices  23.3 us (13%)
  matrix products  3.23 us (2%)
    all_to_all x1, waiting for transfers between devices, shards(): lax.all_to_all(payload, ('src', 'frame', 'tile'), split_axis=0, concat_ax...  52.2 us
    pallas_call x1, Pallas kernels, own_conv(): pl.pallas_call(own_kernel, grid_spec=pltpu.PrefetchScalarGridSpec(num_sca...  26.1 us
    all_to_all x1, starting transfers between devices, shards(): lax.all_to_all(payload, ('src', 'frame', 'tile'), split_axis=0, concat_ax...  12 us
    pallas_call x1, Pallas kernels, prev_conv(): pl.pallas_call(prev_kernel, grid_spec=pltpu.PrefetchScalarGridSpec(num_sc...  10.1 us
    gather x1, local copies, waits for them, and re-layouts, shards(): feats[pick.reshape(-1)].reshape(devices, block, channels)  8.91 us
    gather x1, local copies, waits for them, and re-layouts, shards(): arrived.reshape(-1, channels)[gather_rows]  7.93 us
    concatenate x2, other arithmetic, widen(): return jnp.concatenate([shifted_in, block, shifted_out], axis=-1)  5.53 us
    ppermute x1, waiting for transfers between devices, with_halo(): after = lax.ppermute(leading, axis, down)  5.32 us
  transfers between devices with their start and end apart: 6, of which 3 were waited for; matrix products, arithmetic and copies ran while one was open for 4% of the time, Pallas kernels for 15%

profile of v12, /device:TPU:1, one launch (start us, length us, event | category | flops | bytes accessed | tf_op | source)
XLA Modules:
  0.0 177.1 jit_solution(12962062337752273188)
XLA Ops:
  0.0 0.7 fusion.11
  0.7 1.2 fusion.48
  1.9 3.3 %multiply_reduce_fusion.2 = f32[4,512]{1,0:T(4,128)S(1)} fusion(f32[4,1536]{1,0:T(4,128)S(1)} %bitcast.32, f32[1536,512]{1,0:T(8,128)} %param.7), kind=kLoop, calls=%fused_computation.4 | loop fusion | flops 6289408 | bytes 3178496 | tf_op jit(solution)/shard_map/reduce_sum | solution.py:60
  5.8 1.3 multiply_reduce_fusion.1
  7.1 0.8 subtract_multiply_fusion
  7.9 1.1 multiply_reduce_fusion
  9.3 5.1 %sort.21 = (s32[1536]{0:T(1024)}, s32[1536]{0:T(1024)S(1)}, s32[1536]{0:T(1024)S(1)}) sort(s32[1536]{0:T(1024)S(1)} %get-tuple-element.29, s32[1536]{0:T(1024)S(1)} %get-tuple-element.30, s32[1536]{0:T(1024)S(1)} %iota.38), dimensions={0}, to_apply=%region_0.1 | sort | flops 16896 | bytes 36864 | tf_op jit(solution)/shard_map/sort | solution.py:73
  14.8 8.9 %gather_fusion = f32[2048,512]{1,0:T(8,128)} fusion(f32[1536,512]{1,0:T(8,128)S(1)} %copy-done, s32[2048]{0:T(1024)S(1)} %broadcast_clamp_fusion), kind=kCustom, calls=%fused_computation | custom fusion | bytes 8396800 | tf_op jit(solution)/shard_map/gather | solution.py:89
  23.9 5.2 %broadcast_select_fusion = f32[128,16,512]{2,1,0:T(8,128)} fusion(f32[128,16,512]{2,1,0:T(8,128)} %bitcast.27, f32[128,512]{1,0:T(8,128)S(1)} %maximum_maximum_fusion.2, pred[16]{0:T(512)(128)(4,1)S(1)} %iota_compare_fusion.11), kind=kLoop, calls=%fused_computation.12 | loop fusion | flops 1048576 | bytes 8650768 | tf_op jit(solution)/shard_map/jit(_where)/select_n | solution.py:88
  29.1 12.0 %all-to-all-start = ((f32[128,16,512]{2,1,0:T(8,128)}), f32[128,16,512]{2,1,0:T(8,128)}, u32[]{:S(2)}, u32[]{:S(2)}) async-start(f32[128,16,512]{2,1,0:T(8,128)} %broadcast_select_fusion), calls=%async_computation | async-start | bytes 8388608 | tf_op jit(solution)/shard_map/all_to_all | solution.py:91
  41.5 52.2 %all-to-all-done = f32[128,16,512]{2,1,0:T(8,128)} async-done(((f32[128,16,512]{2,1,0:T(8,128)}), f32[128,16,512]{2,1,0:T(8,128)}, u32[]{:S(2)}, u32[]{:S(2)}) %all-to-all-start) | async-done | bytes 4194336 | tf_op jit(solution)/shard_map/all_to_all | solution.py:91
  93.7 1.9 %slice.107 = f32[128,1,512]{2,1,0:T(1,128)S(1)} slice(f32[128,16,512]{2,1,0:T(8,128)} %all-to-all-done), slice={[0:128], [12:13], [0:512]} | slice | bytes 524288 | tf_op jit(solution)/shard_map/slice | solution.py:95
  97.5 1.7 fusion.2
  99.3 7.9 %gather_fusion.1 = f32[1536,512]{1,0:T(8,128)} fusion(f32[2048,512]{1,0:T(8,128)} %bitcast.5, s32[2048]{0:T(1024)S(1)} %pad_clamp_fusion), kind=kCustom, calls=%fused_computation.1 | custom fusion | bytes 6297600 | tf_op jit(solution)/shard_map/gather | solution.py:115
  107.2 2.9 %multiply_convert_fusion = bf16[6,8,32,512]{3,2,1,0:T(8,128)(2,1)S(1)} fusion(f32[6,8,32,512]{3,2,1,0:T(8,128)} %bitcast.25, f32[512]{0:T(512)S(1)} %copy-done.1, f32[512]{0:T(512)S(1)} %copy-done.2, f32[6,512]{1,0:T(8,128)S(1)} %mul.141, f32[6,512]{1,0:T(8,128)S(1)} %sub.56), kind=kLoop, calls=%fused_computation.9 | loop fusion | flops 7077888 | bytes 4747264 | tf_op jit(solution)/shard_map/convert_element_type | solution.py:128
  110.1 3.6 %collective-permute-start = (bf16[6,1,32,512]{3,2,1,0:T(8,128)(2,1)S(1)}, bf16[6,1,32,512]{3,2,1,0:T(8,128)(2,1)S(1)}, u32[]{:S(2)}, u32[]{:S(2)}) collective-permute-start(bf16[6,1,32,512]{3,2,1,0:T(8,128)(2,1)S(1)} %get-tuple-element.19), channel_id=1, source_target_pairs={{0,1},{1,2},{2,3},{4,5},{5,6},{6,7},{8,9},{9,10},{10,11},{12,13},{... | collective-permute-start | bytes 589832 | tf_op jit(solution)/shard_map/ppermute | solution.py:29
  113.8 1.9 %collective-permute-start.1 = (bf16[6,1,32,512]{3,2,1,0:T(8,128)(2,1)S(1)}, bf16[6,1,32,512]{3,2,1,0:T(8,128)(2,1)S(1)}, u32[]{:S(2)}, u32[]{:S(2)}) collective-permute-start(bf16[6,1,32,512]{3,2,1,0:T(8,128)(2,1)S(1)} %get-tuple-element.20), channel_id=1, source_target_pairs={{1,0},{2,1},{3,2},{5,4},{6,5},{7,6},{9,8},{10,9},{11,10},{13,12},{... | collective-permute-start | bytes 589832 | tf_op jit(solution)/shard_map/ppermute | solution.py:30
  115.8 0.6 select_n.123.valid_ref
  116.4 0.6 reshape.248.valid_ref
  116.9 5.3 %collective-permute-done.1 = bf16[6,1,32,512]{3,2,1,0:T(8,128)(2,1)S(1)} collective-permute-done((bf16[6,1,32,512]{3,2,1,0:T(8,128)(2,1)S(1)}, bf16[6,1,32,512]{3,2,1,0:T(8,128)(2,1)S(1)}, u32[]{:S(2)}, u32[]{:S(2)}) %collective-permute-start.1) | collective-permute-done | bytes 196640 | tf_op jit(solution)/shard_map/ppermute | solution.py:30
  122.5 1.5 collective-permute-start.2
  123.9 1.5 collective-permute-start.3
  125.7 1.3 fusion.43
  127.1 2.8 %collective-permute-done.3 = bf16[6,10,1,512]{3,2,1,0:T(2,128)(2,1)S(1)} collective-permute-done((bf16[6,10,1,512]{3,2,1,0:T(2,128)(2,1)S(1)}, bf16[6,10,1,512]{3,2,1,0:T(2,128)(2,1)S(1)}, u32[]{:S(2)}, u32[]{:S(2)}) %collective-permute-start.3) | collective-permute-done | bytes 61472 | tf_op jit(solution)/shard_map/ppermute | solution.py:133
  130.1 0.7 copy.23
  130.8 2.9 %collective-permute-start.4 = (bf16[2,10,34,512]{3,0,2,1:T(2,128)(2,1)S(1)}, bf16[2,10,34,512]{3,0,2,1:T(2,128)(2,1)S(1)}, u32[]{:S(2)}, u32[]{:S(2)}) collective-permute-start(bf16[2,10,34,512]{3,0,2,1:T(2,128)(2,1)S(1)} %copy.23), channel_id=1, source_target_pairs={{0,4},{4,8},{8,12},{12,16},{16,20},{20,24},{24,28},{1,5},{5,9},{9,... | collective-permute-start | bytes 2088968 | tf_op jit(solution)/shard_map/ppermute | solution.py:19
  133.7 3.8 %maximum_maximum_fusion.x_ref = bf16[6,10,32,1536]{3,2,1,0:T(8,128)(2,1)} fusion(bf16[6,10,1,512]{3,2,1,0:T(2,128)(2,1)S(1)} %collective-permute-done.3, bf16[6,10,31,512]{3,2,1,0:T(8,128)(2,1)S(1)} %get-tuple-element.16, bf16[6,1,32,512]{3,2,1,0:T(8,128)(2,1)S(1)} %collective-permute-done.1, bf16[6,8,32,512]{3,2,1,0:T(8,128)(2,1)S(1)} %multiply_convert_fusion, ...), kind=kLoop, calls=%fused_computation.7 | loop fusion | flops 41287680 | bytes 11796480 | tf_op jit(solution)/shard_map/concatenate | solution.py:156
  137.5 26.1 %shard_map.73 = (bf16[6,8,32,512]{3,2,1,0:T(8,128)(2,1)}, f32[2,8,32,512]{3,2,1,0:T(8,128)}) custom-call(s32[18]{0:T(128)} %select_n.123.valid_ref, bf16[6,10,32,1536]{3,2,1,0:T(8,128)(2,1)} %maximum_maximum_fusion.x_ref, bf16[9,1536,512]{2,1,0:T(8,128)(2,1)} %bitcast.23, f32[1,512]{1,0:T(1,128)} %bitcast.36, f32[6,8,32,512]{3,2,1,0:T(8,128)} %bitcast.26), custom_call_target="tpu_custom_call" | custom-call | tf_op jit(solution)/shard_map/pallas_call | solution.py:193
  163.6 0.7 fusion.46
  164.5 0.5 slice.121
  165.2 1.7 maximum_maximum_fusion.1.x_ref
  166.9 10.1 %shard_map.74 = bf16[6,8,32,512]{3,2,1,0:T(8,128)(2,1)} custom-call(s32[4]{0:T(128)} %reshape.248.valid_ref, bf16[2,10,32,1536]{3,2,1,0:T(8,128)(2,1)} %maximum_maximum_fusion.1.x_ref, bf16[9,1536,512]{2,1,0:T(8,128)(2,1)} %bitcast.24, f32[2,8,32,512]{3,2,1,0:T(8,128)} %get-tuple-element.11.early_ref, ...), custom_call_target="tpu_custom_call", output_to_operand_aliasing={{}: (4, {})} | custom-call | tf_op jit(solution)/shard_map/pallas_call | solution.py:252
  (75 shorter events, 4.8 us)
Async XLA Ops:
  1.9 5.2 %copy-start = (f32[1536,512]{1,0:T(8,128)S(1)}, f32[1536,512]{1,0:T(8,128)}, u32[]{:S(2)}) copy-start(f32[1536,512]{1,0:T(8,128)} %param.7) | copy-start | bytes 9437188
  29.1 12.0 %copy-start.3 = (s32[48]{0:T(128)S(1)}, s32[48]{0:T(128)}, u32[]{:S(2)}) copy-start(s32[48]{0:T(128)} %param.9) | copy-start | bytes 580
  29.1 64.6 %all-to-all-start = ((f32[128,16,512]{2,1,0:T(8,128)}), f32[128,16,512]{2,1,0:T(8,128)}, u32[]{:S(2)}, u32[]{:S(2)}) async-start(f32[128,16,512]{2,1,0:T(8,128)} %broadcast_select_fusion), calls=%async_computation | async-start | bytes 8388608 | tf_op jit(solution)/shard_map/all_to_all | solution.py:91
  99.2 8.0 %copy-start.1 = (f32[512]{0:T(512)S(1)}, f32[512]{0:T(512)}, u32[]{:S(2)}) copy-start(f32[512]{0:T(512)} %param.11) | copy-start | bytes 6148
  99.3 7.9 %copy-start.2 = (f32[512]{0:T(512)S(1)}, f32[512]{0:T(512)}, u32[]{:S(2)}) copy-start(f32[512]{0:T(512)} %param.10) | copy-start | bytes 6148
  110.1 6.8 %collective-permute-start = (bf16[6,1,32,512]{3,2,1,0:T(8,128)(2,1)S(1)}, bf16[6,1,32,512]{3,2,1,0:T(8,128)(2,1)S(1)}, u32[]{:S(2)}, u32[]{:S(2)}) collective-permute-start(bf16[6,1,32,512]{3,2,1,0:T(8,128)(2,1)S(1)} %get-tuple-element.19), channel_id=1, source_target_pairs={{0,1},{1,2},{2,3},{4,5},{5,6},{6,7},{8,9},{9,10},{10,11},{12,13},{... | collective-permute-start | bytes 589832 | tf_op jit(solution)/shard_map/ppermute | solution.py:29
  113.8 8.5 %collective-permute-start.1 = (bf16[6,1,32,512]{3,2,1,0:T(8,128)(2,1)S(1)}, bf16[6,1,32,512]{3,2,1,0:T(8,128)(2,1)S(1)}, u32[]{:S(2)}, u32[]{:S(2)}) collective-permute-start(bf16[6,1,32,512]{3,2,1,0:T(8,128)(2,1)S(1)} %get-tuple-element.20), channel_id=1, source_target_pairs={{1,0},{2,1},{3,2},{5,4},{6,5},{7,6},{9,8},{10,9},{11,10},{13,12},{... | collective-permute-start | bytes 589832 | tf_op jit(solution)/shard_map/ppermute | solution.py:30
  122.5 4.5 %collective-permute-start.2 = (bf16[6,10,1,512]{3,2,1,0:T(2,128)(2,1)S(1)}, bf16[6,10,1,512]{3,2,1,0:T(2,128)(2,1)S(1)}, u32[]{:S(2)}, u32[]{:S(2)}) collective-permute-start(bf16[6,10,1,512]{3,2,1,0:T(2,128)(2,1)S(1)} %get-tuple-element.17), channel_id=1, source_target_pairs={{0,32},{32,64},{64,96},{1,33},{33,65},{65,97},{2,34},{34,66},{66,9... | collective-permute-start | bytes 184328 | tf_op jit(solution)/shard_map/ppermute | solution.py:132
  123.9 6.0 %collective-permute-start.3 = (bf16[6,10,1,512]{3,2,1,0:T(2,128)(2,1)S(1)}, bf16[6,10,1,512]{3,2,1,0:T(2,128)(2,1)S(1)}, u32[]{:S(2)}, u32[]{:S(2)}) collective-permute-start(bf16[6,10,1,512]{3,2,1,0:T(2,128)(2,1)S(1)} %get-tuple-element.18), channel_id=1, source_target_pairs={{32,0},{64,32},{96,64},{33,1},{65,33},{97,65},{34,2},{66,34},{98,6... | collective-permute-start | bytes 184328 | tf_op jit(solution)/shard_map/ppermute | solution.py:133
  130.8 32.8 %collective-permute-start.4 = (bf16[2,10,34,512]{3,0,2,1:T(2,128)(2,1)S(1)}, bf16[2,10,34,512]{3,0,2,1:T(2,128)(2,1)S(1)}, u32[]{:S(2)}, u32[]{:S(2)}) collective-permute-start(bf16[2,10,34,512]{3,0,2,1:T(2,128)(2,1)S(1)} %copy.23), channel_id=1, source_target_pairs={{0,4},{4,8},{8,12},{12,16},{16,20},{20,24},{24,28},{1,5},{5,9},{9,... | collective-permute-start | bytes 2088968 | tf_op jit(solution)/shard_map/ppermute | solution.py:19

commit v13 on v12

--- a/solution.py
+++ b/solution.py
@@ -142,12 +142,13 @@
         [(window_ids[a : a + FR_DEV] == own_ids).astype(jnp.int32) for a in range(3)]
     )
     reach = jnp.arange(3)[:, None] + jnp.arange(FR_DEV)[None, :]
-    own_valid = jnp.where(reach >= 2, validity, 0).reshape(-1)
+    own_valid = jnp.where(reach >= 2, validity, 0)
     prev_valid = jnp.where(reach < 2, validity, 0)[:2, :2].reshape(-1)
+    late_valid = jnp.concatenate([prev_valid, own_valid[2]])
     weights = conv_weight.reshape(9, 3 * channels, channels)
     bias = conv_bias.reshape(1, channels)
-    decoded, early = own_conv(own_valid, own_wide, weights, features, bias)
-    return prev_conv(prev_valid, prev_wide, weights, early, decoded)
+    early = early_conv(own_valid[:2].reshape(-1), own_wide, weights)
+    return late_conv(late_valid, prev_wide, weights, bias, own_wide, early, features)
 
 
 def widen(block, left, right):
@@ -156,17 +157,15 @@
     return jnp.concatenate([shifted_in, block, shifted_out], axis=-1)
 
 
-def own_kernel(valid_ref, x_ref, w_ref, b_ref, f_hbm, o_ref, early_ref, f_ref, acc_ref, sem):
+def early_kernel(valid_ref, x_ref, w_ref, acc_ref):
     tap_time = pl.program_id(0)
     tap_high = pl.program_id(1)
-    fetch = pltpu.make_async_copy(f_hbm, f_ref, sem)
 
     @pl.when((tap_time == 0) & (tap_high == 0))
     def _():
-        fetch.start()
         acc_ref[...] = jnp.zeros_like(acc_ref)
 
-    for a in range(3):
+    for a in range(2):
 
         @pl.when(tap_time == a)
         def _():
@@ -178,97 +177,107 @@
                 keep = valid_ref[a * FR_DEV + t].astype(jnp.float32)
                 acc_ref[t] += part[j * HR * WCOL : (j + 1) * HR * WCOL] * keep
 
-    @pl.when((tap_time == 2) & (tap_high == 2))
-    def _():
-        fetch.wait()
-        for t in range(FR_DEV):
-            total = (f_ref[t] + acc_ref[t].reshape(HR, WCOL, -1)) + b_ref[...]
-            if t < 2:
-                early_ref[t] = total
-            else:
-                o_ref[t] = total.astype(o_ref.dtype)
-
-
-def own_conv(validity, wide, weights, features, bias):
+
+def early_conv(validity, wide, weights):
+    frames = wide.shape[0]
+    channels = weights.shape[-1]
     return pl.pallas_call(
-        own_kernel,
-        grid_spec=pltpu.PrefetchScalarGridSpec(
-            num_scalar_prefetch=1,
-            grid=(3, 3),
-            in_specs=[
-                pl.BlockSpec(wide.shape, lambda a, b, v: (0, 0, 0, 0), pipeline_mode=pl.Buffered(1)),
-                pl.BlockSpec((1,) + weights.shape[1:], lambda a, b, v: (a * 3 + b, 0, 0)),
-                pl.BlockSpec(bias.shape, lambda a, b, v: (0, 0), pipeline_mode=pl.Buffered(1)),
-                pl.BlockSpec(memory_space=pl.ANY),
-            ],
-            out_specs=[
-                pl.BlockSpec(features.shape, lambda a, b, v: (0, 0, 0, 0)),
-                pl.BlockSpec((2,) + features.shape[1:], lambda a, b, v: (0, 0, 0, 0)),
-            ],
-            scratch_shapes=[
-                pltpu.VMEM(features.shape, jnp.float32),
-                pltpu.VMEM((features.shape[0], HR * WCOL, features.shape[-1]), jnp.float32),
-                pltpu.SemaphoreType.DMA(()),
-            ],
-        ),
-        out_shape=[
-            jax.ShapeDtypeStruct(features.shape, jnp.bfloat16),
-            jax.ShapeDtypeStruct((2,) + features.shape[1:], jnp.float32),
-        ],
-        compiler_params=pltpu.CompilerParams(
-            dimension_semantics=("arbitrary", "arbitrary"), vmem_limit_bytes=60 * 1024 * 1024
-        ),
-    )(validity, wide, weights, bias, features)
-
-
-def prev_kernel(valid_ref, x_ref, w_ref, early_ref, whole_ref, o_ref, acc_ref):
-    del whole_ref
-    tap_time = pl.program_id(0)
-    tap_high = pl.program_id(1)
-
-    @pl.when((tap_time == 0) & (tap_high == 0))
-    def _():
-        acc_ref[...] = jnp.zeros_like(acc_ref)
-
-    for a in range(2):
-
-        @pl.when(tap_time == a)
-        def _():
-            reach = 2 - a
-            lhs = x_ref[a : a + reach, pl.ds(tap_high, HR)].reshape(reach * HR * WCOL, -1)
-            part = jnp.dot(lhs, w_ref[0], preferred_element_type=jnp.float32)
-            for t in range(reach):
-                keep = valid_ref[a * 2 + t].astype(jnp.float32)
-                acc_ref[t] += part[t * HR * WCOL : (t + 1) * HR * WCOL] * keep
-
-    @pl.when((tap_time == 1) & (tap_high == 2))
-    def _():
-        for t in range(2):
-            total = early_ref[t] + acc_ref[t].reshape(HR, WCOL, -1)
-            o_ref[t] = total.astype(o_ref.dtype)
-
-
-def prev_conv(validity, wide, weights, early, decoded):
-    return pl.pallas_call(
-        prev_kernel,
+        early_kernel,
         grid_spec=pltpu.PrefetchScalarGridSpec(
             num_scalar_prefetch=1,
             grid=(2, 3),
             in_specs=[
                 pl.BlockSpec(wide.shape, lambda a, b, v: (0, 0, 0, 0), pipeline_mode=pl.Buffered(1)),
                 pl.BlockSpec((1,) + weights.shape[1:], lambda a, b, v: (a * 3 + b, 0, 0)),
-                pl.BlockSpec(early.shape, lambda a, b, v: (0, 0, 0, 0), pipeline_mode=pl.Buffered(1)),
+            ],
+            out_specs=pl.BlockSpec((frames, HR * WCOL, channels), lambda a, b, v: (0, 0, 0)),
+        ),
+        out_shape=jax.ShapeDtypeStruct((frames, HR * WCOL, channels), jnp.float32),
+        compiler_params=pltpu.CompilerParams(
+            dimension_semantics=("arbitrary", "arbitrary"), vmem_limit_bytes=60 * 1024 * 1024
+        ),
+    )(validity, wide, weights)
+
+
+def late_kernel(
+    valid_ref, xp_ref, w_ref, b_ref, xo_hbm, early_hbm, f_hbm, o_ref,
+    xo_ref, early_ref, f_ref, acc_ref, sems,
+):
+    tap_time = pl.program_id(0)
+    tap_high = pl.program_id(1)
+    own_copy = pltpu.make_async_copy(xo_hbm, xo_ref, sems.at[0])
+    early_copy = pltpu.make_async_copy(early_hbm, early_ref, sems.at[1])
+    feature_copy = pltpu.make_async_copy(f_hbm, f_ref, sems.at[2])
+
+    @pl.when((tap_time == 0) & (tap_high == 0))
+    def _():
+        own_copy.start()
+        early_copy.start()
+        feature_copy.start()
+        acc_ref[...] = jnp.zeros_like(acc_ref)
+
+    for a in range(2):
+
+        @pl.when(tap_time == a)
+        def _():
+            reach = 2 - a
+            lhs = xp_ref[a : a + reach, pl.ds(tap_high, HR)].reshape(reach * HR * WCOL, -1)
+            part = jnp.dot(lhs, w_ref[0], preferred_element_type=jnp.float32)
+            for t in range(reach):
+                keep = valid_ref[a * 2 + t].astype(jnp.float32)
+                acc_ref[t] += part[t * HR * WCOL : (t + 1) * HR * WCOL] * keep
+
+    @pl.when((tap_time == 2) & (tap_high == 0))
+    def _():
+        own_copy.wait()
+
+    @pl.when(tap_time == 2)
+    def _():
+        lhs = xo_ref[:, pl.ds(tap_high, HR)].reshape(FR_DEV * HR * WCOL, -1)
+        part = jnp.dot(lhs, w_ref[0], preferred_element_type=jnp.float32)
+        for t in range(FR_DEV):
+            keep = valid_ref[4 + t].astype(jnp.float32)
+            acc_ref[t] += part[t * HR * WCOL : (t + 1) * HR * WCOL] * keep
+
+    @pl.when((tap_time == 2) & (tap_high == 2))
+    def _():
+        early_copy.wait()
+        feature_copy.wait()
+        for t in range(FR_DEV):
+            conv_sum = (early_ref[t] + acc_ref[t]).reshape(HR, WCOL, -1)
+            o_ref[t] = ((f_ref[t] + conv_sum) + b_ref[...]).astype(o_ref.dtype)
+
+
+def late_conv(validity, prev_wide, weights, bias, own_wide, early, features):
+    return pl.pallas_call(
+        late_kernel,
+        grid_spec=pltpu.PrefetchScalarGridSpec(
+            num_scalar_prefetch=1,
+            grid=(3, 3),
+            in_specs=[
+                pl.BlockSpec(
+                    prev_wide.shape, lambda a, b, v: (0, 0, 0, 0), pipeline_mode=pl.Buffered(1)
+                ),
+                pl.BlockSpec((1,) + weights.shape[1:], lambda a, b, v: (a * 3 + b, 0, 0)),
+                pl.BlockSpec(bias.shape, lambda a, b, v: (0, 0), pipeline_mode=pl.Buffered(1)),
+                pl.BlockSpec(memory_space=pl.ANY),
+                pl.BlockSpec(memory_space=pl.ANY),
                 pl.BlockSpec(memory_space=pl.ANY),
             ],
-            out_specs=pl.BlockSpec(early.shape, lambda a, b, v: (0, 0, 0, 0)),
-            scratch_shapes=[pltpu.VMEM((2, HR * WCOL, early.shape[-1]), jnp.float32)],
-        ),
-        out_shape=jax.ShapeDtypeStruct(decoded.shape, decoded.dtype),
-        input_output_aliases={4: 0},
+            out_specs=pl.BlockSpec(features.shape, lambda a, b, v: (0, 0, 0, 0)),
+            scratch_shapes=[
+                pltpu.VMEM(own_wide.shape, own_wide.dtype),
+                pltpu.VMEM(early.shape, jnp.float32),
+                pltpu.VMEM(features.shape, jnp.float32),
+                pltpu.VMEM(early.shape, jnp.float32),
+                pltpu.SemaphoreType.DMA((3,)),
+            ],
+        ),
+        out_shape=jax.ShapeDtypeStruct(features.shape, jnp.bfloat16),
         compiler_params=pltpu.CompilerParams(
             dimension_semantics=("arbitrary", "arbitrary"), vmem_limit_bytes=60 * 1024 * 1024
         ),
-    )(validity, wide, weights, early, decoded)
+    )(validity, prev_wide, weights, bias, own_wide, early, features)
 
 
 def solution(mesh):

time: 178 us -> 181 us (1.017)
  Pallas kernels: 36.2 us -> 39.6 us
    pallas_call x2, Pallas kernels: 36.2 us -> 39.6 us  [the longest x1 21.8 us: late_conv(): pl.pallas_call(late_kernel, grid_spec=pltpu.PrefetchScalarGridSpec(num_sc...]
  transfers between devices with their start and end apart: 6 -> 6, of which waited for: 3 -> 3; matrix products, arithmetic and copies ran while one was open for 4% -> 4% of each run, Pallas kernels for 15% -> 10%
where the time goes in v13:
time: 181 us
  waiting for transfers between devices  60.3 us (33%)
  Pallas kernels  39.6 us (22%)
  other arithmetic  28.3 us (16%)
  local copies, waits for them, and re-layouts  25.3 us (14%)
  starting transfers between devices  23.3 us (13%)
  matrix products  3.23 us (2%)
    all_to_all x1, waiting for transfers between devices, shards(): lax.all_to_all(payload, ('src', 'frame', 'tile'), split_axis=0, concat_ax...  52.2 us
    pallas_call x1, Pallas kernels, late_conv(): pl.pallas_call(late_kernel, grid_spec=pltpu.PrefetchScalarGridSpec(num_sc...  21.8 us
    pallas_call x1, Pallas kernels, early_conv(): pl.pallas_call(early_kernel, grid_spec=pltpu.PrefetchScalarGridSpec(num_s...  17.8 us
    all_to_all x1, starting transfers between devices, shards(): lax.all_to_all(payload, ('src', 'frame', 'tile'), split_axis=0, concat_ax...  12 us
    gather x1, local copies, waits for them, and re-layouts, shards(): feats[pick.reshape(-1)].reshape(devices, block, channels)  8.91 us
    gather x1, local copies, waits for them, and re-layouts, shards(): arrived.reshape(-1, channels)[gather_rows]  7.93 us
    concatenate x2, other arithmetic, widen(): return jnp.concatenate([shifted_in, block, shifted_out], axis=-1)  5.58 us
    ppermute x1, waiting for transfers between devices, with_halo(): after = lax.ppermute(leading, axis, down)  5.25 us
  transfers between devices with their start and end apart: 6, of which 3 were waited for; matrix products, arithmetic and copies ran while one was open for 4% of the time, Pallas kernels for 10%

profile of v13, /device:TPU:1, one launch (start us, length us, event | category | flops | bytes accessed | tf_op | source)
XLA Modules:
  0.0 180.7 jit_solution(17764912470625331035)
XLA Ops:
  0.0 0.7 fusion.11
  0.7 1.2 fusion.48
  1.9 3.3 %multiply_reduce_fusion.2 = f32[4,512]{1,0:T(4,128)S(1)} fusion(f32[4,1536]{1,0:T(4,128)S(1)} %bitcast.34, f32[1536,512]{1,0:T(8,128)} %param.7), kind=kLoop, calls=%fused_computation.4 | loop fusion | flops 6289408 | bytes 3178496 | tf_op jit(solution)/shard_map/reduce_sum | solution.py:60
  5.8 1.3 multiply_reduce_fusion.1
  7.1 0.8 subtract_multiply_fusion
  7.9 1.1 multiply_reduce_fusion
  9.3 5.1 %sort.21 = (s32[1536]{0:T(1024)}, s32[1536]{0:T(1024)S(1)}, s32[1536]{0:T(1024)S(1)}) sort(s32[1536]{0:T(1024)S(1)} %get-tuple-element.25, s32[1536]{0:T(1024)S(1)} %get-tuple-element.26, s32[1536]{0:T(1024)S(1)} %iota.36), dimensions={0}, to_apply=%region_0.1 | sort | flops 16896 | bytes 36864 | tf_op jit(solution)/shard_map/sort | solution.py:73
  14.8 8.9 %gather_fusion = f32[2048,512]{1,0:T(8,128)} fusion(f32[1536,512]{1,0:T(8,128)S(1)} %copy-done, s32[2048]{0:T(1024)S(1)} %broadcast_clamp_fusion), kind=kCustom, calls=%fused_computation | custom fusion | bytes 8396800 | tf_op jit(solution)/shard_map/gather | solution.py:89
  23.9 5.2 %broadcast_select_fusion = f32[128,16,512]{2,1,0:T(8,128)} fusion(f32[128,16,512]{2,1,0:T(8,128)} %bitcast.29, f32[128,512]{1,0:T(8,128)S(1)} %maximum_maximum_fusion.2, pred[16]{0:T(512)(128)(4,1)S(1)} %iota_compare_fusion.11), kind=kLoop, calls=%fused_computation.12 | loop fusion | flops 1048576 | bytes 8650768 | tf_op jit(solution)/shard_map/jit(_where)/select_n | solution.py:88
  29.1 12.0 %all-to-all-start = ((f32[128,16,512]{2,1,0:T(8,128)}), f32[128,16,512]{2,1,0:T(8,128)}, u32[]{:S(2)}, u32[]{:S(2)}) async-start(f32[128,16,512]{2,1,0:T(8,128)} %broadcast_select_fusion), calls=%async_computation | async-start | bytes 8388608 | tf_op jit(solution)/shard_map/all_to_all | solution.py:91
  41.6 52.2 %all-to-all-done = f32[128,16,512]{2,1,0:T(8,128)} async-done(((f32[128,16,512]{2,1,0:T(8,128)}), f32[128,16,512]{2,1,0:T(8,128)}, u32[]{:S(2)}, u32[]{:S(2)}) %all-to-all-start) | async-done | bytes 4194336 | tf_op jit(solution)/shard_map/all_to_all | solution.py:91
  93.7 1.9 %slice.115 = f32[128,1,512]{2,1,0:T(1,128)S(1)} slice(f32[128,16,512]{2,1,0:T(8,128)} %all-to-all-done), slice={[0:128], [12:13], [0:512]} | slice | bytes 524288 | tf_op jit(solution)/shard_map/slice | solution.py:95
  97.5 1.7 fusion.2
  99.3 7.9 %gather_fusion.1 = f32[1536,512]{1,0:T(8,128)} fusion(f32[2048,512]{1,0:T(8,128)} %bitcast.6, s32[2048]{0:T(1024)S(1)} %pad_clamp_fusion), kind=kCustom, calls=%fused_computation.1 | custom fusion | bytes 6297600 | tf_op jit(solution)/shard_map/gather | solution.py:115
  107.2 2.9 %multiply_convert_fusion = bf16[6,8,32,512]{3,2,1,0:T(8,128)(2,1)S(1)} fusion(f32[6,8,32,512]{3,2,1,0:T(8,128)} %bitcast.27, f32[512]{0:T(512)S(1)} %copy-done.1, f32[512]{0:T(512)S(1)} %copy-done.2, f32[6,512]{1,0:T(8,128)S(1)} %mul.141, f32[6,512]{1,0:T(8,128)S(1)} %sub.56), kind=kLoop, calls=%fused_computation.9 | loop fusion | flops 7077888 | bytes 4747264 | tf_op jit(solution)/shard_map/convert_element_type | solution.py:128
  110.1 3.6 %collective-permute-start = (bf16[6,1,32,512]{3,2,1,0:T(8,128)(2,1)S(1)}, bf16[6,1,32,512]{3,2,1,0:T(8,128)(2,1)S(1)}, u32[]{:S(2)}, u32[]{:S(2)}) collective-permute-start(bf16[6,1,32,512]{3,2,1,0:T(8,128)(2,1)S(1)} %get-tuple-element.15), channel_id=1, source_target_pairs={{0,1},{1,2},{2,3},{4,5},{5,6},{6,7},{8,9},{9,10},{10,11},{12,13},{... | collective-permute-start | bytes 589832 | tf_op jit(solution)/shard_map/ppermute | solution.py:29
  113.8 1.9 %collective-permute-start.1 = (bf16[6,1,32,512]{3,2,1,0:T(8,128)(2,1)S(1)}, bf16[6,1,32,512]{3,2,1,0:T(8,128)(2,1)S(1)}, u32[]{:S(2)}, u32[]{:S(2)}) collective-permute-start(bf16[6,1,32,512]{3,2,1,0:T(8,128)(2,1)S(1)} %get-tuple-element.16), channel_id=1, source_target_pairs={{1,0},{2,1},{3,2},{5,4},{6,5},{7,6},{9,8},{10,9},{11,10},{13,12},{... | collective-permute-start | bytes 589832 | tf_op jit(solution)/shard_map/ppermute | solution.py:30
  115.7 0.6 reshape.254.valid_ref
  116.4 0.6 pad_add_fusion.valid_ref
  117.0 5.2 %collective-permute-done.1 = bf16[6,1,32,512]{3,2,1,0:T(8,128)(2,1)S(1)} collective-permute-done((bf16[6,1,32,512]{3,2,1,0:T(8,128)(2,1)S(1)}, bf16[6,1,32,512]{3,2,1,0:T(8,128)(2,1)S(1)}, u32[]{:S(2)}, u32[]{:S(2)}) %collective-permute-start.1) | collective-permute-done | bytes 196640 | tf_op jit(solution)/shard_map/ppermute | solution.py:30
  122.5 1.5 collective-permute-start.2
  123.9 1.5 collective-permute-start.3
  125.7 1.3 fusion.43
  127.1 2.8 %collective-permute-done.3 = bf16[6,10,1,512]{3,2,1,0:T(2,128)(2,1)S(1)} collective-permute-done((bf16[6,10,1,512]{3,2,1,0:T(2,128)(2,1)S(1)}, bf16[6,10,1,512]{3,2,1,0:T(2,128)(2,1)S(1)}, u32[]{:S(2)}, u32[]{:S(2)}) %collective-permute-start.3) | collective-permute-done | bytes 61472 | tf_op jit(solution)/shard_map/ppermute | solution.py:133
  130.1 0.7 copy.22
  130.8 2.9 %collective-permute-start.4 = (bf16[2,10,34,512]{3,0,2,1:T(2,128)(2,1)S(1)}, bf16[2,10,34,512]{3,0,2,1:T(2,128)(2,1)S(1)}, u32[]{:S(2)}, u32[]{:S(2)}) collective-permute-start(bf16[2,10,34,512]{3,0,2,1:T(2,128)(2,1)S(1)} %copy.22), channel_id=1, source_target_pairs={{0,4},{4,8},{8,12},{12,16},{16,20},{20,24},{24,28},{1,5},{5,9},{9,... | collective-permute-start | bytes 2088968 | tf_op jit(solution)/shard_map/ppermute | solution.py:19
  133.7 3.8 %maximum_maximum_fusion.x_ref.xo_hbm = bf16[6,10,32,1536]{3,2,1,0:T(8,128)(2,1)} fusion(bf16[6,10,1,512]{3,2,1,0:T(2,128)(2,1)S(1)} %collective-permute-done.3, bf16[6,10,31,512]{3,2,1,0:T(8,128)(2,1)S(1)} %get-tuple-element.12, bf16[6,1,32,512]{3,2,1,0:T(8,128)(2,1)S(1)} %collective-permute-done.1, bf16[6,8,32,512]{3,2,1,0:T(8,128)(2,1)S(1)} %multiply_convert_fusion, ...), kind=kLoop, calls=%fused_computation.7 | loop fusion | flops 41287680 | bytes 11796480 | tf_op jit(solution)/shard_map/concatenate | solution.py:157
  137.5 17.8 %shard_map.73.early_hbm = f32[6,256,512]{2,1,0:T(8,128)} custom-call(s32[12]{0:T(128)} %reshape.254.valid_ref, bf16[6,10,32,1536]{3,2,1,0:T(8,128)(2,1)} %maximum_maximum_fusion.x_ref.xo_hbm, bf16[9,1536,512]{2,1,0:T(8,128)(2,1)} %bitcast.25), custom_call_target="tpu_custom_call" | custom-call | tf_op jit(solution)/shard_map/pallas_call | solution.py:184
  155.3 0.7 fusion.46
  156.2 0.5 slice.129
  156.9 1.7 maximum_maximum_fusion.1.xp_ref
  158.7 21.8 %shard_map.74 = bf16[6,8,32,512]{3,2,1,0:T(8,128)(2,1)} custom-call(s32[10]{0:T(128)} %pad_add_fusion.valid_ref, bf16[2,10,32,1536]{3,2,1,0:T(8,128)(2,1)} %maximum_maximum_fusion.1.xp_ref, bf16[9,1536,512]{2,1,0:T(8,128)(2,1)} %bitcast.26, f32[1,512]{1,0:T(1,128)} %bitcast.38, bf16[6,10,32,1536]{3,2,1,0:T(8,128)(2,1)} %maximum_maximum_fusion.x_ref.xo_hbm, ...), custom_call_target="tpu_custom_call" | custom-call | tf_op jit(solution)/shard_map/pallas_call | solution.py:252
  (78 shorter events, 4.9 us)
Async XLA Ops:
  1.9 5.2 %copy-start = (f32[1536,512]{1,0:T(8,128)S(1)}, f32[1536,512]{1,0:T(8,128)}, u32[]{:S(2)}) copy-start(f32[1536,512]{1,0:T(8,128)} %param.7) | copy-start | bytes 9437188
  29.1 12.0 %copy-start.3 = (s32[48]{0:T(128)S(1)}, s32[48]{0:T(128)}, u32[]{:S(2)}) copy-start(s32[48]{0:T(128)} %param.9) | copy-start | bytes 580
  29.1 64.6 %all-to-all-start = ((f32[128,16,512]{2,1,0:T(8,128)}), f32[128,16,512]{2,1,0:T(8,128)}, u32[]{:S(2)}, u32[]{:S(2)}) async-start(f32[128,16,512]{2,1,0:T(8,128)} %broadcast_select_fusion), calls=%async_computation | async-start | bytes 8388608 | tf_op jit(solution)/shard_map/all_to_all | solution.py:91
  99.2 8.0 %copy-start.1 = (f32[512]{0:T(512)S(1)}, f32[512]{0:T(512)}, u32[]{:S(2)}) copy-start(f32[512]{0:T(512)} %param.11) | copy-start | bytes 6148
  99.3 7.9 %copy-start.2 = (f32[512]{0:T(512)S(1)}, f32[512]{0:T(512)}, u32[]{:S(2)}) copy-start(f32[512]{0:T(512)} %param.10) | copy-start | bytes 6148
  110.1 6.9 %collective-permute-start = (bf16[6,1,32,512]{3,2,1,0:T(8,128)(2,1)S(1)}, bf16[6,1,32,512]{3,2,1,0:T(8,128)(2,1)S(1)}, u32[]{:S(2)}, u32[]{:S(2)}) collective-permute-start(bf16[6,1,32,512]{3,2,1,0:T(8,128)(2,1)S(1)} %get-tuple-element.15), channel_id=1, source_target_pairs={{0,1},{1,2},{2,3},{4,5},{5,6},{6,7},{8,9},{9,10},{10,11},{12,13},{... | collective-permute-start | bytes 589832 | tf_op jit(solution)/shard_map/ppermute | solution.py:29
  113.8 8.5 %collective-permute-start.1 = (bf16[6,1,32,512]{3,2,1,0:T(8,128)(2,1)S(1)}, bf16[6,1,32,512]{3,2,1,0:T(8,128)(2,1)S(1)}, u32[]{:S(2)}, u32[]{:S(2)}) collective-permute-start(bf16[6,1,32,512]{3,2,1,0:T(8,128)(2,1)S(1)} %get-tuple-element.16), channel_id=1, source_target_pairs={{1,0},{2,1},{3,2},{5,4},{6,5},{7,6},{9,8},{10,9},{11,10},{13,12},{... | collective-permute-start | bytes 589832 | tf_op jit(solution)/shard_map/ppermute | solution.py:30
  122.5 4.5 %collective-permute-start.2 = (bf16[6,10,1,512]{3,2,1,0:T(2,128)(2,1)S(1)}, bf16[6,10,1,512]{3,2,1,0:T(2,128)(2,1)S(1)}, u32[]{:S(2)}, u32[]{:S(2)}) collective-permute-start(bf16[6,10,1,512]{3,2,1,0:T(2,128)(2,1)S(1)} %get-tuple-element.13), channel_id=1, source_target_pairs={{0,32},{32,64},{64,96},{1,33},{33,65},{65,97},{2,34},{34,66},{66,9... | collective-permute-start | bytes 184328 | tf_op jit(solution)/shard_map/ppermute | solution.py:132
  123.9 6.0 %collective-permute-start.3 = (bf16[6,10,1,512]{3,2,1,0:T(2,128)(2,1)S(1)}, bf16[6,10,1,512]{3,2,1,0:T(2,128)(2,1)S(1)}, u32[]{:S(2)}, u32[]{:S(2)}) collective-permute-start(bf16[6,10,1,512]{3,2,1,0:T(2,128)(2,1)S(1)} %get-tuple-element.14), channel_id=1, source_target_pairs={{32,0},{64,32},{96,64},{33,1},{65,33},{97,65},{34,2},{66,34},{98,6... | collective-permute-start | bytes 184328 | tf_op jit(solution)/shard_map/ppermute | solution.py:133
  130.8 24.5 %collective-permute-start.4 = (bf16[2,10,34,512]{3,0,2,1:T(2,128)(2,1)S(1)}, bf16[2,10,34,512]{3,0,2,1:T(2,128)(2,1)S(1)}, u32[]{:S(2)}, u32[]{:S(2)}) collective-permute-start(bf16[2,10,34,512]{3,0,2,1:T(2,128)(2,1)S(1)} %copy.22), channel_id=1, source_target_pairs={{0,4},{4,8},{8,12},{12,16},{16,20},{20,24},{24,28},{1,5},{5,9},{9,... | collective-permute-start | bytes 2088968 | tf_op jit(solution)/shard_map/ppermute | solution.py:19

commit v14 on v12

--- a/solution.py
+++ b/solution.py
@@ -224,9 +224,8 @@
 def prev_kernel(valid_ref, x_ref, w_ref, early_ref, whole_ref, o_ref, acc_ref):
     del whole_ref
     tap_time = pl.program_id(0)
-    tap_high = pl.program_id(1)
-
-    @pl.when((tap_time == 0) & (tap_high == 0))
+
+    @pl.when(tap_time == 0)
     def _():
         acc_ref[...] = jnp.zeros_like(acc_ref)
 
@@ -235,13 +234,14 @@
         @pl.when(tap_time == a)
         def _():
             reach = 2 - a
-            lhs = x_ref[a : a + reach, pl.ds(tap_high, HR)].reshape(reach * HR * WCOL, -1)
-            part = jnp.dot(lhs, w_ref[0], preferred_element_type=jnp.float32)
-            for t in range(reach):
-                keep = valid_ref[a * 2 + t].astype(jnp.float32)
-                acc_ref[t] += part[t * HR * WCOL : (t + 1) * HR * WCOL] * keep
-
-    @pl.when((tap_time == 1) & (tap_high == 2))
+            for b in range(3):
+                lhs = x_ref[a : a + reach, b : b + HR].reshape(reach * HR * WCOL, -1)
+                part = jnp.dot(lhs, w_ref[0, b], preferred_element_type=jnp.float32)
+                for t in range(reach):
+                    keep = valid_ref[a * 2 + t].astype(jnp.float32)
+                    acc_ref[t] += part[t * HR * WCOL : (t + 1) * HR * WCOL] * keep
+
+    @pl.when(tap_time == 1)
     def _():
         for t in range(2):
             total = early_ref[t] + acc_ref[t].reshape(HR, WCOL, -1)
@@ -249,26 +249,27 @@
 
 
 def prev_conv(validity, wide, weights, early, decoded):
+    taps = weights.reshape(3, 3, *weights.shape[1:])
     return pl.pallas_call(
         prev_kernel,
         grid_spec=pltpu.PrefetchScalarGridSpec(
             num_scalar_prefetch=1,
-            grid=(2, 3),
+            grid=(2,),
             in_specs=[
-                pl.BlockSpec(wide.shape, lambda a, b, v: (0, 0, 0, 0), pipeline_mode=pl.Buffered(1)),
-                pl.BlockSpec((1,) + weights.shape[1:], lambda a, b, v: (a * 3 + b, 0, 0)),
-                pl.BlockSpec(early.shape, lambda a, b, v: (0, 0, 0, 0), pipeline_mode=pl.Buffered(1)),
+                pl.BlockSpec(wide.shape, lambda a, v: (0, 0, 0, 0), pipeline_mode=pl.Buffered(1)),
+                pl.BlockSpec((1,) + taps.shape[1:], lambda a, v: (a, 0, 0, 0)),
+                pl.BlockSpec(early.shape, lambda a, v: (0, 0, 0, 0), pipeline_mode=pl.Buffered(1)),
                 pl.BlockSpec(memory_space=pl.ANY),
             ],
-            out_specs=pl.BlockSpec(early.shape, lambda a, b, v: (0, 0, 0, 0)),
+            out_specs=pl.BlockSpec(early.shape, lambda a, v: (0, 0, 0, 0)),
             scratch_shapes=[pltpu.VMEM((2, HR * WCOL, early.shape[-1]), jnp.float32)],
         ),
         out_shape=jax.ShapeDtypeStruct(decoded.shape, decoded.dtype),
         input_output_aliases={4: 0},
         compiler_params=pltpu.CompilerParams(
-            dimension_semantics=("arbitrary", "arbitrary"), vmem_limit_bytes=60 * 1024 * 1024
-        ),
-    )(validity, wide, weights, early, decoded)
+            dimension_semantics=("arbitrary",), vmem_limit_bytes=60 * 1024 * 1024
+        ),
+    )(validity, wide, taps, early, decoded)
 
 
 def solution(mesh):

time: 178 us -> 176 us (0.989)
  no operation moved by 1% of the time
where the time goes in v14:
time: 176 us
  waiting for transfers between devices  60.4 us (34%)
  Pallas kernels  34.8 us (20%)
  other arithmetic  27.6 us (16%)
  local copies, waits for them, and re-layouts  25.8 us (15%)
  starting transfers between devices  23.3 us (13%)
  matrix products  3.23 us (2%)
    all_to_all x1, waiting for transfers between devices, shards(): lax.all_to_all(payload, ('src', 'frame', 'tile'), split_axis=0, concat_ax...  52.2 us
    pallas_call x1, Pallas kernels, own_conv(): pl.pallas_call(own_kernel, grid_spec=pltpu.PrefetchScalarGridSpec(num_sca...  26.1 us
    all_to_all x1, starting transfers between devices, shards(): lax.all_to_all(payload, ('src', 'frame', 'tile'), split_axis=0, concat_ax...  12 us
    gather x1, local copies, waits for them, and re-layouts, shards(): feats[pick.reshape(-1)].reshape(devices, block, channels)  8.91 us
    pallas_call x1, Pallas kernels, prev_conv(): pl.pallas_call(prev_kernel, grid_spec=pltpu.PrefetchScalarGridSpec(num_sc...  8.76 us
    gather x1, local copies, waits for them, and re-layouts, shards(): arrived.reshape(-1, channels)[gather_rows]  7.93 us
    concatenate x2, other arithmetic, widen(): return jnp.concatenate([shifted_in, block, shifted_out], axis=-1)  5.53 us
    ppermute x1, waiting for transfers between devices, with_halo(): after = lax.ppermute(leading, axis, down)  5.32 us
  transfers between devices with their start and end apart: 6, of which 3 were waited for; matrix products, arithmetic and copies ran while one was open for 4% of the time, Pallas kernels for 15%

profile of v14, /device:TPU:1, one launch (start us, length us, event | category | flops | bytes accessed | tf_op | source)
XLA Modules:
  0.0 175.7 jit_solution(2507318195105157368)
XLA Ops:
  0.0 0.7 fusion.11
  0.7 1.2 fusion.48
  1.9 3.3 %multiply_reduce_fusion.2 = f32[4,512]{1,0:T(4,128)S(1)} fusion(f32[4,1536]{1,0:T(4,128)S(1)} %bitcast.33, f32[1536,512]{1,0:T(8,128)} %param.7), kind=kLoop, calls=%fused_computation.4 | loop fusion | flops 6289408 | bytes 3178496 | tf_op jit(solution)/shard_map/reduce_sum | solution.py:60
  5.8 1.3 multiply_reduce_fusion.1
  7.1 0.8 subtract_multiply_fusion
  7.9 1.1 multiply_reduce_fusion
  9.3 5.1 %sort.21 = (s32[1536]{0:T(1024)}, s32[1536]{0:T(1024)S(1)}, s32[1536]{0:T(1024)S(1)}) sort(s32[1536]{0:T(1024)S(1)} %get-tuple-element.29, s32[1536]{0:T(1024)S(1)} %get-tuple-element.30, s32[1536]{0:T(1024)S(1)} %iota.38), dimensions={0}, to_apply=%region_0.1 | sort | flops 16896 | bytes 36864 | tf_op jit(solution)/shard_map/sort | solution.py:73
  14.8 8.9 %gather_fusion = f32[2048,512]{1,0:T(8,128)} fusion(f32[1536,512]{1,0:T(8,128)S(1)} %copy-done, s32[2048]{0:T(1024)S(1)} %broadcast_clamp_fusion), kind=kCustom, calls=%fused_computation | custom fusion | bytes 8396800 | tf_op jit(solution)/shard_map/gather | solution.py:89
  23.9 5.2 %broadcast_select_fusion = f32[128,16,512]{2,1,0:T(8,128)} fusion(f32[128,16,512]{2,1,0:T(8,128)} %bitcast.28, f32[128,512]{1,0:T(8,128)S(1)} %maximum_maximum_fusion.2, pred[16]{0:T(512)(128)(4,1)S(1)} %iota_compare_fusion.11), kind=kLoop, calls=%fused_computation.12 | loop fusion | flops 1048576 | bytes 8650768 | tf_op jit(solution)/shard_map/jit(_where)/select_n | solution.py:88
  29.1 12.0 %all-to-all-start = ((f32[128,16,512]{2,1,0:T(8,128)}), f32[128,16,512]{2,1,0:T(8,128)}, u32[]{:S(2)}, u32[]{:S(2)}) async-start(f32[128,16,512]{2,1,0:T(8,128)} %broadcast_select_fusion), calls=%async_computation | async-start | bytes 8388608 | tf_op jit(solution)/shard_map/all_to_all | solution.py:91
  41.5 52.2 %all-to-all-done = f32[128,16,512]{2,1,0:T(8,128)} async-done(((f32[128,16,512]{2,1,0:T(8,128)}), f32[128,16,512]{2,1,0:T(8,128)}, u32[]{:S(2)}, u32[]{:S(2)}) %all-to-all-start) | async-done | bytes 4194336 | tf_op jit(solution)/shard_map/all_to_all | solution.py:91
  93.7 1.9 %slice.107 = f32[128,1,512]{2,1,0:T(1,128)S(1)} slice(f32[128,16,512]{2,1,0:T(8,128)} %all-to-all-done), slice={[0:128], [12:13], [0:512]} | slice | bytes 524288 | tf_op jit(solution)/shard_map/slice | solution.py:95
  97.5 1.7 fusion.2
  99.3 7.9 %gather_fusion.1 = f32[1536,512]{1,0:T(8,128)} fusion(f32[2048,512]{1,0:T(8,128)} %bitcast.5, s32[2048]{0:T(1024)S(1)} %pad_clamp_fusion), kind=kCustom, calls=%fused_computation.1 | custom fusion | bytes 6297600 | tf_op jit(solution)/shard_map/gather | solution.py:115
  107.2 2.9 %multiply_convert_fusion = bf16[6,8,32,512]{3,2,1,0:T(8,128)(2,1)S(1)} fusion(f32[6,8,32,512]{3,2,1,0:T(8,128)} %bitcast.26, f32[512]{0:T(512)S(1)} %copy-done.1, f32[512]{0:T(512)S(1)} %copy-done.2, f32[6,512]{1,0:T(8,128)S(1)} %mul.141, f32[6,512]{1,0:T(8,128)S(1)} %sub.56), kind=kLoop, calls=%fused_computation.9 | loop fusion | flops 7077888 | bytes 4747264 | tf_op jit(solution)/shard_map/convert_element_type | solution.py:128
  110.1 3.6 %collective-permute-start = (bf16[6,1,32,512]{3,2,1,0:T(8,128)(2,1)S(1)}, bf16[6,1,32,512]{3,2,1,0:T(8,128)(2,1)S(1)}, u32[]{:S(2)}, u32[]{:S(2)}) collective-permute-start(bf16[6,1,32,512]{3,2,1,0:T(8,128)(2,1)S(1)} %get-tuple-element.19), channel_id=1, source_target_pairs={{0,1},{1,2},{2,3},{4,5},{5,6},{6,7},{8,9},{9,10},{10,11},{12,13},{... | collective-permute-start | bytes 589832 | tf_op jit(solution)/shard_map/ppermute | solution.py:29
  113.8 1.9 %collective-permute-start.1 = (bf16[6,1,32,512]{3,2,1,0:T(8,128)(2,1)S(1)}, bf16[6,1,32,512]{3,2,1,0:T(8,128)(2,1)S(1)}, u32[]{:S(2)}, u32[]{:S(2)}) collective-permute-start(bf16[6,1,32,512]{3,2,1,0:T(8,128)(2,1)S(1)} %get-tuple-element.20), channel_id=1, source_target_pairs={{1,0},{2,1},{3,2},{5,4},{6,5},{7,6},{9,8},{10,9},{11,10},{13,12},{... | collective-permute-start | bytes 589832 | tf_op jit(solution)/shard_map/ppermute | solution.py:30
  115.8 0.6 select_n.123.valid_ref
  116.4 0.6 reshape.248.valid_ref
  116.9 5.3 %collective-permute-done.1 = bf16[6,1,32,512]{3,2,1,0:T(8,128)(2,1)S(1)} collective-permute-done((bf16[6,1,32,512]{3,2,1,0:T(8,128)(2,1)S(1)}, bf16[6,1,32,512]{3,2,1,0:T(8,128)(2,1)S(1)}, u32[]{:S(2)}, u32[]{:S(2)}) %collective-permute-start.1) | collective-permute-done | bytes 196640 | tf_op jit(solution)/shard_map/ppermute | solution.py:30
  122.5 1.5 collective-permute-start.2
  123.9 1.5 collective-permute-start.3
  125.7 1.3 fusion.43
  127.1 2.8 %collective-permute-done.3 = bf16[6,10,1,512]{3,2,1,0:T(2,128)(2,1)S(1)} collective-permute-done((bf16[6,10,1,512]{3,2,1,0:T(2,128)(2,1)S(1)}, bf16[6,10,1,512]{3,2,1,0:T(2,128)(2,1)S(1)}, u32[]{:S(2)}, u32[]{:S(2)}) %collective-permute-start.3) | collective-permute-done | bytes 61472 | tf_op jit(solution)/shard_map/ppermute | solution.py:133
  130.1 0.7 copy.23
  130.8 2.9 %collective-permute-start.4 = (bf16[2,10,34,512]{3,0,2,1:T(2,128)(2,1)S(1)}, bf16[2,10,34,512]{3,0,2,1:T(2,128)(2,1)S(1)}, u32[]{:S(2)}, u32[]{:S(2)}) collective-permute-start(bf16[2,10,34,512]{3,0,2,1:T(2,128)(2,1)S(1)} %copy.23), channel_id=1, source_target_pairs={{0,4},{4,8},{8,12},{12,16},{16,20},{20,24},{24,28},{1,5},{5,9},{9,... | collective-permute-start | bytes 2088968 | tf_op jit(solution)/shard_map/ppermute | solution.py:19
  133.7 3.8 %maximum_maximum_fusion.x_ref = bf16[6,10,32,1536]{3,2,1,0:T(8,128)(2,1)} fusion(bf16[6,10,1,512]{3,2,1,0:T(2,128)(2,1)S(1)} %collective-permute-done.3, bf16[6,10,31,512]{3,2,1,0:T(8,128)(2,1)S(1)} %get-tuple-element.16, bf16[6,1,32,512]{3,2,1,0:T(8,128)(2,1)S(1)} %collective-permute-done.1, bf16[6,8,32,512]{3,2,1,0:T(8,128)(2,1)S(1)} %multiply_convert_fusion, ...), kind=kLoop, calls=%fused_computation.7 | loop fusion | flops 41287680 | bytes 11796480 | tf_op jit(solution)/shard_map/concatenate | solution.py:156
  137.5 26.1 %shard_map.73 = (bf16[6,8,32,512]{3,2,1,0:T(8,128)(2,1)}, f32[2,8,32,512]{3,2,1,0:T(8,128)}) custom-call(s32[18]{0:T(128)} %select_n.123.valid_ref, bf16[6,10,32,1536]{3,2,1,0:T(8,128)(2,1)} %maximum_maximum_fusion.x_ref, bf16[9,1536,512]{2,1,0:T(8,128)(2,1)} %bitcast.24, f32[1,512]{1,0:T(1,128)} %bitcast.37, f32[6,8,32,512]{3,2,1,0:T(8,128)} %bitcast.27), custom_call_target="tpu_custom_call" | custom-call | tf_op jit(solution)/shard_map/pallas_call | solution.py:193
  163.6 0.7 fusion.46
  164.5 0.5 slice.121
  165.2 1.7 maximum_maximum_fusion.1.x_ref
  166.9 8.8 %shard_map.74 = bf16[6,8,32,512]{3,2,1,0:T(8,128)(2,1)} custom-call(s32[4]{0:T(128)} %reshape.248.valid_ref, bf16[2,10,32,1536]{3,2,1,0:T(8,128)(2,1)} %maximum_maximum_fusion.1.x_ref, bf16[3,3,1536,512]{3,2,1,0:T(8,128)(2,1)} %bitcast.25, f32[2,8,32,512]{3,2,1,0:T(8,128)} %get-tuple-element.11.early_ref, ...), custom_call_target="tpu_custom_call", output_to_operand_aliasing={{}: (4, {})} | custom-call | tf_op jit(solution)/shard_map/pallas_call | solution.py:253
  (75 shorter events, 4.8 us)
Async XLA Ops:
  1.9 5.2 %copy-start = (f32[1536,512]{1,0:T(8,128)S(1)}, f32[1536,512]{1,0:T(8,128)}, u32[]{:S(2)}) copy-start(f32[1536,512]{1,0:T(8,128)} %param.7) | copy-start | bytes 9437188
  29.1 12.0 %copy-start.3 = (s32[48]{0:T(128)S(1)}, s32[48]{0:T(128)}, u32[]{:S(2)}) copy-start(s32[48]{0:T(128)} %param.9) | copy-start | bytes 580
  29.1 64.6 %all-to-all-start = ((f32[128,16,512]{2,1,0:T(8,128)}), f32[128,16,512]{2,1,0:T(8,128)}, u32[]{:S(2)}, u32[]{:S(2)}) async-start(f32[128,16,512]{2,1,0:T(8,128)} %broadcast_select_fusion), calls=%async_computation | async-start | bytes 8388608 | tf_op jit(solution)/shard_map/all_to_all | solution.py:91
  99.2 8.0 %copy-start.1 = (f32[512]{0:T(512)S(1)}, f32[512]{0:T(512)}, u32[]{:S(2)}) copy-start(f32[512]{0:T(512)} %param.11) | copy-start | bytes 6148
  99.3 7.9 %copy-start.2 = (f32[512]{0:T(512)S(1)}, f32[512]{0:T(512)}, u32[]{:S(2)}) copy-start(f32[512]{0:T(512)} %param.10) | copy-start | bytes 6148
  110.1 6.8 %collective-permute-start = (bf16[6,1,32,512]{3,2,1,0:T(8,128)(2,1)S(1)}, bf16[6,1,32,512]{3,2,1,0:T(8,128)(2,1)S(1)}, u32[]{:S(2)}, u32[]{:S(2)}) collective-permute-start(bf16[6,1,32,512]{3,2,1,0:T(8,128)(2,1)S(1)} %get-tuple-element.19), channel_id=1, source_target_pairs={{0,1},{1,2},{2,3},{4,5},{5,6},{6,7},{8,9},{9,10},{10,11},{12,13},{... | collective-permute-start | bytes 589832 | tf_op jit(solution)/shard_map/ppermute | solution.py:29
  113.8 8.5 %collective-permute-start.1 = (bf16[6,1,32,512]{3,2,1,0:T(8,128)(2,1)S(1)}, bf16[6,1,32,512]{3,2,1,0:T(8,128)(2,1)S(1)}, u32[]{:S(2)}, u32[]{:S(2)}) collective-permute-start(bf16[6,1,32,512]{3,2,1,0:T(8,128)(2,1)S(1)} %get-tuple-element.20), channel_id=1, source_target_pairs={{1,0},{2,1},{3,2},{5,4},{6,5},{7,6},{9,8},{10,9},{11,10},{13,12},{... | collective-permute-start | bytes 589832 | tf_op jit(solution)/shard_map/ppermute | solution.py:30
  122.5 4.5 %collective-permute-start.2 = (bf16[6,10,1,512]{3,2,1,0:T(2,128)(2,1)S(1)}, bf16[6,10,1,512]{3,2,1,0:T(2,128)(2,1)S(1)}, u32[]{:S(2)}, u32[]{:S(2)}) collective-permute-start(bf16[6,10,1,512]{3,2,1,0:T(2,128)(2,1)S(1)} %get-tuple-element.17), channel_id=1, source_target_pairs={{0,32},{32,64},{64,96},{1,33},{33,65},{65,97},{2,34},{34,66},{66,9... | collective-permute-start | bytes 184328 | tf_op jit(solution)/shard_map/ppermute | solution.py:132
  123.9 6.0 %collective-permute-start.3 = (bf16[6,10,1,512]{3,2,1,0:T(2,128)(2,1)S(1)}, bf16[6,10,1,512]{3,2,1,0:T(2,128)(2,1)S(1)}, u32[]{:S(2)}, u32[]{:S(2)}) collective-permute-start(bf16[6,10,1,512]{3,2,1,0:T(2,128)(2,1)S(1)} %get-tuple-element.18), channel_id=1, source_target_pairs={{32,0},{64,32},{96,64},{33,1},{65,33},{97,65},{34,2},{66,34},{98,6... | collective-permute-start | bytes 184328 | tf_op jit(solution)/shard_map/ppermute | solution.py:133
  130.8 32.8 %collective-permute-start.4 = (bf16[2,10,34,512]{3,0,2,1:T(2,128)(2,1)S(1)}, bf16[2,10,34,512]{3,0,2,1:T(2,128)(2,1)S(1)}, u32[]{:S(2)}, u32[]{:S(2)}) collective-permute-start(bf16[2,10,34,512]{3,0,2,1:T(2,128)(2,1)S(1)} %copy.23), channel_id=1, source_target_pairs={{0,4},{4,8},{8,12},{12,16},{16,20},{20,24},{24,28},{1,5},{5,9},{9,... | collective-permute-start | bytes 2088968 | tf_op jit(solution)/shard_map/ppermute | solution.py:19

commit v15 on v11

--- a/solution.py
+++ b/solution.py
@@ -132,11 +132,9 @@
     left = lax.ppermute(high_padded[:, :, WCOL - 1 :], "src", up)
     right = lax.ppermute(high_padded[:, :, :1], "src", [(j, i) for i, j in up])
     own_wide = widen(high_padded, left, right)
-    sent_prev = jnp.concatenate(
-        [high_padded[FR_DEV - 2 :], left[FR_DEV - 2 :], right[FR_DEV - 2 :]], axis=2
-    )
-    prev = passed_along(sent_prev, "frame", 1)
-    prev_wide = widen(prev[:, :, :WCOL], prev[:, :, WCOL : WCOL + 1], prev[:, :, WCOL + 1 :])
+    cols = jnp.concatenate([left[FR_DEV - 2 :], right[FR_DEV - 2 :]], axis=2)
+    prev_high, prev_cols = passed_along((high_padded[FR_DEV - 2 :], cols), "frame", 1)
+    prev_wide = widen(prev_high, prev_cols[:, :, :1], prev_cols[:, :, 1:])
 
     validity = jnp.stack(
         [(window_ids[a : a + FR_DEV] == own_ids).astype(jnp.int32) for a in range(3)]

time: 176 us -> 175 us (level)
  starting transfers between devices: 23.3 us -> 26.4 us
  waiting for transfers between devices: 60.4 us -> 57.6 us
  local copies, waits for them, and re-layouts: 25.8 us -> 23.9 us
    ppermute x1 -> x2, starting transfers between devices: 2.86 us -> 5.93 us  [passed_along(): return lax.ppermute(x, axis, pairs)]
    ppermute x1, waiting for transfers between devices: 2.84 us -> 0.01 us  [shards(): right = lax.ppermute(high_padded[:, :, :1], 'src', [(j, i) for i, j in up])]
  transfers between devices with their start and end apart: 6 -> 7, of which waited for: 3 -> 2; matrix products, arithmetic and copies ran while one was open for 4% -> 4% of each run, Pallas kernels for 15% -> 15%
where the time goes in v15:
time: 175 us; the launch traced here: 173 us
  waiting for transfers between devices  57.6 us (33%)
  Pallas kernels  33.5 us (19%)
  other arithmetic  27.6 us (16%)
  starting transfers between devices  26.4 us (15%)
  local copies, waits for them, and re-layouts  23.9 us (14%)
  matrix products  3.23 us (2%)
    all_to_all x1, waiting for transfers between devices, shards(): lax.all_to_all(payload, ('src', 'frame', 'tile'), split_axis=0, concat_ax...  52.2 us
    pallas_call x1, Pallas kernels, own_conv(): pl.pallas_call(own_kernel, grid_spec=pltpu.PrefetchScalarGridSpec(num_sca...  26.1 us
    all_to_all x1, starting transfers between devices, shards(): lax.all_to_all(payload, ('src', 'frame', 'tile'), split_axis=0, concat_ax...  12 us
    gather x1, local copies, waits for them, and re-layouts, shards(): feats[pick.reshape(-1)].reshape(devices, block, channels)  8.91 us
    gather x1, local copies, waits for them, and re-layouts, shards(): arrived.reshape(-1, channels)[gather_rows]  7.93 us
    pallas_call x1, Pallas kernels, prev_conv(): pl.pallas_call(prev_kernel, grid_spec=pltpu.PrefetchScalarGridSpec(num_sc...  7.43 us
    ppermute x2, starting transfers between devices, passed_along(): return lax.ppermute(x, axis, pairs)  5.93 us
    concatenate x2, other arithmetic, widen(): return jnp.concatenate([shifted_in, block, shifted_out], axis=-1)  5.53 us
  transfers between devices with their start and end apart: 7, of which 2 were waited for; matrix products, arithmetic and copies ran while one was open for 4% of the time, Pallas kernels for 15%

profile of v15, /device:TPU:1, one launch (start us, length us, event | category | flops | bytes accessed | tf_op | source)
XLA Modules:
  0.0 172.7 jit_solution(1501247162356566449)
XLA Ops:
  0.0 0.7 fusion.11
  0.7 1.2 fusion.48
  1.9 3.3 %multiply_reduce_fusion.2 = f32[4,512]{1,0:T(4,128)S(1)} fusion(f32[4,1536]{1,0:T(4,128)S(1)} %bitcast.32, f32[1536,512]{1,0:T(8,128)} %param.7), kind=kLoop, calls=%fused_computation.4 | loop fusion | flops 6289408 | bytes 3178496 | tf_op jit(solution)/shard_map/reduce_sum | solution.py:60
  5.8 1.3 multiply_reduce_fusion.1
  7.1 0.8 subtract_multiply_fusion
  7.9 1.1 multiply_reduce_fusion
  9.3 5.1 %sort.21 = (s32[1536]{0:T(1024)}, s32[1536]{0:T(1024)S(1)}, s32[1536]{0:T(1024)S(1)}) sort(s32[1536]{0:T(1024)S(1)} %get-tuple-element.29, s32[1536]{0:T(1024)S(1)} %get-tuple-element.30, s32[1536]{0:T(1024)S(1)} %iota.38), dimensions={0}, to_apply=%region_0.1 | sort | flops 16896 | bytes 36864 | tf_op jit(solution)/shard_map/sort | solution.py:73
  14.8 8.9 %gather_fusion = f32[2048,512]{1,0:T(8,128)} fusion(f32[1536,512]{1,0:T(8,128)S(1)} %copy-done, s32[2048]{0:T(1024)S(1)} %broadcast_clamp_fusion), kind=kCustom, calls=%fused_computation | custom fusion | bytes 8396800 | tf_op jit(solution)/shard_map/gather | solution.py:89
  23.9 5.2 %broadcast_select_fusion = f32[128,16,512]{2,1,0:T(8,128)} fusion(f32[128,16,512]{2,1,0:T(8,128)} %bitcast.27, f32[128,512]{1,0:T(8,128)S(1)} %maximum_maximum_fusion.2, pred[16]{0:T(512)(128)(4,1)S(1)} %iota_compare_fusion.11), kind=kLoop, calls=%fused_computation.12 | loop fusion | flops 1048576 | bytes 8650768 | tf_op jit(solution)/shard_map/jit(_where)/select_n | solution.py:88
  29.1 12.0 %all-to-all-start = ((f32[128,16,512]{2,1,0:T(8,128)}), f32[128,16,512]{2,1,0:T(8,128)}, u32[]{:S(2)}, u32[]{:S(2)}) async-start(f32[128,16,512]{2,1,0:T(8,128)} %broadcast_select_fusion), calls=%async_computation | async-start | bytes 8388608 | tf_op jit(solution)/shard_map/all_to_all | solution.py:91
  41.5 52.2 %all-to-all-done = f32[128,16,512]{2,1,0:T(8,128)} async-done(((f32[128,16,512]{2,1,0:T(8,128)}), f32[128,16,512]{2,1,0:T(8,128)}, u32[]{:S(2)}, u32[]{:S(2)}) %all-to-all-start) | async-done | bytes 4194336 | tf_op jit(solution)/shard_map/all_to_all | solution.py:91
  93.7 1.9 %slice.101 = f32[128,1,512]{2,1,0:T(1,128)S(1)} slice(f32[128,16,512]{2,1,0:T(8,128)} %all-to-all-done), slice={[0:128], [12:13], [0:512]} | slice | bytes 524288 | tf_op jit(solution)/shard_map/slice | solution.py:95
  97.5 1.7 fusion.2
  99.3 7.9 %gather_fusion.1 = f32[1536,512]{1,0:T(8,128)} fusion(f32[2048,512]{1,0:T(8,128)} %bitcast.5, s32[2048]{0:T(1024)S(1)} %pad_clamp_fusion), kind=kCustom, calls=%fused_computation.1 | custom fusion | bytes 6297600 | tf_op jit(solution)/shard_map/gather | solution.py:115
  107.2 2.9 %multiply_convert_fusion = bf16[6,8,32,512]{3,2,1,0:T(8,128)(2,1)S(1)} fusion(f32[6,8,32,512]{3,2,1,0:T(8,128)} %bitcast.25, f32[512]{0:T(512)S(1)} %copy-done.1, f32[512]{0:T(512)S(1)} %copy-done.2, f32[6,512]{1,0:T(8,128)S(1)} %mul.141, f32[6,512]{1,0:T(8,128)S(1)} %sub.56), kind=kLoop, calls=%fused_computation.9 | loop fusion | flops 7077888 | bytes 4747264 | tf_op jit(solution)/shard_map/convert_element_type | solution.py:128
  110.1 3.6 %collective-permute-start = (bf16[6,1,32,512]{3,2,1,0:T(8,128)(2,1)S(1)}, bf16[6,1,32,512]{3,2,1,0:T(8,128)(2,1)S(1)}, u32[]{:S(2)}, u32[]{:S(2)}) collective-permute-start(bf16[6,1,32,512]{3,2,1,0:T(8,128)(2,1)S(1)} %get-tuple-element.19), channel_id=1, source_target_pairs={{0,1},{1,2},{2,3},{4,5},{5,6},{6,7},{8,9},{9,10},{10,11},{12,13},{... | collective-permute-start | bytes 589832 | tf_op jit(solution)/shard_map/ppermute | solution.py:29
  113.8 1.9 %collective-permute-start.1 = (bf16[6,1,32,512]{3,2,1,0:T(8,128)(2,1)S(1)}, bf16[6,1,32,512]{3,2,1,0:T(8,128)(2,1)S(1)}, u32[]{:S(2)}, u32[]{:S(2)}) collective-permute-start(bf16[6,1,32,512]{3,2,1,0:T(8,128)(2,1)S(1)} %get-tuple-element.20), channel_id=1, source_target_pairs={{1,0},{2,1},{3,2},{5,4},{6,5},{7,6},{9,8},{10,9},{11,10},{13,12},{... | collective-permute-start | bytes 589832 | tf_op jit(solution)/shard_map/ppermute | solution.py:30
  115.8 0.6 select_n.123.valid_ref
  116.4 0.6 reshape.248.valid_ref
  116.9 5.3 %collective-permute-done.1 = bf16[6,1,32,512]{3,2,1,0:T(8,128)(2,1)S(1)} collective-permute-done((bf16[6,1,32,512]{3,2,1,0:T(8,128)(2,1)S(1)}, bf16[6,1,32,512]{3,2,1,0:T(8,128)(2,1)S(1)}, u32[]{:S(2)}, u32[]{:S(2)}) %collective-permute-start.1) | collective-permute-done | bytes 196640 | tf_op jit(solution)/shard_map/ppermute | solution.py:30
  122.3 0.2 pad_maximum_fusion.2
  122.5 1.5 collective-permute-start.2
  123.9 1.5 collective-permute-start.3
  125.4 0.2 pad_maximum_fusion
  125.7 1.3 fusion.43
  127.0 3.0 %collective-permute-start.5 = (bf16[2,10,32,512]{3,2,1,0:T(8,128)(2,1)S(1)}, bf16[2,10,32,512]{3,2,1,0:T(8,128)(2,1)S(1)}, u32[]{:S(2)}, u32[]{:S(2)}) collective-permute-start(bf16[2,10,32,512]{3,2,1,0:T(8,128)(2,1)S(1)} %slice.113), channel_id=1, source_target_pairs={{0,4},{4,8},{8,12},{12,16},{16,20},{20,24},{24,28},{1,5},{5,9},{9,... | collective-permute-start | bytes 1966088 | tf_op jit(solution)/shard_map/ppermute | solution.py:19
  130.2 2.9 %collective-permute-start.4 = (bf16[2,10,2,512]{3,2,1,0:T(2,128)(2,1)S(1)}, bf16[2,10,2,512]{3,2,1,0:T(2,128)(2,1)S(1)}, u32[]{:S(2)}, u32[]{:S(2)}) collective-permute-start(bf16[2,10,2,512]{3,2,1,0:T(2,128)(2,1)S(1)} %pad_maximum_fusion.3), channel_id=1, source_target_pairs={{0,4},{4,8},{8,12},{12,16},{16,20},{20,24},{24,28},{1,5},{5,9},{9,... | collective-permute-start | bytes 122888 | tf_op jit(solution)/shard_map/ppermute | solution.py:19
  133.2 3.8 %maximum_maximum_fusion.x_ref = bf16[6,10,32,1536]{3,2,1,0:T(8,128)(2,1)} fusion(bf16[6,10,1,512]{3,2,1,0:T(2,128)(2,1)S(1)} %collective-permute-done.3, bf16[6,10,31,512]{3,2,1,0:T(8,128)(2,1)S(1)} %get-tuple-element.16, bf16[6,1,32,512]{3,2,1,0:T(8,128)(2,1)S(1)} %collective-permute-done.1, bf16[6,8,32,512]{3,2,1,0:T(8,128)(2,1)S(1)} %multiply_convert_fusion, ...), kind=kLoop, calls=%fused_computation.7 | loop fusion | flops 41287680 | bytes 11796480 | tf_op jit(solution)/shard_map/concatenate | solution.py:154
  137.0 26.1 %shard_map.73 = (bf16[6,8,32,512]{3,2,1,0:T(8,128)(2,1)}, f32[2,8,32,512]{3,2,1,0:T(8,128)}) custom-call(s32[18]{0:T(128)} %select_n.123.valid_ref, bf16[6,10,32,1536]{3,2,1,0:T(8,128)(2,1)} %maximum_maximum_fusion.x_ref, bf16[9,1536,512]{2,1,0:T(8,128)(2,1)} %bitcast.23, f32[1,512]{1,0:T(1,128)} %bitcast.36, f32[6,8,32,512]{3,2,1,0:T(8,128)} %bitcast.26), custom_call_target="tpu_custom_call" | custom-call | tf_op jit(solution)/shard_map/pallas_call | solution.py:191
  163.2 0.3 fusion.45
  163.5 1.7 maximum_maximum_fusion.1.x_ref
  165.2 7.4 %shard_map.74 = bf16[6,8,32,512]{3,2,1,0:T(8,128)(2,1)} custom-call(s32[4]{0:T(128)} %reshape.248.valid_ref, bf16[2,10,32,1536]{3,2,1,0:T(8,128)(2,1)} %maximum_maximum_fusion.1.x_ref, bf16[9,1536,512]{2,1,0:T(8,128)(2,1)} %bitcast.24, f32[2,8,32,512]{3,2,1,0:T(8,128)} %get-tuple-element.11.early_ref, ...), custom_call_target="tpu_custom_call", output_to_operand_aliasing={{}: (4, {})} | custom-call | tf_op jit(solution)/shard_map/pallas_call | solution.py:247
  (70 shorter events, 4.0 us)
Async XLA Ops:
  1.9 5.2 %copy-start = (f32[1536,512]{1,0:T(8,128)S(1)}, f32[1536,512]{1,0:T(8,128)}, u32[]{:S(2)}) copy-start(f32[1536,512]{1,0:T(8,128)} %param.7) | copy-start | bytes 9437188
  29.1 12.0 %copy-start.3 = (s32[48]{0:T(128)S(1)}, s32[48]{0:T(128)}, u32[]{:S(2)}) copy-start(s32[48]{0:T(128)} %param.9) | copy-start | bytes 580
  29.1 64.6 %all-to-all-start = ((f32[128,16,512]{2,1,0:T(8,128)}), f32[128,16,512]{2,1,0:T(8,128)}, u32[]{:S(2)}, u32[]{:S(2)}) async-start(f32[128,16,512]{2,1,0:T(8,128)} %broadcast_select_fusion), calls=%async_computation | async-start | bytes 8388608 | tf_op jit(solution)/shard_map/all_to_all | solution.py:91
  99.2 8.0 %copy-start.1 = (f32[512]{0:T(512)S(1)}, f32[512]{0:T(512)}, u32[]{:S(2)}) copy-start(f32[512]{0:T(512)} %param.11) | copy-start | bytes 6148
  99.3 7.9 %copy-start.2 = (f32[512]{0:T(512)S(1)}, f32[512]{0:T(512)}, u32[]{:S(2)}) copy-start(f32[512]{0:T(512)} %param.10) | copy-start | bytes 6148
  110.1 6.8 %collective-permute-start = (bf16[6,1,32,512]{3,2,1,0:T(8,128)(2,1)S(1)}, bf16[6,1,32,512]{3,2,1,0:T(8,128)(2,1)S(1)}, u32[]{:S(2)}, u32[]{:S(2)}) collective-permute-start(bf16[6,1,32,512]{3,2,1,0:T(8,128)(2,1)S(1)} %get-tuple-element.19), channel_id=1, source_target_pairs={{0,1},{1,2},{2,3},{4,5},{5,6},{6,7},{8,9},{9,10},{10,11},{12,13},{... | collective-permute-start | bytes 589832 | tf_op jit(solution)/shard_map/ppermute | solution.py:29
  113.8 8.5 %collective-permute-start.1 = (bf16[6,1,32,512]{3,2,1,0:T(8,128)(2,1)S(1)}, bf16[6,1,32,512]{3,2,1,0:T(8,128)(2,1)S(1)}, u32[]{:S(2)}, u32[]{:S(2)}) collective-permute-start(bf16[6,1,32,512]{3,2,1,0:T(8,128)(2,1)S(1)} %get-tuple-element.20), channel_id=1, source_target_pairs={{1,0},{2,1},{3,2},{5,4},{6,5},{7,6},{9,8},{10,9},{11,10},{13,12},{... | collective-permute-start | bytes 589832 | tf_op jit(solution)/shard_map/ppermute | solution.py:30
  122.5 7.5 %collective-permute-start.2 = (bf16[6,10,1,512]{3,2,1,0:T(2,128)(2,1)S(1)}, bf16[6,10,1,512]{3,2,1,0:T(2,128)(2,1)S(1)}, u32[]{:S(2)}, u32[]{:S(2)}) collective-permute-start(bf16[6,10,1,512]{3,2,1,0:T(2,128)(2,1)S(1)} %get-tuple-element.17), channel_id=1, source_target_pairs={{0,32},{32,64},{64,96},{1,33},{33,65},{65,97},{2,34},{34,66},{66,9... | collective-permute-start | bytes 184328 | tf_op jit(solution)/shard_map/ppermute | solution.py:132
  123.9 6.1 %collective-permute-start.3 = (bf16[6,10,1,512]{3,2,1,0:T(2,128)(2,1)S(1)}, bf16[6,10,1,512]{3,2,1,0:T(2,128)(2,1)S(1)}, u32[]{:S(2)}, u32[]{:S(2)}) collective-permute-start(bf16[6,10,1,512]{3,2,1,0:T(2,128)(2,1)S(1)} %get-tuple-element.18), channel_id=1, source_target_pairs={{32,0},{64,32},{96,64},{33,1},{65,33},{97,65},{34,2},{66,34},{98,6... | collective-permute-start | bytes 184328 | tf_op jit(solution)/shard_map/ppermute | solution.py:133
  127.0 36.2 %collective-permute-start.5 = (bf16[2,10,32,512]{3,2,1,0:T(8,128)(2,1)S(1)}, bf16[2,10,32,512]{3,2,1,0:T(8,128)(2,1)S(1)}, u32[]{:S(2)}, u32[]{:S(2)}) collective-permute-start(bf16[2,10,32,512]{3,2,1,0:T(8,128)(2,1)S(1)} %slice.113), channel_id=1, source_target_pairs={{0,4},{4,8},{8,12},{12,16},{16,20},{20,24},{24,28},{1,5},{5,9},{9,... | collective-permute-start | bytes 1966088 | tf_op jit(solution)/shard_map/ppermute | solution.py:19
  130.2 32.9 %collective-permute-start.4 = (bf16[2,10,2,512]{3,2,1,0:T(2,128)(2,1)S(1)}, bf16[2,10,2,512]{3,2,1,0:T(2,128)(2,1)S(1)}, u32[]{:S(2)}, u32[]{:S(2)}) collective-permute-start(bf16[2,10,2,512]{3,2,1,0:T(2,128)(2,1)S(1)} %pad_maximum_fusion.3), channel_id=1, source_target_pairs={{0,4},{4,8},{8,12},{12,16},{16,20},{20,24},{24,28},{1,5},{5,9},{9,... | collective-permute-start | bytes 122888 | tf_op jit(solution)/shard_map/ppermute | solution.py:19
